TPU v7x, 32 devices: a whole 2x2x4 slice. The times are simulated.
32 devices in a mesh: chol: 4 (over z), orb: 8 (over y, x, core).
Axes of the slice: x: 2, y: 2, z: 4, core: 2. Of those that a mesh axis runs over, the one named last changes fastest.
Arguments:
- chol_vec: bfloat16 [16, 1536, 1536], P('chol', 'orb'), may hold values from -6 to 6
- env_weight: float32 [1536], P('orb'), may hold values from -5 to 5
- lno_coef: bfloat16 [8, 1024, 384], P('orb'), may hold values from -0.1875 to 0.1875
- domain: int32 [8, 1024], replicated, may hold values from 0 to 1535, as said below
- block_fill: int32 [8, 8], replicated, may hold values from 32 to 128, as said below
- lno_count: int32 [8], replicated, may hold values from 144 to 384
Outputs:
- rotated: bfloat16 [16, 8, 384, 384], P('chol', 'orb')
- dressing: bfloat16 [8, 384, 384], P('orb')
Inputs may be any that keep to these rules, and one draw needn't show every extreme that they name: `domain`: for each fragment and each j < 8, slots j * 128 to (j + 1) * 128 - 1 hold distinct orbitals of the row block o * 192 to (o + 1) * 192 - 1 of a single o; the 8 groups of a fragment lie in distinct row blocks. `block_fill`: every fragment has one full group.
All inputs are finite; a program needn't handle non-finite values.
Results may differ from a plain program's by a relative error of at most 0.0064.
Values may be sent and summed in bfloat16 or wider, within the bound.
No kernel may reach another device: no remote copies, remote signals or barrier semaphores. Data moves between devices by JAX's collectives and lax.ppermute only.
A program may use at most 192 MiB of HBM per device.

v0:
```python
import math

import jax
import jax.numpy as jnp
from jax import lax
from jax.sharding import PartitionSpec as P


def per_device(chol_vec, env_weight, lno_coef, domain, block_fill, lno_count):
    chol_local, orb_rows, orb_total = chol_vec.shape
    frag_total, slot_total = domain.shape
    group_count = block_fill.shape[1]
    group_width = slot_total // group_count
    lno_width = lno_coef.shape[2]
    chol_size = lax.axis_size("chol")
    my_index = lax.axis_index("orb")
    norm_factor = 1.0 / math.sqrt(chol_local * chol_size * orb_total)
    slot_index = jnp.arange(slot_total, dtype=jnp.int32)
    slot_ok = (slot_index % group_width)[None, :] < jnp.repeat(block_fill, group_width, axis=1)
    column_ok = jnp.arange(lno_width, dtype=jnp.int32)[None, :] < lno_count[:, None]
    all_coef = lax.all_gather(lno_coef, "orb", axis=0, tiled=True)
    keep_mask = (slot_ok[:, :, None] & column_ok[:, None, :]).astype(jnp.bfloat16)
    masked = all_coef * keep_mask
    row_base = my_index * orb_rows

    def per_fragment(inputs):
        orbitals, coef = inputs
        columns = jnp.take(chol_vec, orbitals, axis=2)
        half_rot = jnp.dot(
            columns.reshape(-1, slot_total), coef, preferred_element_type=jnp.float32
        )
        half_rot = half_rot.astype(jnp.bfloat16).reshape(chol_local, orb_rows, lno_width)
        weighted = (half_rot.astype(jnp.float32) * env_weight[None, :, None]).astype(jnp.bfloat16)
        dressing_part = lax.dot_general(
            weighted.reshape(-1, lno_width),
            half_rot.reshape(-1, lno_width),
            (((0,), (0,)), ((), ())),
            preferred_element_type=jnp.float32,
        )
        group_here = orbitals[::group_width] // orb_rows == my_index
        group = jnp.argmax(group_here)
        present = jnp.any(group_here).astype(jnp.bfloat16)
        local_rows = lax.dynamic_slice_in_dim(orbitals, group * group_width, group_width) - row_base
        local_rows = jnp.clip(local_rows, 0, orb_rows - 1)
        outgoing = jnp.take(columns, local_rows, axis=1) * present
        return (dressing_part, outgoing)

    partials, outgoing = lax.map(per_fragment, (domain, masked))
    own_orbitals = lax.dynamic_index_in_dim(domain, my_index, 0, keepdims=False)
    own_coef = lax.dynamic_index_in_dim(masked, my_index, 0, keepdims=False)
    sources = own_orbitals[::group_width] // orb_rows
    received = lax.all_to_all(outgoing, "orb", split_axis=0, concat_axis=0, tiled=True)
    ordered = jnp.take(received, sources, axis=0)
    domain_block = jnp.transpose(ordered, (1, 0, 2, 3)).reshape(chol_local, slot_total, slot_total)
    domain_rot = jnp.einsum(
        "gde,en->gdn", domain_block, own_coef, preferred_element_type=jnp.float32
    ).astype(jnp.bfloat16)
    rotated = jnp.einsum(
        "dn,gdm->gnm", own_coef, domain_rot, preferred_element_type=jnp.float32
    ).astype(jnp.bfloat16)[:, None]
    flat_terms = partials.reshape(frag_total * lno_width, lno_width)
    share = lax.psum_scatter(flat_terms, "orb", scatter_dimension=0, tiled=True)
    dressing = (lax.psum(share, "chol") * norm_factor).astype(jnp.bfloat16)
    return (rotated, dressing[None])


def solution(mesh):
    return jax.shard_map(
        per_device,
        mesh=mesh,
        in_specs=(P("chol", "orb", None), P("orb"), P("orb", None, None), P(), P(), P()),
        out_specs=(P("chol", "orb", None, None), P("orb", None, None)),
        check_vma=False,
    )
```

profile of v0, /device:TPU:0, one launch (start us, length us, event | category | flops | bytes accessed | tf_op | source)
XLA Modules:
  0.0 512.6 jit_solution(1115826445903817480)
XLA Ops:
  7.9 5.7 %copy.25 = bf16[4,192,1536]{1,0,2:T(4,128)(2,1)} copy(bf16[4,192,1536]{2,1,0:T(8,128)(2,1)} %param.8) | data formatting | bytes 4718592 | tf_op jit(solution)/shard_map/while | solution.py:48
  13.9 44.3 %all-gather.2.cloned.1.call-done = bf16[8,1024,384]{2,1,0:T(8,128)(2,1)} async-done(((bf16[1,1024,384]{2,1,0:T(8,128)(2,1)}), bf16[8,1024,384]{2,1,0:T(8,128)(2,1)}) %all-gather.2.cloned.1.call-update) | async-done | bytes 6291472 | tf_op jit(solution)/shard_map/all_gather | solution.py:21
  58.2 6.8 %and_select_fusion.1 = bf16[8,1024,384]{2,1,0:T(8,128)(2,1)} fusion(bf16[8,1024,384]{2,1,0:T(8,128)(2,1)} %all-gather.2.cloned.1.call-done, pred[8,384]{1,0:T(8,128)(4,1)S(1)} %iota_compare_fusion, pred[8,1024]{1,0:T(8,128)(4,1)S(1)} %bitcast_compare_fusion), kind=kLoop, calls=%fused_computation.29 | loop fusion | flops 6291456 | bytes 12594176 | tf_op jit(solution)/shard_map/mul | solution.py:23
  65.0 285.5 %while.15 = (s32[]{:T(128)}, f32[8,384,384]{2,1,0:T(8,128)}, bf16[8,4,128,1024]{3,2,1,0:T(8,128)(2,1)}, s32[8,1024]{1,0:T(8,128)}, bf16[4,192,1536]{1,0,2:T(4,12...) while((s32[]{:T(128)}, f32[8,384,384]{2,1,0:T(8,128)}, ...), condition=%wide.region_3.4_spmd, body=%wide.region_0.3_spmd.sunk | while | flops 833499648 | bytes 23645616 | solution.py:48
  65.8 10.5 %gather_fusion = bf16[1024,4,192]{2,1,0:T(4,128)(2,1)} fusion(bf16[4,192,1536]{1,0,2:T(4,128)(2,1)} %get-tuple-element.313, s32[1024]{0:T(1024)S(1)} %broadcast_clamp_fusion.2), kind=kCustom, calls=%fused_computation.clone.1 | custom fusion | bytes 3149824 | tf_op jit(solution)/shard_map/while/body/eval_jaxpr/jit(_take)/gather | solution.py:28
  76.3 5.2 %select_bitcast_fusion.3 = bf16[4,192,1024]{1,0,2:T(4,128)(2,1)S(1)} fusion(bf16[1024,4,192]{2,1,0:T(4,128)(2,1)} %gather_fusion, pred[1024]{0:T(1024)(128)(4,1)S(1)} %compare_and_fusion.5), kind=kLoop, calls=%fused_computation.3.clone.1 | loop fusion | flops 786432 | bytes 3146752 | tf_op jit(solution)/shard_map/while/body/eval_jaxpr/jit(_take)/select_n | solution.py:28
  88.3 3.9 copy.39
  101.5 10.5 %gather_fusion = bf16[1024,4,192]{2,1,0:T(4,128)(2,1)} fusion(bf16[4,192,1536]{1,0,2:T(4,128)(2,1)} %get-tuple-element.313, s32[1024]{0:T(1024)S(1)} %broadcast_clamp_fusion.2), kind=kCustom, calls=%fused_computation.clone.1 | custom fusion | bytes 3149824 | tf_op jit(solution)/shard_map/while/body/eval_jaxpr/jit(_take)/gather | solution.py:28
  112.0 5.2 %select_bitcast_fusion.3 = bf16[4,192,1024]{1,0,2:T(4,128)(2,1)S(1)} fusion(bf16[1024,4,192]{2,1,0:T(4,128)(2,1)} %gather_fusion, pred[1024]{0:T(1024)(128)(4,1)S(1)} %compare_and_fusion.5), kind=kLoop, calls=%fused_computation.3.clone.1 | loop fusion | flops 786432 | bytes 3146752 | tf_op jit(solution)/shard_map/while/body/eval_jaxpr/jit(_take)/select_n | solution.py:28
  124.0 3.9 copy.39
  137.1 10.5 %gather_fusion = bf16[1024,4,192]{2,1,0:T(4,128)(2,1)} fusion(bf16[4,192,1536]{1,0,2:T(4,128)(2,1)} %get-tuple-element.313, s32[1024]{0:T(1024)S(1)} %broadcast_clamp_fusion.2), kind=kCustom, calls=%fused_computation.clone.1 | custom fusion | bytes 3149824 | tf_op jit(solution)/shard_map/while/body/eval_jaxpr/jit(_take)/gather | solution.py:28
  147.6 5.2 %select_bitcast_fusion.3 = bf16[4,192,1024]{1,0,2:T(4,128)(2,1)S(1)} fusion(bf16[1024,4,192]{2,1,0:T(4,128)(2,1)} %gather_fusion, pred[1024]{0:T(1024)(128)(4,1)S(1)} %compare_and_fusion.5), kind=kLoop, calls=%fused_computation.3.clone.1 | loop fusion | flops 786432 | bytes 3146752 | tf_op jit(solution)/shard_map/while/body/eval_jaxpr/jit(_take)/select_n | solution.py:28
  159.7 3.9 copy.39
  172.9 10.5 %gather_fusion = bf16[1024,4,192]{2,1,0:T(4,128)(2,1)} fusion(bf16[4,192,1536]{1,0,2:T(4,128)(2,1)} %get-tuple-element.313, s32[1024]{0:T(1024)S(1)} %broadcast_clamp_fusion.2), kind=kCustom, calls=%fused_computation.clone.1 | custom fusion | bytes 3149824 | tf_op jit(solution)/shard_map/while/body/eval_jaxpr/jit(_take)/gather | solution.py:28
  183.4 5.2 %select_bitcast_fusion.3 = bf16[4,192,1024]{1,0,2:T(4,128)(2,1)S(1)} fusion(bf16[1024,4,192]{2,1,0:T(4,128)(2,1)} %gather_fusion, pred[1024]{0:T(1024)(128)(4,1)S(1)} %compare_and_fusion.5), kind=kLoop, calls=%fused_computation.3.clone.1 | loop fusion | flops 786432 | bytes 3146752 | tf_op jit(solution)/shard_map/while/body/eval_jaxpr/jit(_take)/select_n | solution.py:28
  195.4 3.9 copy.39
  208.6 10.5 %gather_fusion = bf16[1024,4,192]{2,1,0:T(4,128)(2,1)} fusion(bf16[4,192,1536]{1,0,2:T(4,128)(2,1)} %get-tuple-element.313, s32[1024]{0:T(1024)S(1)} %broadcast_clamp_fusion.2), kind=kCustom, calls=%fused_computation.clone.1 | custom fusion | bytes 3149824 | tf_op jit(solution)/shard_map/while/body/eval_jaxpr/jit(_take)/gather | solution.py:28
  219.1 5.2 %select_bitcast_fusion.3 = bf16[4,192,1024]{1,0,2:T(4,128)(2,1)S(1)} fusion(bf16[1024,4,192]{2,1,0:T(4,128)(2,1)} %gather_fusion, pred[1024]{0:T(1024)(128)(4,1)S(1)} %compare_and_fusion.5), kind=kLoop, calls=%fused_computation.3.clone.1 | loop fusion | flops 786432 | bytes 3146752 | tf_op jit(solution)/shard_map/while/body/eval_jaxpr/jit(_take)/select_n | solution.py:28
  231.1 3.9 copy.39
  244.2 10.5 %gather_fusion = bf16[1024,4,192]{2,1,0:T(4,128)(2,1)} fusion(bf16[4,192,1536]{1,0,2:T(4,128)(2,1)} %get-tuple-element.313, s32[1024]{0:T(1024)S(1)} %broadcast_clamp_fusion.2), kind=kCustom, calls=%fused_computation.clone.1 | custom fusion | bytes 3149824 | tf_op jit(solution)/shard_map/while/body/eval_jaxpr/jit(_take)/gather | solution.py:28
  254.7 5.2 %select_bitcast_fusion.3 = bf16[4,192,1024]{1,0,2:T(4,128)(2,1)S(1)} fusion(bf16[1024,4,192]{2,1,0:T(4,128)(2,1)} %gather_fusion, pred[1024]{0:T(1024)(128)(4,1)S(1)} %compare_and_fusion.5), kind=kLoop, calls=%fused_computation.3.clone.1 | loop fusion | flops 786432 | bytes 3146752 | tf_op jit(solution)/shard_map/while/body/eval_jaxpr/jit(_take)/select_n | solution.py:28
  279.9 10.5 %gather_fusion = bf16[1024,4,192]{2,1,0:T(4,128)(2,1)} fusion(bf16[4,192,1536]{1,0,2:T(4,128)(2,1)} %get-tuple-element.313, s32[1024]{0:T(1024)S(1)} %broadcast_clamp_fusion.2), kind=kCustom, calls=%fused_computation.clone.1 | custom fusion | bytes 3149824 | tf_op jit(solution)/shard_map/while/body/eval_jaxpr/jit(_take)/gather | solution.py:28
  290.4 5.2 %select_bitcast_fusion.3 = bf16[4,192,1024]{1,0,2:T(4,128)(2,1)S(1)} fusion(bf16[1024,4,192]{2,1,0:T(4,128)(2,1)} %gather_fusion, pred[1024]{0:T(1024)(128)(4,1)S(1)} %compare_and_fusion.5), kind=kLoop, calls=%fused_computation.3.clone.1 | loop fusion | flops 786432 | bytes 3146752 | tf_op jit(solution)/shard_map/while/body/eval_jaxpr/jit(_take)/select_n | solution.py:28
  315.6 10.5 %gather_fusion = bf16[1024,4,192]{2,1,0:T(4,128)(2,1)} fusion(bf16[4,192,1536]{1,0,2:T(4,128)(2,1)} %get-tuple-element.313, s32[1024]{0:T(1024)S(1)} %broadcast_clamp_fusion.2), kind=kCustom, calls=%fused_computation.clone.1 | custom fusion | bytes 3149824 | tf_op jit(solution)/shard_map/while/body/eval_jaxpr/jit(_take)/gather | solution.py:28
  326.2 5.2 %select_bitcast_fusion.3 = bf16[4,192,1024]{1,0,2:T(4,128)(2,1)S(1)} fusion(bf16[1024,4,192]{2,1,0:T(4,128)(2,1)} %gather_fusion, pred[1024]{0:T(1024)(128)(4,1)S(1)} %compare_and_fusion.5), kind=kLoop, calls=%fused_computation.3.clone.1 | loop fusion | flops 786432 | bytes 3146752 | tf_op jit(solution)/shard_map/while/body/eval_jaxpr/jit(_take)/select_n | solution.py:28
  350.5 5.0 all-to-all-start
  357.4 94.5 %reduce-scatter.2.cloned.1.call-done = f32[384,384]{1,0:T(8,128)} async-done(((f32[3072,384]{1,0:T(8,128)}), f32[384,384]{1,0:T(8,128)}) %reduce-scatter.2.cloned.1.call-update) | async-done | bytes 589840 | tf_op jit(solution)/shard_map/reduce_scatter | solution.py:62
  451.9 16.6 %all-to-all-done = bf16[8,4,128,1024]{3,2,1,0:T(8,128)(2,1)} async-done(((bf16[8,4,128,1024]{3,2,1,0:T(8,128)(2,1)}), bf16[8,4,128,1024]{3,2,1,0:T(8,128)(2,1)}, u32[]{:S(2)}, u32[]{:S(2)}) %all-to-all-start) | async-done | bytes 8388640 | tf_op jit(solution)/shard_map/all_to_all | solution.py:52
  468.5 8.2 %gather_fusion.2 = bf16[8,4,128,1024]{3,2,1,0:T(8,128)(2,1)} fusion(bf16[8,4,128,1024]{3,2,1,0:T(8,128)(2,1)} %all-to-all-done, s32[1024]{0:T(1024)S(1)} %pad_clamp_fusion.1), kind=kCustom, calls=%fused_computation.2 | custom fusion | bytes 16777248 | tf_op jit(solution)/shard_map/jit(_take)/gather | solution.py:53
  476.7 7.6 %select_bitcast_fusion.1 = bf16[4,8,128,1024]{3,2,0,1:T(8,128)(2,1)} fusion(bf16[8,4,128,1024]{3,2,1,0:T(8,128)(2,1)} %gather_fusion.2, pred[8]{0:T(512)(128)(4,1)S(1)} %get-tuple-element.208), kind=kLoop, calls=%fused_computation.30 | loop fusion | flops 4194304 | bytes 16777224 | tf_op jit(solution)/shard_map/jit(_take)/select_n | solution.py:53
  484.3 8.4 %copy.27 = bf16[4,8,128,1024]{3,2,1,0:T(8,128)(2,1)} copy(bf16[4,8,128,1024]{3,2,0,1:T(8,128)(2,1)} %select_bitcast_fusion.1) | data formatting | bytes 16777216 | tf_op jit(solution)/shard_map/jit(_take)/select_n | solution.py:53
  492.7 10.1 %fusion.12 = bf16[4,1,384,384]{2,3,0,1:T(8,128)(2,1)S(1)} fusion(bf16[4,1024,1024]{2,1,0:T(8,128)(2,1)} %bitcast.74, bf16[8,1024,384]{2,1,0:T(8,128)(2,1)} %get-tuple-element.329, s32[]{:T(128)S(6)} %select_n.139), kind=kOutput, calls=%fused_computation.34 | convolution fusion | flops 4431347712 | bytes 11142144 | tf_op jit(solution)/shard_map/dn,gdm->gnm/dot_general | solution.py:58
  (164 shorter events, 134.9 us)
Async XLA Ops:
  7.2 6.5 %copy-start.1 = (s32[8,8]{1,0:T(8,128)S(1)}, s32[8,8]{1,0:T(8,128)}, u32[]{:S(2)}) copy-start(s32[8,8]{1,0:T(8,128)} %param.12) | copy-start | bytes 772
  7.2 6.5 %copy-start.2 = (s32[8]{0:T(128)S(1)}, s32[8]{0:T(128)}, u32[]{:S(2)}) copy-start(s32[8]{0:T(128)} %param.13) | copy-start | bytes 100
  7.2 51.0 %all-gather.2.cloned.1.call-start = ((), (), s32[]{:S(2)}) async-start(), calls=%async_computation.2 | async-start | bytes 7077888 | tf_op jit(solution)/shard_map/all_gather | solution.py:21
  13.9 51.1 %copy-start = (f32[192]{0:T(256)S(1)}, f32[192]{0:T(256)}, u32[]{:S(2)}) copy-start(f32[192]{0:T(256)} %param.9) | copy-start | bytes 2308
  350.5 118.0 %all-to-all-start = ((bf16[8,4,128,1024]{3,2,1,0:T(8,128)(2,1)}), bf16[8,4,128,1024]{3,2,1,0:T(8,128)(2,1)}, u32[]{:S(2)}, u32[]{:S(2)}) async-start(bf16[8,4,128,1024]{3,2,1,0:T(8,128)(2,1)} %get-tuple-element.147), calls=%async_computation | async-start | bytes 16777216 | tf_op jit(solution)/shard_map/all_to_all | solution.py:52
  355.5 96.4 %reduce-scatter.2.cloned.1.call-start = ((), (), s32[]{:S(2)}) async-start(), calls=%async_computation.3 | async-start | bytes 5308416 | tf_op jit(solution)/shard_map/reduce_scatter | solution.py:62
  356.2 148.1 %all-reduce.2.cloned.1.call-start = ((), (), s32[]{:S(2)}) async-start(), calls=%async_computation.4 | async-start | bytes 1179648 | tf_op jit(solution)/shard_map/psum | solution.py:63
Sparse Core Ops, SparseCore 0:
  9.9 48.2 all-gather.1
  359.8 92.0 reduce-scatter.1
  454.3 40.1 all-reduce.1
where the time goes:
time: 516 us; the launch traced here: 513 us
  local copies, waits for them, and re-layouts  196 us (38%)
  waiting for transfers between devices  157 us (30%)
  other arithmetic  87.3 us (17%)
  matrix products  42.7 us (8%)
  between operations  13.8 us (3%)
  loops' own time  11.2 us (2%)
  starting transfers between devices  5.26 us (1%)
    reduce_scatter x1, waiting for transfers between devices, per_device(): share = lax.psum_scatter(flat_terms, 'orb', scatter_dimension=0, tiled=True)  94.5 us
    gather x8, local copies, waits for them, and re-layouts, per_fragment(): columns = jnp.take(chol_vec, orbitals, axis=2)  84 us
    select_n x16, local copies, waits for them, and re-layouts, per_fragment(): columns = jnp.take(chol_vec, orbitals, axis=2)  52.2 us
    select_n x16, other arithmetic, per_fragment(): columns = jnp.take(chol_vec, orbitals, axis=2)  48.1 us
    all_gather x1, waiting for transfers between devices, per_device(): all_coef = lax.all_gather(lno_coef, 'orb', axis=0, tiled=True)  44.3 us
    gather x8, local copies, waits for them, and re-layouts, per_fragment(): outgoing = jnp.take(columns, local_rows, axis=1) * present  22.8 us
    dot_general x8, matrix products, per_fragment(): jnp.dot(columns.reshape(-1, slot_total), coef, preferred_element_type=jnp...  20.6 us
    all_to_all x1, waiting for transfers between devices, per_device(): lax.all_to_all(outgoing, 'orb', split_axis=0, concat_axis=0, tiled=True)  16.6 us
  transfers between devices with their start and end apart: 4, of which 3 were waited for; matrix products, arithmetic and copies ran while one was open for 8% of the time, Pallas kernels for 0%

commit v1 on v0

v1 whole, which is shorter than its diff:
```python
import math

import jax
import jax.numpy as jnp
from jax import lax
from jax.sharding import PartitionSpec as P


def per_device(chol_vec, env_weight, lno_coef, domain, block_fill, lno_count):
    chol_local, orb_rows, orb_total = chol_vec.shape
    frag_total, slot_total = domain.shape
    group_count = block_fill.shape[1]
    group_width = slot_total // group_count
    lno_width = lno_coef.shape[2]
    chol_size = lax.axis_size("chol")
    orb_size = lax.axis_size("orb")
    my_index = lax.axis_index("orb")
    norm_factor = 1.0 / math.sqrt(chol_local * chol_size * orb_total)

    slot_index = jnp.arange(slot_total, dtype=jnp.int32)
    slot_ok = (slot_index % group_width)[None, :] < jnp.repeat(block_fill, group_width, axis=1)
    column_ok = jnp.arange(lno_width, dtype=jnp.int32)[None, :] < lno_count[:, None]
    keep_mask = (slot_ok[:, :, None] & column_ok[:, None, :]).astype(jnp.bfloat16)

    weight_all = lax.all_gather(env_weight, "orb", axis=0, tiled=True)
    all_coef = lax.all_gather(lno_coef, "orb", axis=0, tiled=True)
    masked = all_coef * keep_mask

    chol_t = chol_vec.reshape(chol_local * orb_rows, orb_total).T
    picked = jnp.take(chol_t, domain, axis=0)
    half = jnp.einsum(
        "fsk,fsa->fka", picked, masked, preferred_element_type=jnp.float32
    ).astype(jnp.bfloat16)
    half = half.reshape(frag_total, chol_local, orb_rows, lno_width)

    received = lax.all_to_all(half, "orb", split_axis=0, concat_axis=0, tiled=True)

    with jax.named_scope("dressing"):
        weighted = (
            received.astype(jnp.float32)
            * weight_all.reshape(orb_size, 1, orb_rows, 1)
        ).astype(jnp.bfloat16)
        dressing_part = lax.dot_general(
            weighted.reshape(-1, lno_width),
            received.reshape(-1, lno_width),
            (((0,), (0,)), ((), ())),
            preferred_element_type=jnp.float32,
        )
        dressing = (lax.psum(dressing_part, "chol") * norm_factor).astype(jnp.bfloat16)

    with jax.named_scope("rotated"):
        own_orbitals = lax.dynamic_index_in_dim(domain, my_index, 0, keepdims=False)
        own_coef = lax.dynamic_index_in_dim(masked, my_index, 0, keepdims=False)
        block = own_orbitals // orb_rows
        local = own_orbitals % orb_rows
        chol_ids = jnp.arange(chol_local, dtype=jnp.int32)
        flat_rows = (block[None, :] * chol_local + chol_ids[:, None]) * orb_rows + local[None, :]
        domain_rows = jnp.take(received.reshape(-1, lno_width), flat_rows, axis=0)
        rotated = jnp.einsum(
            "sa,gsb->gab", own_coef, domain_rows, preferred_element_type=jnp.float32
        ).astype(jnp.bfloat16)[:, None]
    return (rotated, dressing[None])


def solution(mesh):
    return jax.shard_map(
        per_device,
        mesh=mesh,
        in_specs=(P("chol", "orb", None), P("orb"), P("orb", None, None), P(), P(), P()),
        out_specs=(P("chol", "orb", None, None), P("orb", None, None)),
        check_vma=False,
    )
```

time: 516 us -> 202 us (0.39)
  waiting for transfers between devices: 157 us -> 15.9 us
  local copies, waits for them, and re-layouts: 196 us -> 78.5 us
  other arithmetic: 87.3 us -> 7.04 us
  blocking collectives: 0 us -> 59.9 us
  matrix products: 42.7 us -> 19.5 us
  loops' own time: 11.2 us -> 0 us
    reduce_scatter x1 -> x0, waiting for transfers between devices: 94.5 us -> none  [per_device(): share = lax.psum_scatter(flat_terms, 'orb', scatter_dimension=0, tiled=True)]
    select_n x17 -> x0, local copies, waits for them, and re-layouts: 60.5 us -> none  [the longest x16 52.2 us: per_fragment(): columns = jnp.take(chol_vec, orbitals, axis=2)]
    unnamed x0 -> x1, blocking collectives: none -> 59.9 us
    select_n x25 -> x0, other arithmetic: 55.7 us -> none  [the longest x16 48.1 us: per_fragment(): columns = jnp.take(chol_vec, orbitals, axis=2)]
    all_gather x1, waiting for transfers between devices: 44.3 us -> 0.02 us  [per_device(): all_coef = lax.all_gather(lno_coef, 'orb', axis=0, tiled=True)]
    gather x17 -> x4, local copies, waits for them, and re-layouts: 115 us -> 71 us  [the longest x2 51 us: per_device(): picked = jnp.take(chol_t, domain, axis=0)]
    dot_general x17 -> x3, matrix products: 42.7 us -> 19.5 us  [the longest x1 8.2 us: per_device(): jnp.einsum('fsk,fsa->fka', picked, masked, preferred_element_type=jnp.flo...]
    all_to_all x1, waiting for transfers between devices: 16.6 us -> 0.01 us  [per_device(): lax.all_to_all(half, 'orb', split_axis=0, concat_axis=0, tiled=True)]
  transfers between devices with their start and end apart: 4 -> 3, of which waited for: 3 -> 1; matrix products, arithmetic and copies ran while one was open for 8% -> 40% of each run, Pallas kernels for 0% -> 0%
where the time goes in v1:
time: 202 us; the launch traced here: 201 us
  local copies, waits for them, and re-layouts  78.5 us (39%)
  blocking collectives  59.9 us (30%)
  matrix products  19.5 us (10%)
  waiting for transfers between devices  15.9 us (8%)
  between operations  14.8 us (7%)
  other arithmetic  7.04 us (3%)
  starting transfers between devices  5.6 us (3%)
    unnamed x1, blocking collectives  59.9 us
    gather x2, local copies, waits for them, and re-layouts, per_device(): picked = jnp.take(chol_t, domain, axis=0)  51 us
    gather x2, local copies, waits for them, and re-layouts, per_device(): domain_rows = jnp.take(received.reshape(-1, lno_width), flat_rows, axis=0)  20 us
    psum x1, waiting for transfers between devices, per_device(): lax.psum(dressing_part, 'chol') * norm_factor  15.2 us
    dot_general x1, matrix products, per_device(): jnp.einsum('fsk,fsa->fka', picked, masked, preferred_element_type=jnp.flo...  8.2 us
    dot_general x1, matrix products, per_device(): lax.dot_general(weighted.reshape(-1, lno_width), received.reshape(-1, lno...  7.36 us
    all_to_all x1, starting transfers between devices, per_device(): lax.all_to_all(half, 'orb', split_axis=0, concat_axis=0, tiled=True)  5.53 us
    mul x1, other arithmetic, per_device(): masked = all_coef * keep_mask  4.94 us
  transfers between devices with their start and end apart: 3, of which 1 were waited for; matrix products, arithmetic and copies ran while one was open for 40% of the time, Pallas kernels for 0%

profile of v1, /device:TPU:0, one launch (start us, length us, event | category | flops | bytes accessed | tf_op | source)
XLA Modules:
  0.0 201.3 jit_solution(7967591339381590676)
XLA Ops:
  7.2 0.0 copy-start.2
  7.2 0.0 all-gather.2.cloned.1.call-start
  7.2 0.7 all-gather.2.cloned.1.call-update
  7.9 0.8 copy.20
  8.7 2.8 %copy.18 = bf16[768,1536]{0,1:T(8,128)(2,1)S(1)} copy(bf16[768,1536]{1,0:T(8,128)(2,1)} %bitcast.40) | data formatting | bytes 4718592 | tf_op jit(solution)/shard_map/reshape | solution.py:29
  11.5 0.0 copy-done.2
  11.6 34.5 %gather_fusion = bf16[8192,768]{1,0:T(8,128)(2,1)} fusion(bf16[1536,768]{1,0:T(8,128)(2,1)S(1)} %bitcast.36, s32[8192]{0:T(1024)S(1)} %bitcast_clamp_fusion), kind=kCustom, calls=%fused_computation | custom fusion | bytes 25198592 | tf_op jit(solution)/shard_map/jit(_take)/gather | solution.py:30
  46.0 16.6 %copy.19 = bf16[8,1024,768]{1,2,0:T(8,128)(2,1)} copy(bf16[8,1024,768]{2,1,0:T(8,128)(2,1)} %bitcast.37) | data formatting | bytes 25165824 | tf_op jit(solution)/shard_map/jit(_take)/gather | solution.py:30
  62.6 0.0 copy-done.4
  62.6 0.1 iota_compare_fusion
  62.7 0.1 bitcast_compare_fusion
  62.8 0.0 all-gather.2.cloned.1.call-done
  62.8 4.9 %and_select_fusion = bf16[8,1024,384]{2,1,0:T(8,128)(2,1)S(1)} fusion(bf16[8,1024,384]{2,1,0:T(8,128)(2,1)} %all-gather.2.cloned.1.call-done, pred[8,384]{1,0:T(8,128)(4,1)S(1)} %iota_compare_fusion, pred[8,1024]{1,0:T(8,128)(4,1)S(1)} %bitcast_compare_fusion), kind=kLoop, calls=%fused_computation.4 | loop fusion | flops 6291456 | bytes 12594176 | tf_op jit(solution)/shard_map/mul | solution.py:27
  67.8 1.5 copy-done
  69.3 8.2 %fusion.9 = bf16[8,768,384]{2,1,0:T(8,128)(2,1)} fusion(bf16[8,1024,384]{2,1,0:T(8,128)(2,1)S(1)} %and_select_fusion, bf16[8,1024,768]{1,2,0:T(8,128)(2,1)S(1)} %copy-done, pred[8,1024]{1,0:T(8,128)(4,1)S(1)} %compare_and_fusion), kind=kOutput, calls=%fused_computation.13 | convolution fusion | flops 4840488960 | bytes 23601152 | tf_op jit(solution)/shard_map/fsk,fsa->fka/dot_general | solution.py:31
  77.5 0.0 copy-done.1
  77.5 5.5 %all-to-all-start = ((bf16[8,4,192,384]{3,2,1,0:T(8,128)(2,1)}), bf16[8,4,192,384]{3,2,1,0:T(8,128)(2,1)}, u32[]{:S(2)}, u32[]{:S(2)}) async-start(bf16[8,4,192,384]{3,2,1,0:T(8,128)(2,1)} %bitcast.39), calls=%async_computation | async-start | bytes 9437184 | tf_op jit(solution)/shard_map/all_to_all | solution.py:36
  83.0 0.0 all-reduce.3.cloned.1.call-start
  83.0 0.0 copy-done.5
  83.1 0.6 dynamic-slice
  84.3 0.3 dynamic-update-slice
  84.6 59.9 %all-reduce = f32[1536]{0:T(1024)S(1)} all-reduce(f32[1536]{0:T(1024)S(1)} %dynamic-update-slice), channel_id=1, replica_groups=mesh['chol'=4,'orb'=8] {'orb'}, use_global_device_ids=true, to_apply=%add | all-reduce | flops 1536 | bytes 12288
  144.5 0.1 mul.53
  144.6 0.0 all-to-all-done
  144.6 7.4 %fusion.19 = f32[384,384]{1,0:T(8,128)} fusion(bf16[8,4,192,384]{3,2,1,0:T(8,128)(2,1)} %all-to-all-done, f32[8,192]{1,0:T(8,128)S(1)} %mul.53), kind=kOutput, calls=%fused_computation.17 | convolution fusion | flops 1819017216 | bytes 5314560 | tf_op jit(solution)/shard_map/dressing/dot_general | solution.py:43
  152.0 0.0 all-reduce.3.cloned.1.call-update
  152.1 17.0 %gather_fusion.1 = bf16[4096,384]{1,0:T(8,128)(2,1)S(1)} fusion(bf16[6144,384]{1,0:T(8,128)(2,1)} %bitcast.7, s32[4096]{0:T(1024)S(1)} %bitcast_clamp_fusion.1), kind=kCustom, calls=%fused_computation.1 | custom fusion | bytes 6307840 | tf_op jit(solution)/shard_map/rotated/jit(_take)/gather | solution.py:58
  169.1 3.0 %copy.21 = bf16[4,1024,384]{1,2,0:T(8,128)(2,1)} copy(bf16[4,1024,384]{2,1,0:T(8,128)(2,1)S(1)} %bitcast.38) | data formatting | bytes 6291456 | tf_op jit(solution)/shard_map/rotated/jit(_take)/gather | solution.py:58
  172.0 3.9 %fusion.16 = bf16[4,1,384,384]{2,3,0,1:T(8,128)(2,1)S(1)} fusion(bf16[4,1024,384]{1,2,0:T(8,128)(2,1)} %copy.21, pred[4,1024]{1,0:T(4,128)(4,1)S(1)} %compare_and_fusion.1, bf16[8,1024,384]{2,1,0:T(8,128)(2,1)} %copy-done.1, s32[]{:T(128)S(6)} %select_n.57), kind=kOutput, calls=%fused_computation.16 | convolution fusion | flops 1210122240 | bytes 5115908 | tf_op jit(solution)/shard_map/rotated/sa,gsb->gab/dot_general | solution.py:59
  175.9 1.5 copy.22
  177.4 15.2 %all-reduce.3.cloned.1.call-done = f32[384,384]{1,0:T(8,128)} async-done(((f32[384,384]{1,0:T(8,128)}), f32[384,384]{1,0:T(8,128)}) %all-reduce.3.cloned.1.call-update) | async-done | bytes 589840 | tf_op jit(solution)/shard_map/dressing/psum | solution.py:49
  192.6 1.8 fusion.22
  (15 shorter events, 0.1 us)
Async XLA Ops:
  7.2 4.3 %copy-start.2 = (s32[8,1024]{1,0:T(8,128)S(1)}, s32[8,1024]{1,0:T(8,128)}, u32[]{:S(2)}) copy-start(s32[8,1024]{1,0:T(8,128)} %param.9) | copy-start | bytes 98308
  7.2 55.6 %all-gather.2.cloned.1.call-start = ((), (), s32[]{:S(2)}) async-start(), calls=%async_computation.1 | async-start | bytes 7077888 | tf_op jit(solution)/shard_map/all_gather | solution.py:26
  46.0 16.6 %copy-start.4 = (s32[8]{0:T(128)S(1)}, s32[8]{0:T(128)}, u32[]{:S(2)}) copy-start(s32[8]{0:T(128)} %param.11) | copy-start | bytes 100
  62.8 6.5 %copy-start = (bf16[8,1024,768]{1,2,0:T(8,128)(2,1)S(1)}, bf16[8,1024,768]{1,2,0:T(8,128)(2,1)}, u32[]{:S(2)}) copy-start(bf16[8,1024,768]{1,2,0:T(8,128)(2,1)} %copy.19) | copy-start | bytes 37748740
  69.3 8.2 %copy-start.1 = (bf16[8,1024,384]{2,1,0:T(8,128)(2,1)}, bf16[8,1024,384]{2,1,0:T(8,128)(2,1)S(1)}, u32[]{:S(2)}) copy-start(bf16[8,1024,384]{2,1,0:T(8,128)(2,1)S(1)} %and_select_fusion) | copy-start | bytes 18874372
  77.5 5.6 %copy-start.5 = (u32[32]{0:T(128)S(1)}, u32[32]{0:T(128)}, u32[]{:S(2)}) copy-start(u32[32]{0:T(128)} %constant.84) | copy-start | bytes 388
  77.5 6.8 %copy-start.3 = (f32[192]{0:T(256)S(1)}, f32[192]{0:T(256)}, u32[]{:S(2)}) copy-start(f32[192]{0:T(256)} %param.7) | copy-start | bytes 2308
  77.5 67.2 %all-to-all-start = ((bf16[8,4,192,384]{3,2,1,0:T(8,128)(2,1)}), bf16[8,4,192,384]{3,2,1,0:T(8,128)(2,1)}, u32[]{:S(2)}, u32[]{:S(2)}) async-start(bf16[8,4,192,384]{3,2,1,0:T(8,128)(2,1)} %bitcast.39), calls=%async_computation | async-start | bytes 9437184 | tf_op jit(solution)/shard_map/all_to_all | solution.py:36
  83.0 109.6 %all-reduce.3.cloned.1.call-start = ((), (), s32[]{:S(2)}) async-start(), calls=%async_computation.2 | async-start | bytes 1179648 | tf_op jit(solution)/shard_map/dressing/psum | solution.py:49
Sparse Core Ops, SparseCore 0:
  9.9 48.2 all-gather.1
  152.1 40.4 all-reduce.2

commit v2 on v1

v2 whole, which is shorter than its diff:
```python
import math

import jax
import jax.numpy as jnp
from jax import lax
from jax.sharding import PartitionSpec as P


def split_bf16(x):
    hi = x.astype(jnp.bfloat16)
    rest = x - hi.astype(jnp.float32)
    mid = rest.astype(jnp.bfloat16)
    lo = (rest - mid.astype(jnp.float32)).astype(jnp.bfloat16)
    return jnp.stack([hi, mid, lo])


def join_bf16(parts):
    parts = parts.astype(jnp.float32)
    return (parts[0] + parts[1]) + parts[2]


def per_device(chol_vec, env_weight, lno_coef, domain, block_fill, lno_count):
    chol_local, orb_rows, orb_total = chol_vec.shape
    frag_total, slot_total = domain.shape
    group_count = block_fill.shape[1]
    group_width = slot_total // group_count
    lno_width = lno_coef.shape[2]
    chol_size = lax.axis_size("chol")
    orb_size = lax.axis_size("orb")
    my_index = lax.axis_index("orb")
    norm_factor = 1.0 / math.sqrt(chol_local * chol_size * orb_total)

    slot_index = jnp.arange(slot_total, dtype=jnp.int32)
    slot_ok = (slot_index % group_width)[None, :] < jnp.repeat(block_fill, group_width, axis=1)
    column_ok = jnp.arange(lno_width, dtype=jnp.int32)[None, :] < lno_count[:, None]
    keep_mask = (slot_ok[:, :, None] & column_ok[:, None, :]).astype(jnp.bfloat16)

    weight_rows = -(-3 * orb_rows // lno_width)
    pad_rows = -(-weight_rows // 8) * 8
    weight_parts = split_bf16(env_weight).reshape(-1)
    weight_parts = jnp.pad(weight_parts, (0, pad_rows * lno_width - weight_parts.shape[0]))
    payload = jnp.concatenate(
        [lno_coef, weight_parts.reshape(1, pad_rows, lno_width)], axis=1
    )
    gathered = lax.all_gather(payload, "orb", axis=0, tiled=True)
    all_coef = gathered[:, :slot_total]
    weight_all = join_bf16(
        gathered[:, slot_total:].reshape(orb_size, -1)[:, : 3 * orb_rows].reshape(orb_size, 3, orb_rows).transpose(1, 0, 2)
    )
    masked = all_coef * keep_mask

    with jax.named_scope("scatter_coef"):
        groups = domain.reshape(frag_total, group_count, group_width)
        group_block = groups[:, :, 0] // orb_rows
        block_ids = jnp.arange(orb_size, dtype=jnp.int32)
        sel = group_block[:, None, :] == block_ids[None, :, None]
        present = jnp.any(sel, axis=2)
        group_of_block = jnp.argmax(sel, axis=2).astype(jnp.int32)
        local = jnp.take_along_axis(groups, group_of_block[:, :, None], axis=1)
        local = local - block_ids[None, :, None] * orb_rows
        coef_groups = masked.reshape(frag_total, group_count, group_width, lno_width)
        coef_perm = jnp.take_along_axis(coef_groups, group_of_block[:, :, None, None], axis=1)
        row_ids = jnp.arange(orb_rows, dtype=jnp.int32)
        onehot = (
            (local[:, :, None, :] == row_ids[None, None, :, None]) & present[:, :, None, None]
        ).astype(jnp.bfloat16)
        w_full = jnp.einsum(
            "fbrs,fbsa->fbra", onehot, coef_perm, preferred_element_type=jnp.float32
        ).astype(jnp.bfloat16)

    with jax.named_scope("half"):
        half = jnp.einsum(
            "kc,fca->fka",
            chol_vec.reshape(chol_local * orb_rows, orb_total),
            w_full.reshape(frag_total, orb_size * orb_rows, lno_width),
            preferred_element_type=jnp.float32,
        ).astype(jnp.bfloat16)
        half = half.reshape(frag_total, chol_local, orb_rows, lno_width)

    received = lax.all_to_all(half, "orb", split_axis=0, concat_axis=0, tiled=True)

    with jax.named_scope("dressing"):
        weighted = (
            received.astype(jnp.float32) * weight_all.reshape(orb_size, 1, orb_rows, 1)
        ).astype(jnp.bfloat16)
        dressing_part = lax.dot_general(
            weighted.reshape(-1, lno_width),
            received.reshape(-1, lno_width),
            (((0,), (0,)), ((), ())),
            preferred_element_type=jnp.float32,
        )
        dressing = (lax.psum(dressing_part, "chol") * norm_factor).astype(jnp.bfloat16)

    with jax.named_scope("rotated"):
        own_w = lax.dynamic_index_in_dim(w_full, my_index, 0, keepdims=False)
        rotated = jnp.einsum(
            "ora,ogrb->gab", own_w, received, preferred_element_type=jnp.float32
        ).astype(jnp.bfloat16)[:, None]
    return (rotated, dressing[None])


def solution(mesh):
    return jax.shard_map(
        per_device,
        mesh=mesh,
        in_specs=(P("chol", "orb", None), P("orb"), P("orb", None, None), P(), P(), P()),
        out_specs=(P("chol", "orb", None, None), P("orb", None, None)),
        check_vma=False,
    )
```

time: 202 us -> 216 us (1.069)
  waiting for transfers between devices: 15.9 us -> 129 us
  local copies, waits for them, and re-layouts: 78.5 us -> 18.4 us
  blocking collectives: 59.9 us -> 0 us
  matrix products: 19.5 us -> 34.8 us
  other arithmetic: 7.04 us -> 13.7 us
    gather x4 -> x3, local copies, waits for them, and re-layouts: 71 us -> 7.66 us  [the longest x1 6.82 us: per_device(): jnp.take_along_axis(coef_groups, group_of_block[:, :, None, None], axis=1)]
    unnamed x1 -> x0, blocking collectives: 59.9 us -> none
    all_to_all x1, waiting for transfers between devices: 0.01 us -> 53.6 us  [per_device(): lax.all_to_all(half, 'orb', split_axis=0, concat_axis=0, tiled=True)]
    all_gather x1, waiting for transfers between devices: 0.02 us -> 44 us  [per_device(): gathered = lax.all_gather(payload, 'orb', axis=0, tiled=True)]
    psum x1, waiting for transfers between devices: 15.2 us -> 31.8 us  [per_device(): lax.psum(dressing_part, 'chol') * norm_factor]
    dot_general x2 -> x3, matrix products: 12.1 us -> 27.5 us  [the longest x1 13 us: per_device(): jnp.einsum('kc,fca->fka', chol_vec.reshape(chol_local * orb_rows, orb_tot...]
    convert_element_type x0 -> x2, local copies, waits for them, and re-layouts: none -> 6.74 us  [the longest x1 6.66 us: per_device(): half = jnp.einsum('kc,fca->fka', chol_vec.reshape(chol_local * orb_rows,...]
    reshape x1 -> x2, local copies, waits for them, and re-layouts: 2.83 us -> 0.1 us  [the longest x1 0.09 us: per_device(): weight_parts = split_bf16(env_weight).reshape(-1)]
  transfers between devices with their start and end apart: 3 -> 3, of which waited for: 1 -> 3; matrix products, arithmetic and copies ran while one was open for 40% -> 6% of each run, Pallas kernels for 0% -> 0%
where the time goes in v2:
time: 216 us; the launch traced here: 215 us
  waiting for transfers between devices  129 us (60%)
  matrix products  34.8 us (16%)
  local copies, waits for them, and re-layouts  18.4 us (9%)
  between operations  14.1 us (7%)
  other arithmetic  13.7 us (6%)
  starting transfers between devices  4.86 us (2%)
    all_to_all x1, waiting for transfers between devices, per_device(): lax.all_to_all(half, 'orb', split_axis=0, concat_axis=0, tiled=True)  53.6 us
    all_gather x1, waiting for transfers between devices, per_device(): gathered = lax.all_gather(payload, 'orb', axis=0, tiled=True)  44 us
    psum x1, waiting for transfers between devices, per_device(): lax.psum(dressing_part, 'chol') * norm_factor  31.8 us
    dot_general x1, matrix products, per_device(): jnp.einsum('kc,fca->fka', chol_vec.reshape(chol_local * orb_rows, orb_tot...  13 us
    dot_general x1, matrix products, per_device(): jnp.einsum('fbrs,fbsa->fbra', onehot, coef_perm, preferred_element_type=j...  9.12 us
    dot_general x1, matrix products, per_device(): lax.dot_general(weighted.reshape(-1, lno_width), received.reshape(-1, lno...  7.27 us
    mul x1, other arithmetic, per_device(): masked = all_coef * keep_mask  6.82 us
    gather x1, local copies, waits for them, and re-layouts, per_device(): jnp.take_along_axis(coef_groups, group_of_block[:, :, None, None], axis=1)  6.82 us
  transfers between devices with their start and end apart: 3, of which 3 were waited for; matrix products, arithmetic and copies ran while one was open for 6% of the time, Pallas kernels for 0%

profile of v2, /device:TPU:0, one launch (start us, length us, event | category | flops | bytes accessed | tf_op | source)
XLA Modules:
  0.0 215.3 jit_solution(14774372845133835380)
XLA Ops:
  7.2 0.0 all-gather.2.cloned.1.call-start
  7.2 0.9 fusion.24
  8.1 0.1 reshape.162
  8.2 2.1 pad_maximum_fusion
  10.3 0.0 all-gather.2.cloned.1.call-update
  10.4 0.8 copy.40
  11.1 0.8 copy.53
  11.9 0.1 copy.48
  12.0 0.9 iota_reduce_fusion
  12.9 0.1 reshape.170
  13.0 0.8 gather_fusion
  13.8 0.2 fusion.15
  14.0 0.7 iota_compare_fusion.2
  14.8 0.1 bitcast_compare_fusion
  14.8 0.1 fusion.14
  14.9 44.0 %all-gather.2.cloned.1.call-done = bf16[8,1032,384]{2,1,0:T(8,128)(2,1)} async-done(((bf16[1,1032,384]{2,1,0:T(8,128)(2,1)}), bf16[8,1032,384]{2,1,0:T(8,128)(2,1)}) %all-gather.2.cloned.1.call-update) | async-done | bytes 6340624 | tf_op jit(solution)/shard_map/all_gather | solution.py:45
  58.9 6.8 %and_select_fusion = bf16[8,1024,384]{2,1,0:T(8,128)(2,1)} fusion(bf16[8,1032,384]{2,1,0:T(8,128)(2,1)} %all-gather.2.cloned.1.call-done, pred[8,384]{1,0:T(8,128)(4,1)S(1)} %iota_compare_fusion.2, pred[8,1024]{1,0:T(8,128)(4,1)S(1)} %bitcast_compare_fusion), kind=kLoop, calls=%fused_computation.2 | loop fusion | flops 6291456 | bytes 12594176 | tf_op jit(solution)/shard_map/mul | solution.py:50
  65.8 6.8 %gather_fusion.1 = bf16[64,128,384]{2,1,0:T(8,128)(2,1)} fusion(bf16[8,8,128,384]{3,2,1,0:T(8,128)(2,1)} %bitcast.64, s32[64]{0:T(128)S(1)} %reshape.170), kind=kCustom, calls=%fused_computation.1 | custom fusion | bytes 12583424 | tf_op jit(solution)/shard_map/scatter_coef/jit(take_along_axis)/gather | solution.py:62
  72.6 9.1 %convolution_convert_fusion = bf16[8,8,192,384]{3,2,1,0:T(8,128)(2,1)} fusion(bf16[8,8,128,384]{3,2,1,0:T(8,128)(2,1)} %bitcast.62, pred[8,8]{1,0:T(8,128)(4,1)S(1)} %compare_and_fusion, s32[8,8,128]{2,1,0:T(8,128)S(1)} %fusion.14, pred[8,8]{1,0:T(8,128)(4,1)S(1)} %fusion.15), kind=kOutput, calls=%fused_computation.5 | convolution fusion | flops 1218969600 | bytes 15761536 | tf_op jit(solution)/shard_map/scatter_coef/fbrs,fbsa->fbra/dot_general | solution.py:67
  81.7 13.0 %convert_bitcast_fusion = bf16[8,768,384]{1,2,0:T(8,128)(2,1)} fusion(bf16[8,1536,384]{2,1,0:T(8,128)(2,1)} %bitcast.63, bf16[768,1536,1]{1,0,2:T(8,128)(2,1)S(1)} %bitcast.61), kind=kOutput, calls=%fused_computation.11 | convolution fusion | flops 7250116608 | bytes 16515072 | tf_op jit(solution)/shard_map/half/kc,fca->fka/dot_general | solution.py:72
  94.7 6.7 %copy.42 = bf16[8,768,384]{2,1,0:T(8,128)(2,1)} copy(bf16[8,768,384]{1,2,0:T(8,128)(2,1)} %convert_bitcast_fusion) | data formatting | bytes 9437184 | tf_op jit(solution)/shard_map/half/convert_element_type | solution.py:77
  101.4 4.6 %all-to-all-start = ((bf16[8,4,192,384]{3,2,1,0:T(8,128)(2,1)}), bf16[8,4,192,384]{3,2,1,0:T(8,128)(2,1)}, u32[]{:S(2)}, u32[]{:S(2)}) async-start(bf16[8,4,192,384]{3,2,1,0:T(8,128)(2,1)} %bitcast.65), calls=%async_computation | async-start | bytes 9437184 | tf_op jit(solution)/shard_map/all_to_all | solution.py:80
  106.0 0.2 all-reduce.3.cloned.1.call-start
  106.2 0.8 slice_bitcast_fusion
  107.1 0.1 reshape.169
  107.2 53.6 %all-to-all-done = bf16[8,4,192,384]{3,2,1,0:T(8,128)(2,1)} async-done(((bf16[8,4,192,384]{3,2,1,0:T(8,128)(2,1)}), bf16[8,4,192,384]{3,2,1,0:T(8,128)(2,1)}, u32[]{:S(2)}, u32[]{:S(2)}) %all-to-all-start) | async-done | bytes 4718624 | tf_op jit(solution)/shard_map/all_to_all | solution.py:80
  160.7 7.3 %fusion.10 = f32[384,384]{1,0:T(8,128)} fusion(bf16[8,4,192,384]{3,2,1,0:T(8,128)(2,1)} %all-to-all-done, f32[8,192]{1,0:T(8,128)S(1)} %bitcast.71), kind=kOutput, calls=%fused_computation.17 | convolution fusion | flops 1819017216 | bytes 5314560 | tf_op jit(solution)/shard_map/dressing/dot_general | solution.py:86
  168.0 0.0 all-reduce.3.cloned.1.call-update
  168.0 5.3 %fusion.9 = bf16[4,1,384,384]{2,3,0,1:T(8,128)(2,1)S(1)} fusion(bf16[8,4,192,384]{3,2,1,0:T(8,128)(2,1)} %all-to-all-done, bf16[8,8,192,384]{3,2,1,0:T(8,128)(2,1)} %convolution_convert_fusion, s32[]{:T(128)S(6)} %select_n.56), kind=kOutput, calls=%fused_computation.16 | convolution fusion | flops 1812529152 | bytes 7077892 | tf_op jit(solution)/shard_map/rotated/ora,ogrb->gab/dot_general | solution.py:96
  173.4 1.5 copy.43
  174.8 31.8 %all-reduce.3.cloned.1.call-done = f32[384,384]{1,0:T(8,128)} async-done(((f32[384,384]{1,0:T(8,128)}), f32[384,384]{1,0:T(8,128)}) %all-reduce.3.cloned.1.call-update) | async-done | bytes 589840 | tf_op jit(solution)/shard_map/dressing/psum | solution.py:92
  206.6 1.8 fusion.13
  (17 shorter events, 0.1 us)
Async XLA Ops:
  7.2 74.5 %copy-start = (bf16[4,192,1536]{2,1,0:T(8,128)(2,1)S(1)}, bf16[4,192,1536]{2,1,0:T(8,128)(2,1)}, u32[]{:S(2)}) copy-start(bf16[4,192,1536]{2,1,0:T(8,128)(2,1)} %param.6) | copy-start | bytes 7077892
  7.2 51.8 %all-gather.2.cloned.1.call-start = ((), (), s32[]{:S(2)}) async-start(), calls=%async_computation.1 | async-start | bytes 7133184 | tf_op jit(solution)/shard_map/all_gather | solution.py:45
  101.4 59.4 %all-to-all-start = ((bf16[8,4,192,384]{3,2,1,0:T(8,128)(2,1)}), bf16[8,4,192,384]{3,2,1,0:T(8,128)(2,1)}, u32[]{:S(2)}, u32[]{:S(2)}) async-start(bf16[8,4,192,384]{3,2,1,0:T(8,128)(2,1)} %bitcast.65), calls=%async_computation | async-start | bytes 9437184 | tf_op jit(solution)/shard_map/all_to_all | solution.py:80
  106.0 100.6 %all-reduce.3.cloned.1.call-start = ((), (), s32[]{:S(2)}) async-start(), calls=%async_computation.2 | async-start | bytes 1179648 | tf_op jit(solution)/shard_map/dressing/psum | solution.py:92
Sparse Core Ops, SparseCore 0:
  10.5 48.4 all-gather.1
  168.2 38.4 all-reduce.2

commit v3 on v1

v3 whole, which is shorter than its diff:
```python
import math

import jax
import jax.numpy as jnp
from jax import lax
from jax.sharding import PartitionSpec as P


def split_bf16(x):
    hi = lax.reduce_precision(x, exponent_bits=8, mantissa_bits=7)
    rest = x - hi
    mid = lax.reduce_precision(rest, exponent_bits=8, mantissa_bits=7)
    lo = rest - mid
    return jnp.stack([hi, mid, lo]).astype(jnp.bfloat16)


def join_bf16(parts):
    parts = parts.astype(jnp.float32)
    return (parts[0] + parts[1]) + parts[2]


def per_device(chol_vec, env_weight, lno_coef, domain, block_fill, lno_count):
    chol_local, orb_rows, orb_total = chol_vec.shape
    frag_total, slot_total = domain.shape
    group_count = block_fill.shape[1]
    group_width = slot_total // group_count
    lno_width = lno_coef.shape[2]
    chol_size = lax.axis_size("chol")
    orb_size = lax.axis_size("orb")
    my_index = lax.axis_index("orb")
    norm_factor = 1.0 / math.sqrt(chol_local * chol_size * orb_total)
    chunks = lno_width // 128 if lno_width % 128 == 0 else 1
    width = lno_width // chunks

    slot_index = jnp.arange(slot_total, dtype=jnp.int32)
    slot_ok = (slot_index % group_width)[None, :] < jnp.repeat(block_fill, group_width, axis=1)
    column_ok = (jnp.arange(lno_width, dtype=jnp.int32)[None, :] < lno_count[:, None]).astype(jnp.float32)

    with jax.named_scope("placement"):
        groups = domain.reshape(frag_total, group_count, group_width)
        group_block = groups[:, :, 0] // orb_rows
        block_ids = jnp.arange(orb_size, dtype=jnp.int32)
        sel = group_block[:, None, :] == block_ids[None, :, None]
        present = jnp.any(sel, axis=2)
        group_of_block = jnp.argmax(sel, axis=2).astype(jnp.int32)
        local = jnp.take_along_axis(groups, group_of_block[:, :, None], axis=1)
        local = local - block_ids[None, :, None] * orb_rows
        slot_ok_perm = jnp.take_along_axis(
            slot_ok.reshape(frag_total, group_count, group_width), group_of_block[:, :, None], axis=1
        )
        row_ids = jnp.arange(orb_rows, dtype=jnp.int32)
        onehot = (
            (local[:, :, None, :] == row_ids[None, None, :, None])
            & (present[:, :, None] & slot_ok_perm)[:, :, None, :]
        ).astype(jnp.bfloat16)

    def place(coef, hot, group_pick, mask):
        picked = jnp.take_along_axis(coef, group_pick, axis=-3)
        placed = jnp.einsum("...brs,...bsa->...bra", hot, picked, preferred_element_type=jnp.float32)
        placed = placed * mask
        return placed.astype(jnp.bfloat16).reshape(placed.shape[:-3] + (-1, placed.shape[-1]))

    own_hot = lax.dynamic_index_in_dim(onehot, my_index, 0, keepdims=False)
    own_pick = lax.dynamic_index_in_dim(group_of_block, my_index, 0, keepdims=False)
    own_mask = lax.dynamic_index_in_dim(column_ok, my_index, 0, keepdims=False)
    own_w = place(
        lno_coef[0].reshape(group_count, group_width, lno_width),
        own_hot,
        own_pick[:, None, None],
        own_mask[None, None, :],
    )

    weight_rows = -(-3 * orb_rows // width)
    pad_rows = -(-weight_rows // 8) * 8
    weight_parts = split_bf16(env_weight).reshape(-1)
    weight_parts = jnp.pad(weight_parts, (0, pad_rows * width - weight_parts.shape[0]))

    chol2d = chol_vec.reshape(chol_local * orb_rows, orb_total)
    received = []
    weighted = []
    rot_parts = []
    blocks = {}
    weight_all = None
    for k in range(chunks):
        cols = slice(k * width, (k + 1) * width)
        payload = lno_coef[:, :, cols]
        if k == 0:
            payload = jnp.concatenate([payload, weight_parts.reshape(1, pad_rows, width)], axis=1)
        gathered = lax.all_gather(payload, "orb", axis=0, tiled=True)
        if k == 0:
            weight_all = join_bf16(
                gathered[:, slot_total:]
                .reshape(orb_size, -1)[:, : 3 * orb_rows]
                .reshape(orb_size, 3, orb_rows)
                .transpose(1, 0, 2)
            )
        with jax.named_scope("half"):
            w_k = place(
                gathered[:, :slot_total].reshape(frag_total, group_count, group_width, width),
                onehot,
                group_of_block[:, :, None, None],
                column_ok[:, None, None, cols],
            )
            half = jnp.einsum("kc,fca->fka", chol2d, w_k, preferred_element_type=jnp.float32)
            half = half.astype(jnp.bfloat16).reshape(frag_total, chol_local, orb_rows, width)
        recv = lax.all_to_all(half, "orb", split_axis=0, concat_axis=0, tiled=True)
        with jax.named_scope("dressing"):
            wtd = (recv.astype(jnp.float32) * weight_all.reshape(orb_size, 1, orb_rows, 1)).astype(jnp.bfloat16)
            received.append(recv.reshape(-1, width))
            weighted.append(wtd.reshape(-1, width))
            for j in range(k + 1):
                for a_i, b_i in {(k, j), (j, k)}:
                    blocks[(a_i, b_i)] = lax.dot_general(
                        weighted[a_i], received[b_i], (((0,), (0,)), ((), ())),
                        preferred_element_type=jnp.float32,
                    )
        with jax.named_scope("rotated"):
            rot_parts.append(
                jnp.einsum(
                    "ora,ogrb->gab", own_w.reshape(orb_size, orb_rows, lno_width), recv,
                    preferred_element_type=jnp.float32,
                ).astype(jnp.bfloat16)
            )

    with jax.named_scope("dressing"):
        dressing_part = jnp.concatenate(
            [jnp.concatenate([blocks[(i, j)] for j in range(chunks)], axis=1) for i in range(chunks)], axis=0
        )
        dressing = (lax.psum(dressing_part, "chol") * norm_factor).astype(jnp.bfloat16)
    rotated = jnp.concatenate(rot_parts, axis=2)[:, None]
    return (rotated, dressing[None])


def solution(mesh):
    return jax.shard_map(
        per_device,
        mesh=mesh,
        in_specs=(P("chol", "orb", None), P("orb"), P("orb", None, None), P(), P(), P()),
        out_specs=(P("chol", "orb", None, None), P("orb", None, None)),
        check_vma=False,
    )
```

time: 202 us -> 235 us (1.16)
  waiting for transfers between devices: 15.9 us -> 104 us
  blocking collectives: 59.9 us -> 0 us
  local copies, waits for them, and re-layouts: 78.5 us -> 33 us
  matrix products: 19.5 us -> 60.5 us
  starting transfers between devices: 5.6 us -> 13.7 us
    all_gather x1 -> x3, waiting for transfers between devices: 0.02 us -> 60.8 us  [per_device(): gathered = lax.all_gather(payload, 'orb', axis=0, tiled=True)]
    unnamed x1 -> x0, blocking collectives: 59.9 us -> none
    gather x4 -> x8, local copies, waits for them, and re-layouts: 71 us -> 14.5 us  [the longest x5 12.9 us: place(): picked = jnp.take_along_axis(coef, group_pick, axis=-3)]
    dot_general x3 -> x19, matrix products: 19.5 us -> 60.5 us  [the longest x9 28.6 us: per_device(): lax.dot_general(weighted[a_i], received[b_i], (((0,), (0,)), ((), ())), p...]
    psum x1, waiting for transfers between devices: 15.2 us -> 31.9 us  [per_device(): lax.psum(dressing_part, 'chol') * norm_factor]
    all_to_all x1 -> x3, waiting for transfers between devices: 0.01 us -> 10.9 us  [per_device(): recv = lax.all_to_all(half, 'orb', split_axis=0, concat_axis=0, tiled=True)]
    convert_element_type x0 -> x5, local copies, waits for them, and re-layouts: none -> 9.39 us  [the longest x3 7.88 us: per_device(): half.astype(jnp.bfloat16).reshape(frag_total, chol_local, orb_rows, width)]
    all_to_all x1 -> x3, starting transfers between devices: 5.53 us -> 13.3 us  [per_device(): recv = lax.all_to_all(half, 'orb', split_axis=0, concat_axis=0, tiled=True)]
  transfers between devices with their start and end apart: 3 -> 7, of which waited for: 1 -> 6; matrix products, arithmetic and copies ran while one was open for 40% -> 35% of each run, Pallas kernels for 0% -> 0%
where the time goes in v3:
time: 235 us; the launch traced here: 234 us
  waiting for transfers between devices  104 us (44%)
  matrix products  60.5 us (26%)
  local copies, waits for them, and re-layouts  33 us (14%)
  between operations  14.2 us (6%)
  starting transfers between devices  13.7 us (6%)
  other arithmetic  8.66 us (4%)
    all_gather x3, waiting for transfers between devices, per_device(): gathered = lax.all_gather(payload, 'orb', axis=0, tiled=True)  60.8 us
    psum x1, waiting for transfers between devices, per_device(): lax.psum(dressing_part, 'chol') * norm_factor  31.9 us
    dot_general x9, matrix products, per_device(): lax.dot_general(weighted[a_i], received[b_i], (((0,), (0,)), ((), ())), p...  28.6 us
    all_to_all x3, starting transfers between devices, per_device(): recv = lax.all_to_all(half, 'orb', split_axis=0, concat_axis=0, tiled=True)  13.3 us
    gather x5, local copies, waits for them, and re-layouts, place(): picked = jnp.take_along_axis(coef, group_pick, axis=-3)  12.9 us
    dot_general x4, matrix products, place(): jnp.einsum('...brs,...bsa->...bra', hot, picked, preferred_element_type=j...  12.2 us
    dot_general x3, matrix products, per_device(): jnp.einsum('kc,fca->fka', chol2d, w_k, preferred_element_type=jnp.float32)  11.6 us
    all_to_all x3, waiting for transfers between devices, per_device(): recv = lax.all_to_all(half, 'orb', split_axis=0, concat_axis=0, tiled=True)  10.9 us
  transfers between devices with their start and end apart: 7, of which 6 were waited for; matrix products, arithmetic and copies ran while one was open for 35% of the time, Pallas kernels for 0%

profile of v3, /device:TPU:0, one launch (start us, length us, event | category | flops | bytes accessed | tf_op | source)
XLA Modules:
  0.0 234.4 jit_solution(5550753373490835491)
XLA Ops:
  15.2 2.8 %fusion = pred[8,8,192,128]{3,2,1,0:T(32,128)(4,1)} fusion(s32[8,8,128]{2,1,0:T(8,128)S(1)} %fusion.53, pred[8,8,128]{2,1,0:T(8,128)(4,1)S(1)} %fusion.55), kind=kLoop, calls=%fused_computation.10 | loop fusion | flops 3145728 | bytes 1613824 | tf_op jit(solution)/shard_map/placement/and | solution.py:53
  17.9 23.2 %all-gather.6.cloned.1.call-done = bf16[8,1024,128]{2,1,0:T(8,128)(2,1)} async-done(((bf16[1,1024,128]{2,1,0:T(8,128)(2,1)}), bf16[8,1024,128]{2,1,0:T(8,128)(2,1)}) %all-gather.6.cloned.1.call-update) | async-done | bytes 2097168 | tf_op jit(solution)/shard_map/all_gather | solution.py:89
  41.1 3.8 %gather_fusion.4 = bf16[64,128,128]{2,1,0:T(8,128)(2,1)} fusion(bf16[8,8,128,128]{3,2,1,0:T(8,128)(2,1)} %bitcast.181, s32[64]{0:T(128)S(1)} %reshape.305), kind=kCustom, calls=%fused_computation.1.clone | custom fusion | bytes 4194816 | tf_op jit(solution)/shard_map/half/jit(take_along_axis)/gather | solution.py:58
  44.9 3.4 %multiply_convert_fusion.1 = bf16[8,8,192,128]{3,2,1,0:T(8,128)(2,1)S(1)} fusion(f32[8,128]{1,0:T(8,128)S(1)} %get-tuple-element.22, bf16[8,8,128,128]{3,2,1,0:T(8,128)(2,1)} %bitcast.183, pred[8,8]{1,0:T(8,128)(4,1)S(1)} %and_bitcast_fusion, s32[8,8,128]{2,1,0:T(8,128)S(1)} %fusion.53, pred[8,8,128]{2,1,0:T(8,128)(4,1)S(1)} %fusion.55), kind=kOutput, calls=%fused_computation.7 | convolution fusion | flops 409993216 | bytes 5288000 | tf_op jit(solution)/shard_map/half/...brs,...bsa->...bra/dot_general | solution.py:59
  48.4 3.9 %fusion.26 = bf16[8,768,128]{1,2,0:T(8,128)(2,1)} fusion(bf16[8,1536,128]{2,1,0:T(8,128)(2,1)S(1)} %bitcast.198, bf16[768,1536,1]{1,0,2:T(8,128)(2,1)S(1)} %bitcast.171), kind=kOutput, calls=%fused_computation.43 | convolution fusion | flops 2416705536 | bytes 7077888 | tf_op jit(solution)/shard_map/half/kc,fca->fka/dot_general | solution.py:104
  52.3 2.6 %copy.97 = bf16[8,768,128]{2,1,0:T(8,128)(2,1)} copy(bf16[8,768,128]{1,2,0:T(8,128)(2,1)} %fusion.26) | data formatting | bytes 3145728 | tf_op jit(solution)/shard_map/half/convert_element_type | solution.py:105
  54.9 4.6 %all-to-all-start.1 = ((bf16[8,4,192,128]{3,2,1,0:T(8,128)(2,1)}), bf16[8,4,192,128]{3,2,1,0:T(8,128)(2,1)}, u32[]{:S(2)}, u32[]{:S(2)}) async-start(bf16[8,4,192,128]{3,2,1,0:T(8,128)(2,1)} %bitcast.175), calls=%async_computation.1 | async-start | bytes 3145728 | tf_op jit(solution)/shard_map/all_to_all | solution.py:106
  63.0 17.7 %all-gather.8.cloned.1.call-done = bf16[8,1024,128]{2,1,0:T(8,128)(2,1)} async-done(((bf16[1,1024,128]{2,1,0:T(8,128)(2,1)}), bf16[8,1024,128]{2,1,0:T(8,128)(2,1)}) %all-gather.8.cloned.1.call-update) | async-done | bytes 2097168 | tf_op jit(solution)/shard_map/all_gather | solution.py:89
  80.7 3.8 %gather_fusion.5 = bf16[64,128,128]{2,1,0:T(8,128)(2,1)} fusion(bf16[8,8,128,128]{3,2,1,0:T(8,128)(2,1)} %bitcast.180, s32[64]{0:T(128)S(1)} %reshape.305), kind=kCustom, calls=%fused_computation.2.clone | custom fusion | bytes 4194816 | tf_op jit(solution)/shard_map/half/jit(take_along_axis)/gather | solution.py:58
  84.5 3.4 %multiply_convert_fusion = bf16[8,8,192,128]{3,2,1,0:T(8,128)(2,1)S(1)} fusion(f32[8,128]{1,0:T(8,128)} %get-tuple-element.21, bf16[8,8,128,128]{3,2,1,0:T(8,128)(2,1)} %bitcast.184, pred[8,8]{1,0:T(8,128)(4,1)} %copy-done.10, s32[8,8,128]{2,1,0:T(8,128)} %copy-done.3, pred[8,8,128]{2,1,0:T(8,128)(4,1)S(1)} %fusion.55), kind=kOutput, calls=%fused_computation.6 | convolution fusion | flops 409993216 | bytes 5288000 | tf_op jit(solution)/shard_map/half/...brs,...bsa->...bra/dot_general | solution.py:59
  87.9 3.9 %fusion.27 = bf16[8,768,128]{1,2,0:T(8,128)(2,1)} fusion(bf16[8,1536,128]{2,1,0:T(8,128)(2,1)S(1)} %bitcast.199, bf16[768,1536,1]{1,0,2:T(8,128)(2,1)S(1)} %bitcast.172), kind=kOutput, calls=%fused_computation.44 | convolution fusion | flops 2416705536 | bytes 7077888 | tf_op jit(solution)/shard_map/half/kc,fca->fka/dot_general | solution.py:104
  94.4 19.9 %all-gather.4.cloned.1.call-done = bf16[8,1032,128]{2,1,0:T(8,128)(2,1)} async-done(((bf16[1,1032,128]{2,1,0:T(8,128)(2,1)}), bf16[8,1032,128]{2,1,0:T(8,128)(2,1)}) %all-gather.4.cloned.1.call-update) | async-done | bytes 2113552 | tf_op jit(solution)/shard_map/all_gather | solution.py:89
  114.3 3.1 %slice.65 = bf16[8,1024,128]{2,1,0:T(8,128)(2,1)} slice(bf16[8,1032,128]{2,1,0:T(8,128)(2,1)} %all-gather.4.cloned.1.call-done), slice={[0:8], [0:1024], [0:128]} | slice | bytes 4194304 | tf_op jit(solution)/shard_map/half/slice | solution.py:99
  117.4 3.7 %gather_fusion.3 = bf16[64,128,128]{2,1,0:T(8,128)(2,1)} fusion(bf16[8,8,128,128]{3,2,1,0:T(8,128)(2,1)} %bitcast.173, s32[64]{0:T(128)S(1)} %reshape.305), kind=kCustom, calls=%fused_computation.clone | custom fusion | bytes 4194816 | tf_op jit(solution)/shard_map/half/jit(take_along_axis)/gather | solution.py:58
  121.1 4.4 %all-to-all-start.2 = ((bf16[8,4,192,128]{3,2,1,0:T(8,128)(2,1)}), bf16[8,4,192,128]{3,2,1,0:T(8,128)(2,1)}, u32[]{:S(2)}, u32[]{:S(2)}) async-start(bf16[8,4,192,128]{3,2,1,0:T(8,128)(2,1)} %bitcast.174), calls=%async_computation.2 | async-start | bytes 3145728 | tf_op jit(solution)/shard_map/all_to_all | solution.py:106
  125.6 3.5 %multiply_convert_fusion.2 = bf16[8,8,192,128]{3,2,1,0:T(8,128)(2,1)S(1)} fusion(f32[8,128]{1,0:T(8,128)S(1)} %get-tuple-element.20, bf16[8,8,128,128]{3,2,1,0:T(8,128)(2,1)} %bitcast.182, pred[8,8]{1,0:T(8,128)(4,1)S(1)} %copy-done.11, s32[8,8,128]{2,1,0:T(8,128)} %copy-done.3, pred[8,8,128]{2,1,0:T(8,128)(4,1)S(1)} %fusion.55), kind=kOutput, calls=%fused_computation.8 | convolution fusion | flops 409993216 | bytes 5288000 | tf_op jit(solution)/shard_map/half/...brs,...bsa->...bra/dot_general | solution.py:59
  129.0 3.9 %fusion.25 = bf16[8,768,128]{1,2,0:T(8,128)(2,1)} fusion(bf16[8,1536,128]{2,1,0:T(8,128)(2,1)S(1)} %bitcast.197, bf16[768,1536,1]{1,0,2:T(8,128)(2,1)S(1)} %bitcast.170), kind=kOutput, calls=%fused_computation.42 | convolution fusion | flops 2416705536 | bytes 7077888 | tf_op jit(solution)/shard_map/half/kc,fca->fka/dot_general | solution.py:104
  132.9 2.6 %copy.95 = bf16[8,768,128]{2,1,0:T(8,128)(2,1)} copy(bf16[8,768,128]{1,2,0:T(8,128)(2,1)} %fusion.25) | data formatting | bytes 3145728 | tf_op jit(solution)/shard_map/half/convert_element_type | solution.py:105
  139.2 7.4 %all-to-all-done.2 = bf16[8,4,192,128]{3,2,1,0:T(8,128)(2,1)} async-done(((bf16[8,4,192,128]{3,2,1,0:T(8,128)(2,1)}), bf16[8,4,192,128]{3,2,1,0:T(8,128)(2,1)}, u32[]{:S(2)}, u32[]{:S(2)}) %all-to-all-start.2) | async-done | bytes 1572896 | tf_op jit(solution)/shard_map/all_to_all | solution.py:106
  146.6 4.3 %all-to-all-start = ((bf16[8,4,192,128]{3,2,1,0:T(8,128)(2,1)}), bf16[8,4,192,128]{3,2,1,0:T(8,128)(2,1)}, u32[]{:S(2)}, u32[]{:S(2)}) async-start(bf16[8,4,192,128]{3,2,1,0:T(8,128)(2,1)} %bitcast.176), calls=%async_computation | async-start | bytes 3145728 | tf_op jit(solution)/shard_map/all_to_all | solution.py:106
  151.2 3.5 %fusion.36 = f32[128,128]{0,1:T(8,128)} fusion(bf16[8,4,192,128]{3,2,1,0:T(8,128)(2,1)} %all-to-all-done.1, bf16[8,4,192,128]{3,2,1,0:T(8,128)(2,1)} %all-to-all-done.2, f32[8,192]{1,0:T(8,128)S(1)} %bitcast.188), kind=kOutput, calls=%fused_computation.57 | convolution fusion | flops 203685888 | bytes 3217408 | tf_op jit(solution)/shard_map/dressing/dot_general | solution.py:113
  154.7 3.5 %fusion.40 = f32[128,128]{0,1:T(8,128)} fusion(bf16[8,4,192,128]{3,2,1,0:T(8,128)(2,1)} %all-to-all-done.2, bf16[8,4,192,128]{3,2,1,0:T(8,128)(2,1)} %all-to-all-done.1, f32[8,192]{1,0:T(8,128)S(1)} %bitcast.189), kind=kOutput, calls=%fused_computation.61 | convolution fusion | flops 203685888 | bytes 3217408 | tf_op jit(solution)/shard_map/dressing/dot_general | solution.py:113
  158.2 3.6 %fusion.39 = f32[128,128]{0,1:T(8,128)} fusion(bf16[8,4,192,128]{3,2,1,0:T(8,128)(2,1)} %all-to-all-done.1, f32[8,192]{1,0:T(8,128)S(1)} %bitcast.190), kind=kOutput, calls=%fused_computation.60 | convolution fusion | flops 203685888 | bytes 1644544 | tf_op jit(solution)/shard_map/dressing/dot_general | solution.py:113
  161.8 3.5 %fusion.37 = f32[128,128]{0,1:T(8,128)} fusion(bf16[8,4,192,128]{3,2,1,0:T(8,128)(2,1)} %all-to-all-done.2, f32[8,192]{1,0:T(8,128)S(1)} %bitcast.191), kind=kOutput, calls=%fused_computation.58 | convolution fusion | flops 203685888 | bytes 1644544 | tf_op jit(solution)/shard_map/dressing/dot_general | solution.py:113
  165.3 3.2 %fusion.33 = bf16[4,384,128]{1,2,0:T(8,128)(2,1)} fusion(bf16[8,4,192,128]{3,2,1,0:T(8,128)(2,1)} %all-to-all-done.1, bf16[8,192,384,1]{2,1,3,0:T(8,128)(2,1)S(1)} %fusion.28), kind=kOutput, calls=%fused_computation.53 | convolution fusion | flops 604176384 | bytes 3145728 | tf_op jit(solution)/shard_map/rotated/ora,ogrb->gab/dot_general | solution.py:119
  168.4 3.5 %all-to-all-done = bf16[8,4,192,128]{3,2,1,0:T(8,128)(2,1)} async-done(((bf16[8,4,192,128]{3,2,1,0:T(8,128)(2,1)}), bf16[8,4,192,128]{3,2,1,0:T(8,128)(2,1)}, u32[]{:S(2)}, u32[]{:S(2)}) %all-to-all-start) | async-done | bytes 1572896 | tf_op jit(solution)/shard_map/all_to_all | solution.py:106
  171.9 2.9 %fusion.38 = f32[128,128]{0,1:T(8,128)S(1)} fusion(bf16[8,4,192,128]{3,2,1,0:T(8,128)(2,1)} %all-to-all-done, bf16[8,4,192,128]{3,2,1,0:T(8,128)(2,1)} %all-to-all-done.1, f32[8,192]{1,0:T(8,128)S(1)} %bitcast.192), kind=kOutput, calls=%fused_computation.59 | convolution fusion | flops 203685888 | bytes 3217408 | tf_op jit(solution)/shard_map/dressing/dot_general | solution.py:113
  174.8 2.9 %fusion.42 = f32[128,128]{0,1:T(8,128)S(1)} fusion(bf16[8,4,192,128]{3,2,1,0:T(8,128)(2,1)} %all-to-all-done.1, bf16[8,4,192,128]{3,2,1,0:T(8,128)(2,1)} %all-to-all-done, f32[8,192]{1,0:T(8,128)S(1)} %bitcast.193), kind=kOutput, calls=%fused_computation.63 | convolution fusion | flops 203685888 | bytes 3217408 | tf_op jit(solution)/shard_map/dressing/dot_general | solution.py:113
  177.7 2.9 %fusion.35 = f32[128,128]{0,1:T(8,128)S(1)} fusion(bf16[8,4,192,128]{3,2,1,0:T(8,128)(2,1)} %all-to-all-done, bf16[8,4,192,128]{3,2,1,0:T(8,128)(2,1)} %all-to-all-done.2, f32[8,192]{1,0:T(8,128)S(1)} %bitcast.194), kind=kOutput, calls=%fused_computation.56 | convolution fusion | flops 203685888 | bytes 3217408 | tf_op jit(solution)/shard_map/dressing/dot_general | solution.py:113
  180.6 2.9 %fusion.43 = f32[128,128]{0,1:T(8,128)S(1)} fusion(bf16[8,4,192,128]{3,2,1,0:T(8,128)(2,1)} %all-to-all-done.2, bf16[8,4,192,128]{3,2,1,0:T(8,128)(2,1)} %all-to-all-done, f32[8,192]{1,0:T(8,128)S(1)} %bitcast.195), kind=kOutput, calls=%fused_computation.64 | convolution fusion | flops 203685888 | bytes 3217408 | tf_op jit(solution)/shard_map/dressing/dot_general | solution.py:113
  183.5 3.0 %fusion.41 = f32[128,128]{0,1:T(8,128)S(1)} fusion(bf16[8,4,192,128]{3,2,1,0:T(8,128)(2,1)} %all-to-all-done, f32[8,192]{1,0:T(8,128)S(1)} %bitcast.196), kind=kOutput, calls=%fused_computation.62 | convolution fusion | flops 203685888 | bytes 1644544 | tf_op jit(solution)/shard_map/dressing/dot_general | solution.py:113
  194.0 31.9 %all-reduce.3.cloned.1.call-done = f32[384,384]{0,1:T(8,128)} async-done(((f32[384,384]{0,1:T(8,128)}), f32[384,384]{0,1:T(8,128)}) %all-reduce.3.cloned.1.call-update) | async-done | bytes 589840 | tf_op jit(solution)/shard_map/dressing/psum | solution.py:129
  (85 shorter events, 27.1 us)
Async XLA Ops:
  7.2 41.2 %copy-start = (bf16[4,192,1536]{2,1,0:T(8,128)(2,1)S(1)}, bf16[4,192,1536]{2,1,0:T(8,128)(2,1)}, u32[]{:S(2)}) copy-start(bf16[4,192,1536]{2,1,0:T(8,128)(2,1)} %param.8) | copy-start | bytes 7077892
  7.2 3.0 %copy-start.12 = (f32[192]{0:T(256)S(1)}, f32[192]{0:T(256)}, u32[]{:S(2)}) copy-start(f32[192]{0:T(256)} %param.9) | copy-start | bytes 2308
  7.2 3.9 %copy-start.8 = (s32[8,1024]{1,0:T(8,128)S(1)}, s32[8,1024]{1,0:T(8,128)}, u32[]{:S(2)}) copy-start(s32[8,1024]{1,0:T(8,128)} %param.11) | copy-start | bytes 98308
  7.2 5.3 %copy-start.13 = (s32[8]{0:T(128)S(1)}, s32[8]{0:T(128)}, u32[]{:S(2)}) copy-start(s32[8]{0:T(128)} %param.13) | copy-start | bytes 100
  7.2 5.4 %copy-start.9 = (s32[8,8]{1,0:T(8,128)S(1)}, s32[8,8]{1,0:T(8,128)}, u32[]{:S(2)}) copy-start(s32[8,8]{1,0:T(8,128)} %param.12) | copy-start | bytes 772
  7.2 33.9 %all-gather.6.cloned.1.call-start = ((), (), s32[]{:S(2)}) async-start(), calls=%async_computation.4 | async-start | bytes 2359296 | tf_op jit(solution)/shard_map/all_gather | solution.py:89
  9.4 71.3 %all-gather.8.cloned.1.call-start = ((), (), s32[]{:S(2)}) async-start(), calls=%async_computation.5 | async-start | bytes 2359296 | tf_op jit(solution)/shard_map/all_gather | solution.py:89
  10.1 104.2 %all-gather.4.cloned.1.call-start = ((), (), s32[]{:S(2)}) async-start(), calls=%async_computation.3 | async-start | bytes 2377728 | tf_op jit(solution)/shard_map/all_gather | solution.py:89
  12.5 32.4 %copy-start.10 = (pred[8,8]{1,0:T(8,128)(4,1)}, pred[8,8]{1,0:T(8,128)(4,1)S(1)}, u32[]{:S(2)}) copy-start(pred[8,8]{1,0:T(8,128)(4,1)S(1)} %and_bitcast_fusion) | copy-start | bytes 196
  15.2 29.8 %copy-start.3 = (s32[8,8,128]{2,1,0:T(8,128)}, s32[8,8,128]{2,1,0:T(8,128)S(1)}, u32[]{:S(2)}) copy-start(s32[8,8,128]{2,1,0:T(8,128)S(1)} %fusion.53) | copy-start | bytes 98308
  54.9 4.6 %copy-start.1 = (bf16[1,1024,384]{2,1,0:T(8,128)(2,1)S(1)}, bf16[1,1024,384]{2,1,0:T(8,128)(2,1)}, u32[]{:S(2)}) copy-start(bf16[1,1024,384]{2,1,0:T(8,128)(2,1)} %param.10) | copy-start | bytes 2359300
  54.9 66.2 %all-to-all-start.1 = ((bf16[8,4,192,128]{3,2,1,0:T(8,128)(2,1)}), bf16[8,4,192,128]{3,2,1,0:T(8,128)(2,1)}, u32[]{:S(2)}, u32[]{:S(2)}) async-start(bf16[8,4,192,128]{3,2,1,0:T(8,128)(2,1)} %bitcast.175), calls=%async_computation.1 | async-start | bytes 3145728 | tf_op jit(solution)/shard_map/all_to_all | solution.py:106
  121.1 4.4 %copy-start.11 = (pred[8,8]{1,0:T(8,128)(4,1)S(1)}, pred[8,8]{1,0:T(8,128)(4,1)}, u32[]{:S(2)}) copy-start(pred[8,8]{1,0:T(8,128)(4,1)} %copy-done.10) | copy-start | bytes 196
  121.1 25.5 %all-to-all-start.2 = ((bf16[8,4,192,128]{3,2,1,0:T(8,128)(2,1)}), bf16[8,4,192,128]{3,2,1,0:T(8,128)(2,1)}, u32[]{:S(2)}, u32[]{:S(2)}) async-start(bf16[8,4,192,128]{3,2,1,0:T(8,128)(2,1)} %bitcast.174), calls=%async_computation.2 | async-start | bytes 3145728 | tf_op jit(solution)/shard_map/all_to_all | solution.py:106
  146.6 25.3 %all-to-all-start = ((bf16[8,4,192,128]{3,2,1,0:T(8,128)(2,1)}), bf16[8,4,192,128]{3,2,1,0:T(8,128)(2,1)}, u32[]{:S(2)}, u32[]{:S(2)}) async-start(bf16[8,4,192,128]{3,2,1,0:T(8,128)(2,1)} %bitcast.176), calls=%async_computation | async-start | bytes 3145728 | tf_op jit(solution)/shard_map/all_to_all | solution.py:106
  150.9 74.9 %all-reduce.3.cloned.1.call-start = ((), (), s32[]{:S(2)}) async-start(), calls=%async_computation.6 | async-start | bytes 1179648 | tf_op jit(solution)/shard_map/dressing/psum | solution.py:129
  183.5 3.1 %copy-start.4 = (f32[128,128]{0,1:T(8,128)S(1)}, f32[128,128]{0,1:T(8,128)}, u32[]{:S(2)}) copy-start(f32[128,128]{0,1:T(8,128)} %fusion.36) | copy-start | bytes 196612
  183.5 3.1 %copy-start.5 = (f32[128,128]{0,1:T(8,128)S(1)}, f32[128,128]{0,1:T(8,128)}, u32[]{:S(2)}) copy-start(f32[128,128]{0,1:T(8,128)} %fusion.40) | copy-start | bytes 196612
  183.5 3.1 %copy-start.6 = (f32[128,128]{0,1:T(8,128)S(1)}, f32[128,128]{0,1:T(8,128)}, u32[]{:S(2)}) copy-start(f32[128,128]{0,1:T(8,128)} %fusion.39) | copy-start | bytes 196612
  183.5 3.1 %copy-start.7 = (f32[128,128]{0,1:T(8,128)S(1)}, f32[128,128]{0,1:T(8,128)}, u32[]{:S(2)}) copy-start(f32[128,128]{0,1:T(8,128)} %fusion.37) | copy-start | bytes 196612
  189.9 2.5 %copy-start.2 = (bf16[4,384,128]{1,2,0:T(8,128)(2,1)S(1)}, bf16[4,384,128]{1,2,0:T(8,128)(2,1)}, u32[]{:S(2)}) copy-start(bf16[4,384,128]{1,2,0:T(8,128)(2,1)} %fusion.33) | copy-start | bytes 1179652
Sparse Core Ops, SparseCore 0:
  10.5 30.5 all-gather.5
  43.0 37.6 all-gather.7
  83.2 31.1 all-gather.3
  187.6 38.2 all-reduce.2

commit v4 on v1

v4 whole, which is shorter than its diff:
```python
import math

import jax
import jax.numpy as jnp
from jax import lax
from jax.sharding import PartitionSpec as P


def split_bf16(x):
    hi = lax.reduce_precision(x, exponent_bits=8, mantissa_bits=7)
    rest = x - hi
    mid = lax.reduce_precision(rest, exponent_bits=8, mantissa_bits=7)
    lo = rest - mid
    return jnp.stack([hi, mid, lo]).astype(jnp.bfloat16)


def join_bf16(parts):
    parts = parts.astype(jnp.float32)
    return (parts[0] + parts[1]) + parts[2]


def swap(x, axis, size, step):
    return lax.ppermute(x, axis, [(i, i ^ step) for i in range(size)])


def per_device(chol_vec, env_weight, lno_coef, domain, block_fill, lno_count):
    chol_local, orb_rows, orb_total = chol_vec.shape
    frag_total, slot_total = domain.shape
    group_count = block_fill.shape[1]
    group_width = slot_total // group_count
    lno_width = lno_coef.shape[2]
    chol_size = lax.axis_size("chol")
    orb_size = lax.axis_size("orb")
    assert orb_size & (orb_size - 1) == 0 and chol_size & (chol_size - 1) == 0
    assert frag_total == orb_size
    my_index = lax.axis_index("orb")
    norm_factor = 1.0 / math.sqrt(chol_local * chol_size * orb_total)

    slot_index = jnp.arange(slot_total, dtype=jnp.int32)
    slot_ok = (slot_index % group_width)[None, :] < jnp.repeat(block_fill, group_width, axis=1)
    column_ok = (jnp.arange(lno_width, dtype=jnp.int32)[None, :] < lno_count[:, None]).astype(jnp.float32)

    with jax.named_scope("placement"):
        groups = domain.reshape(frag_total, group_count, group_width)
        group_block = groups[:, :, 0] // orb_rows
        block_ids = jnp.arange(orb_size, dtype=jnp.int32)
        sel = group_block[:, None, :] == block_ids[None, :, None]
        present = jnp.any(sel, axis=2)
        group_of_block = jnp.argmax(sel, axis=2).astype(jnp.int32)
        local = jnp.take_along_axis(groups, group_of_block[:, :, None], axis=1)
        local = local - block_ids[None, :, None] * orb_rows
        slot_ok_perm = jnp.take_along_axis(
            slot_ok.reshape(frag_total, group_count, group_width), group_of_block[:, :, None], axis=1
        )
        row_ids = jnp.arange(orb_rows, dtype=jnp.int32)
        onehot = (
            (local[:, :, None, :] == row_ids[None, None, :, None])
            & (present[:, :, None] & slot_ok_perm)[:, :, None, :]
        ).astype(jnp.bfloat16)

    def placed_coef(coef, frag):
        hot = lax.dynamic_index_in_dim(onehot, frag, 0, keepdims=False)
        pick = lax.dynamic_index_in_dim(group_of_block, frag, 0, keepdims=False)
        mask = lax.dynamic_index_in_dim(column_ok, frag, 0, keepdims=False)
        picked = jnp.take_along_axis(
            coef.reshape(group_count, group_width, lno_width), pick[:, None, None], axis=0
        )
        placed = jnp.einsum("brs,bsa->bra", hot, picked, preferred_element_type=jnp.float32)
        return (placed * mask).astype(jnp.bfloat16).reshape(orb_total, lno_width)

    chol2d = chol_vec.reshape(chol_local * orb_rows, orb_total)

    def half_of(coef, frag):
        with jax.named_scope("half"):
            return jnp.dot(
                chol2d, placed_coef(coef, frag), preferred_element_type=jnp.float32
            ).astype(jnp.bfloat16)

    own_coef = lno_coef[0]
    own_placed = placed_coef(own_coef, my_index)

    weight_rows = -(-3 * orb_rows // lno_width)
    pad_rows = -(-weight_rows // 8) * 8
    weight_parts = split_bf16(env_weight).reshape(-1)
    weight_parts = jnp.pad(weight_parts, (0, pad_rows * lno_width - weight_parts.shape[0]))
    payload = jnp.concatenate([own_coef, weight_parts.reshape(pad_rows, lno_width)], axis=0)

    def absorb(acc, rows, weights, block):
        dress, rot = acc
        with jax.named_scope("dressing"):
            wtd = (
                rows.reshape(chol_local, orb_rows, lno_width).astype(jnp.float32)
                * weights[None, :, None]
            ).astype(jnp.bfloat16)
            dress = dress + lax.dot_general(
                wtd.reshape(-1, lno_width), rows, (((0,), (0,)), ((), ())),
                preferred_element_type=jnp.float32,
            )
        with jax.named_scope("rotated"):
            coef_rows = lax.dynamic_slice_in_dim(own_placed, block * orb_rows, orb_rows)
            rot = rot + jnp.einsum(
                "ra,grb->gab", coef_rows, rows.reshape(chol_local, orb_rows, lno_width),
                preferred_element_type=jnp.float32,
            )
        return dress, rot

    acc = (
        jnp.zeros((lno_width, lno_width), jnp.float32),
        jnp.zeros((chol_local, lno_width, lno_width), jnp.float32),
    )
    acc = absorb(acc, half_of(own_coef, my_index), env_weight, my_index)
    steps = sorted(range(1, orb_size), key=lambda s: (bin(s).count("1"), s))
    for step in steps:
        partner = my_index ^ step
        got = swap(payload, "orb", orb_size, step)
        half = half_of(got[:slot_total], partner)
        back = swap(half, "orb", orb_size, step)
        weights = join_bf16(got[slot_total:].reshape(-1)[: 3 * orb_rows].reshape(3, orb_rows))
        acc = absorb(acc, back, weights, partner)

    dress, rot = acc
    with jax.named_scope("chol_sum"):
        step = 1
        while step < chol_size:
            dress = dress + swap(dress, "chol", chol_size, step)
            step *= 2
    dressing = (dress * norm_factor).astype(jnp.bfloat16)
    rotated = rot.astype(jnp.bfloat16)[:, None]
    return (rotated, dressing[None])


def solution(mesh):
    return jax.shard_map(
        per_device,
        mesh=mesh,
        in_specs=(P("chol", "orb", None), P("orb"), P("orb", None, None), P(), P(), P()),
        out_specs=(P("chol", "orb", None, None), P("orb", None, None)),
        check_vma=False,
    )
```

time: 202 us -> 238 us (1.18)
  waiting for transfers between devices: 15.9 us -> 110 us
  blocking collectives: 59.9 us -> 0 us
  local copies, waits for them, and re-layouts: 78.5 us -> 36 us
  matrix products: 19.5 us -> 56.3 us
  starting transfers between devices: 5.6 us -> 20.7 us
  between operations: 14.8 us -> 1.38 us
  other arithmetic: 7.04 us -> 12.8 us
    ppermute x0 -> x16, waiting for transfers between devices: none -> 110 us  [swap(): return lax.ppermute(x, axis, [(i, i ^ step) for i in range(size)])]
    unnamed x1 -> x0, blocking collectives: 59.9 us -> none
    gather x4 -> x11, local copies, waits for them, and re-layouts: 71 us -> 14.5 us  [the longest x8 12.8 us: placed_coef(): jnp.take_along_axis(coef.reshape(group_count, group_width, lno_width), pi...]
    dot_general x3 -> x32, matrix products: 19.5 us -> 56.3 us  [the longest x8 22.5 us: absorb(): jnp.einsum('ra,grb->gab', coef_rows, rows.reshape(chol_local, orb_rows, l...]
    ppermute x0 -> x16, starting transfers between devices: none -> 20.7 us  [swap(): return lax.ppermute(x, axis, [(i, i ^ step) for i in range(size)])]
    psum x1 -> x0, waiting for transfers between devices: 15.2 us -> none  [per_device(): lax.psum(dressing_part, 'chol') * norm_factor]
    slice x0 -> x22, local copies, waits for them, and re-layouts: none -> 13.2 us  [the longest x8 8.42 us: per_device(): half = half_of(got[:slot_total], partner)]
    all_to_all x1 -> x0, starting transfers between devices: 5.53 us -> none  [per_device(): lax.all_to_all(half, 'orb', split_axis=0, concat_axis=0, tiled=True)]
  transfers between devices with their start and end apart: 3 -> 16, of which waited for: 1 -> 9; matrix products, arithmetic and copies ran while one was open for 40% -> 21% of each run, Pallas kernels for 0% -> 0%
where the time goes in v4:
time: 238 us; the launch traced here: 237 us
  waiting for transfers between devices  110 us (46%)
  matrix products  56.3 us (24%)
  local copies, waits for them, and re-layouts  36 us (15%)
  starting transfers between devices  20.7 us (9%)
  other arithmetic  12.8 us (5%)
    ppermute x16, waiting for transfers between devices, swap(): return lax.ppermute(x, axis, [(i, i ^ step) for i in range(size)])  110 us
    dot_general x8, matrix products, absorb(): jnp.einsum('ra,grb->gab', coef_rows, rows.reshape(chol_local, orb_rows, l...  22.5 us
    ppermute x16, starting transfers between devices, swap(): return lax.ppermute(x, axis, [(i, i ^ step) for i in range(size)])  20.7 us
    dot_general x8, matrix products, half_of(): jnp.dot(chol2d, placed_coef(coef, frag), preferred_element_type=jnp.float32)  15 us
    dot_general x8, matrix products, placed_coef(): jnp.einsum('brs,bsa->bra', hot, picked, preferred_element_type=jnp.float32)  13.3 us
    gather x8, local copies, waits for them, and re-layouts, placed_coef(): jnp.take_along_axis(coef.reshape(group_count, group_width, lno_width), pi...  12.8 us
    slice x8, local copies, waits for them, and re-layouts, per_device(): half = half_of(got[:slot_total], partner)  8.42 us
    dot_general x8, matrix products, absorb(): lax.dot_general(wtd.reshape(-1, lno_width), rows, (((0,), (0,)), ((), ())...  5.62 us
  transfers between devices with their start and end apart: 16, of which 9 were waited for; matrix products, arithmetic and copies ran while one was open for 21% of the time, Pallas kernels for 0%

profile of v4, /device:TPU:0, one launch (start us, length us, event | category | flops | bytes accessed | tf_op | source)
XLA Modules:
  0.0 237.2 jit_solution(18305559374551981212)
XLA Ops:
  1.7 2.2 pad_maximum_fusion
  3.8 3.3 %collective-permute-start.12 = (bf16[1032,384]{1,0:T(8,128)(2,1)}, bf16[1032,384]{1,0:T(8,128)(2,1)}, u32[]{:S(2)}, u32[]{:S(2)}) collective-permute-start(bf16[1032,384]{1,0:T(8,128)(2,1)} %pad_maximum_fusion), channel_id=1, source_target_pairs={{0,7},{1,6},{2,5},{3,4},{4,3},{5,2},{6,1},{7,0},{8,15},{9,14},{10,... | collective-permute-start | bytes 2377736 | tf_op jit(solution)/shard_map/ppermute | solution.py:23
  24.1 3.0 %fusion.85 = f32[4,384,384]{2,1,0:T(8,128)} fusion(bf16[4,192,384]{2,1,0:T(8,128)(2,1)S(1)} %bitcast.280, bf16[1536,384]{1,0:T(8,128)(2,1)} %bitcast.288, s32[]{:T(128)S(6)} %select_n.132), kind=kOutput, calls=%fused_computation.123 | convolution fusion | flops 226492416 | bytes 3096580 | tf_op jit(solution)/shard_map/rotated/ra,grb->gab/dot_general | solution.py:101
  28.8 14.7 %collective-permute-done.10 = bf16[1032,384]{1,0:T(8,128)(2,1)} collective-permute-done((bf16[1032,384]{1,0:T(8,128)(2,1)}, bf16[1032,384]{1,0:T(8,128)(2,1)}, u32[]{:S(2)}, u32[]{:S(2)}) %collective-permute-start.10) | collective-permute-done | bytes 792608 | tf_op jit(solution)/shard_map/ppermute | solution.py:23
  44.4 15.3 %collective-permute-done.8 = bf16[1032,384]{1,0:T(8,128)(2,1)} collective-permute-done((bf16[1032,384]{1,0:T(8,128)(2,1)}, bf16[1032,384]{1,0:T(8,128)(2,1)}, u32[]{:S(2)}, u32[]{:S(2)}) %collective-permute-start.8) | collective-permute-done | bytes 792608 | tf_op jit(solution)/shard_map/ppermute | solution.py:23
  61.3 15.4 %collective-permute-done.4 = bf16[1032,384]{1,0:T(8,128)(2,1)} collective-permute-done((bf16[1032,384]{1,0:T(8,128)(2,1)}, bf16[1032,384]{1,0:T(8,128)(2,1)}, u32[]{:S(2)}, u32[]{:S(2)}) %collective-permute-start.4) | collective-permute-done | bytes 792608 | tf_op jit(solution)/shard_map/ppermute | solution.py:23
  83.3 2.0 fusion.12
  90.0 2.0 fusion.11
  94.9 1.8 multiply_convert_fusion.2
  96.7 2.0 fusion.10
  101.5 2.0 multiply_convert_fusion.3
  103.5 2.0 fusion.9
  108.2 1.8 multiply_convert_fusion.4
  110.0 1.9 fusion.8
  116.5 2.0 fusion.7
  123.0 2.0 fusion.6
  124.9 2.3 collective-permute-start.5
  131.2 10.1 %collective-permute-done.5 = bf16[768,384]{0,1:T(8,128)(2,1)S(1)} collective-permute-done((bf16[768,384]{0,1:T(8,128)(2,1)S(1)}, bf16[768,384]{0,1:T(8,128)(2,1)S(1)}, u32[]{:S(2)}, u32[]{:S(2)}) %collective-permute-start.5) | collective-permute-done | bytes 589856 | tf_op jit(solution)/shard_map/ppermute | solution.py:23
  141.3 3.0 %collective-permute-start.11 = (bf16[768,384]{0,1:T(8,128)(2,1)}, bf16[768,384]{0,1:T(8,128)(2,1)S(1)}, u32[]{:S(2)}, u32[]{:S(2)}) collective-permute-start(bf16[768,384]{0,1:T(8,128)(2,1)} %fusion.11), channel_id=1, source_target_pairs={{0,6},{1,7},{2,4},{3,5},{4,2},{5,3},{6,0},{7,1},{8,14},{9,15},{10,... | collective-permute-start | bytes 1769480 | tf_op jit(solution)/shard_map/ppermute | solution.py:23
  145.4 7.4 %collective-permute-done.9 = bf16[768,384]{0,1:T(8,128)(2,1)S(1)} collective-permute-done((bf16[768,384]{0,1:T(8,128)(2,1)}, bf16[768,384]{0,1:T(8,128)(2,1)S(1)}, u32[]{:S(2)}, u32[]{:S(2)}) %collective-permute-start.9) | collective-permute-done | bytes 589856 | tf_op jit(solution)/shard_map/ppermute | solution.py:23
  153.3 14.9 %collective-permute-done.11 = bf16[768,384]{0,1:T(8,128)(2,1)S(1)} collective-permute-done((bf16[768,384]{0,1:T(8,128)(2,1)}, bf16[768,384]{0,1:T(8,128)(2,1)S(1)}, u32[]{:S(2)}, u32[]{:S(2)}) %collective-permute-start.11) | collective-permute-done | bytes 589856 | tf_op jit(solution)/shard_map/ppermute | solution.py:23
  168.8 11.2 %collective-permute-done.13 = bf16[768,384]{0,1:T(8,128)(2,1)S(1)} collective-permute-done((bf16[768,384]{0,1:T(8,128)(2,1)}, bf16[768,384]{0,1:T(8,128)(2,1)S(1)}, u32[]{:S(2)}, u32[]{:S(2)}) %collective-permute-start.13) | collective-permute-done | bytes 589856 | tf_op jit(solution)/shard_map/ppermute | solution.py:23
  182.4 2.5 %collective-permute-start.14 = (f32[384,384]{1,0:T(8,128)}, f32[384,384]{1,0:T(8,128)}, u32[]{:S(2)}, u32[]{:S(2)}) collective-permute-start(f32[384,384]{1,0:T(8,128)} %fusion.5), channel_id=1, source_target_pairs={{0,8},{8,0},{16,24},{24,16},{1,9},{9,1},{17,25},{25,17},{2,10},{10... | collective-permute-start | bytes 1769480 | tf_op jit(solution)/shard_map/chol_sum/ppermute | solution.py:23
  185.9 3.1 %fusion.73 = f32[4,384,384]{2,1,0:T(8,128)} fusion(bf16[4,192,384]{2,1,0:T(8,128)(2,1)} %bitcast.283, bf16[1536,384]{1,0:T(8,128)(2,1)} %bitcast.289, s32[]{:T(128)S(6)} %select_n.144), kind=kOutput, calls=%fused_computation.111 | convolution fusion | flops 226492416 | bytes 3096580 | tf_op jit(solution)/shard_map/rotated/ra,grb->gab/dot_general | solution.py:101
  189.4 2.9 %fusion.75 = f32[4,384,384]{2,1,0:T(8,128)} fusion(bf16[4,192,384]{2,1,0:T(8,128)(2,1)S(1)} %bitcast.284, bf16[1536,384]{1,0:T(8,128)(2,1)} %bitcast.290, s32[]{:T(128)S(6)} %select_n.142), kind=kOutput, calls=%fused_computation.113 | convolution fusion | flops 226492416 | bytes 3096580 | tf_op jit(solution)/shard_map/rotated/ra,grb->gab/dot_general | solution.py:101
  192.6 3.2 %fusion.77 = f32[4,384,384]{2,1,0:T(8,128)} fusion(bf16[4,192,384]{2,1,0:T(8,128)(2,1)S(1)} %bitcast.285, bf16[1536,384]{1,0:T(8,128)(2,1)} %bitcast.291, s32[]{:T(128)S(6)} %select_n.140), kind=kOutput, calls=%fused_computation.115 | convolution fusion | flops 226492416 | bytes 3096580 | tf_op jit(solution)/shard_map/rotated/ra,grb->gab/dot_general | solution.py:101
  196.1 3.1 %fusion.79 = f32[4,384,384]{2,1,0:T(8,128)} fusion(bf16[4,192,384]{2,1,0:T(8,128)(2,1)S(1)} %bitcast.286, bf16[1536,384]{1,0:T(8,128)(2,1)} %bitcast.292, s32[]{:T(128)S(6)} %select_n.138), kind=kOutput, calls=%fused_computation.117 | convolution fusion | flops 226492416 | bytes 3096580 | tf_op jit(solution)/shard_map/rotated/ra,grb->gab/dot_general | solution.py:101
  204.3 2.1 add.339
  206.4 2.6 %collective-permute-start.15 = (f32[384,384]{1,0:T(8,128)}, f32[384,384]{1,0:T(8,128)}, u32[]{:S(2)}, u32[]{:S(2)}) collective-permute-start(f32[384,384]{1,0:T(8,128)} %add.339), channel_id=1, source_target_pairs={{0,16},{8,24},{16,0},{24,8},{1,17},{9,25},{17,1},{25,9},{2,18},{10... | collective-permute-start | bytes 1769480 | tf_op jit(solution)/shard_map/chol_sum/ppermute | solution.py:23
  209.0 3.9 %fusion.13 = bf16[4,1,384,384]{2,3,0,1:T(8,128)(2,1)S(1)} fusion(f32[4,384,384]{2,1,0:T(8,128)S(1)} %copy-done.3, f32[4,384,384]{2,1,0:T(8,128)S(1)} %copy-done.4, f32[4,384,384]{2,1,0:T(8,128)} %fusion.77, f32[4,384,384]{2,1,0:T(8,128)} %fusion.79, f32[4,384,384]{2,1,0:T(8,128)S(1)} %fusion.81, f32[4,384,384]{2,1,0:T(8,128)S(1)} %copy-done.2, ...), kind=kOutput, calls=%fused_computation.43 | convolution fusion | flops 231211008 | bytes 18432004 | tf_op jit(solution)/shard_map/rotated/ra,grb->gab/dot_general | solution.py:101
  214.3 20.8 %collective-permute-done.15 = f32[384,384]{1,0:T(8,128)} collective-permute-done((f32[384,384]{1,0:T(8,128)}, f32[384,384]{1,0:T(8,128)}, u32[]{:S(2)}, u32[]{:S(2)}) %collective-permute-start.15) | collective-permute-done | bytes 589856 | tf_op jit(solution)/shard_map/chol_sum/ppermute | solution.py:23
  235.2 2.0 fusion.68
  (210 shorter events, 67.4 us)
Async XLA Ops:
  0.6 20.0 %copy-start = (bf16[4,192,1536]{2,1,0:T(8,128)(2,1)S(1)}, bf16[4,192,1536]{2,1,0:T(8,128)(2,1)}, u32[]{:S(2)}) copy-start(bf16[4,192,1536]{2,1,0:T(8,128)(2,1)} %param.8) | copy-start | bytes 7077892
  0.6 12.3 %copy-start.17 = (f32[192]{0:T(256)S(1)}, f32[192]{0:T(256)}, u32[]{:S(2)}) copy-start(f32[192]{0:T(256)} %param.9) | copy-start | bytes 2308
  0.7 16.2 %copy-start.7 = (bf16[1,1024,384]{2,1,0:T(8,128)(2,1)S(1)}, bf16[1,1024,384]{2,1,0:T(8,128)(2,1)}, u32[]{:S(2)}) copy-start(bf16[1,1024,384]{2,1,0:T(8,128)(2,1)} %param.10) | copy-start | bytes 2359300
  0.7 10.2 %copy-start.14 = (s32[8,1024]{1,0:T(8,128)S(1)}, s32[8,1024]{1,0:T(8,128)}, u32[]{:S(2)}) copy-start(s32[8,1024]{1,0:T(8,128)} %param.11) | copy-start | bytes 98308
  0.7 12.3 %copy-start.26 = (s32[8]{0:T(128)S(1)}, s32[8]{0:T(128)}, u32[]{:S(2)}) copy-start(s32[8]{0:T(128)} %param.13) | copy-start | bytes 100
  0.7 13.9 %copy-start.18 = (s32[8,8]{1,0:T(8,128)S(1)}, s32[8,8]{1,0:T(8,128)}, u32[]{:S(2)}) copy-start(s32[8,8]{1,0:T(8,128)} %param.12) | copy-start | bytes 772
  3.8 23.2 %collective-permute-start.12 = (bf16[1032,384]{1,0:T(8,128)(2,1)}, bf16[1032,384]{1,0:T(8,128)(2,1)}, u32[]{:S(2)}, u32[]{:S(2)}) collective-permute-start(bf16[1032,384]{1,0:T(8,128)(2,1)} %pad_maximum_fusion), channel_id=1, source_target_pairs={{0,7},{1,6},{2,5},{3,4},{4,3},{5,2},{6,1},{7,0},{8,15},{9,14},{10,... | collective-permute-start | bytes 2377736 | tf_op jit(solution)/shard_map/ppermute | solution.py:23
  7.2 36.4 %collective-permute-start.10 = (bf16[1032,384]{1,0:T(8,128)(2,1)}, bf16[1032,384]{1,0:T(8,128)(2,1)}, u32[]{:S(2)}, u32[]{:S(2)}) collective-permute-start(bf16[1032,384]{1,0:T(8,128)(2,1)} %pad_maximum_fusion), channel_id=1, source_target_pairs={{0,6},{1,7},{2,4},{3,5},{4,2},{5,3},{6,0},{7,1},{8,14},{9,15},{10,... | collective-permute-start | bytes 2377736 | tf_op jit(solution)/shard_map/ppermute | solution.py:23
  7.8 51.9 %collective-permute-start.8 = (bf16[1032,384]{1,0:T(8,128)(2,1)}, bf16[1032,384]{1,0:T(8,128)(2,1)}, u32[]{:S(2)}, u32[]{:S(2)}) collective-permute-start(bf16[1032,384]{1,0:T(8,128)(2,1)} %pad_maximum_fusion), channel_id=1, source_target_pairs={{0,5},{1,4},{2,7},{3,6},{4,1},{5,0},{6,3},{7,2},{8,13},{9,12},{10,... | collective-permute-start | bytes 2377736 | tf_op jit(solution)/shard_map/ppermute | solution.py:23
  9.2 51.3 %collective-permute-start.6 = (bf16[1032,384]{1,0:T(8,128)(2,1)}, bf16[1032,384]{1,0:T(8,128)(2,1)}, u32[]{:S(2)}, u32[]{:S(2)}) collective-permute-start(bf16[1032,384]{1,0:T(8,128)(2,1)} %pad_maximum_fusion), channel_id=1, source_target_pairs={{0,3},{1,2},{2,1},{3,0},{4,7},{5,6},{6,5},{7,4},{8,11},{9,10},{10,... | collective-permute-start | bytes 2377736 | tf_op jit(solution)/shard_map/ppermute | solution.py:23
  10.4 66.3 %collective-permute-start.4 = (bf16[1032,384]{1,0:T(8,128)(2,1)}, bf16[1032,384]{1,0:T(8,128)(2,1)}, u32[]{:S(2)}, u32[]{:S(2)}) collective-permute-start(bf16[1032,384]{1,0:T(8,128)(2,1)} %pad_maximum_fusion), channel_id=1, source_target_pairs={{0,4},{1,5},{2,6},{3,7},{4,0},{5,1},{6,2},{7,3},{8,12},{9,13},{10,... | collective-permute-start | bytes 2377736 | tf_op jit(solution)/shard_map/ppermute | solution.py:23
  27.1 50.5 %collective-permute-start.2 = (bf16[1032,384]{1,0:T(8,128)(2,1)}, bf16[1032,384]{1,0:T(8,128)(2,1)S(1)}, u32[]{:S(2)}, u32[]{:S(2)}) collective-permute-start(bf16[1032,384]{1,0:T(8,128)(2,1)} %pad_maximum_fusion), channel_id=1, source_target_pairs={{0,2},{1,3},{2,0},{3,1},{4,6},{5,7},{6,4},{7,5},{8,10},{9,11},{10,... | collective-permute-start | bytes 2377736 | tf_op jit(solution)/shard_map/ppermute | solution.py:23
  43.6 34.1 %collective-permute-start = (bf16[1032,384]{1,0:T(8,128)(2,1)}, bf16[1032,384]{1,0:T(8,128)(2,1)}, u32[]{:S(2)}, u32[]{:S(2)}) collective-permute-start(bf16[1032,384]{1,0:T(8,128)(2,1)} %pad_maximum_fusion), channel_id=1, source_target_pairs={{0,1},{1,0},{2,3},{3,2},{4,5},{5,4},{6,7},{7,6},{8,9},{9,8},{10,11... | collective-permute-start | bytes 2377736 | tf_op jit(solution)/shard_map/ppermute | solution.py:23
  78.5 3.0 %copy-start.25 = (f32[384]{0:T(512)S(1)}, f32[384]{0:T(512)}, u32[]{:S(2)}) copy-start(f32[384]{0:T(512)} %get-tuple-element.15) | copy-start | bytes 4612
  124.9 16.4 %collective-permute-start.5 = (bf16[768,384]{0,1:T(8,128)(2,1)S(1)}, bf16[768,384]{0,1:T(8,128)(2,1)S(1)}, u32[]{:S(2)}, u32[]{:S(2)}) collective-permute-start(bf16[768,384]{0,1:T(8,128)(2,1)S(1)} %copy-done.34), channel_id=1, source_target_pairs={{0,4},{1,5},{2,6},{3,7},{4,0},{5,1},{6,2},{7,3},{8,12},{9,13},{10,... | collective-permute-start | bytes 1769480 | tf_op jit(solution)/shard_map/ppermute | solution.py:23
  127.2 17.6 %collective-permute-start.7 = (bf16[768,384]{0,1:T(8,128)(2,1)}, bf16[768,384]{0,1:T(8,128)(2,1)S(1)}, u32[]{:S(2)}, u32[]{:S(2)}) collective-permute-start(bf16[768,384]{0,1:T(8,128)(2,1)} %fusion.9), channel_id=1, source_target_pairs={{0,3},{1,2},{2,1},{3,0},{4,7},{5,6},{6,5},{7,4},{8,11},{9,10},{10,... | collective-permute-start | bytes 1769480 | tf_op jit(solution)/shard_map/ppermute | solution.py:23
  128.1 24.7 %collective-permute-start.9 = (bf16[768,384]{0,1:T(8,128)(2,1)}, bf16[768,384]{0,1:T(8,128)(2,1)S(1)}, u32[]{:S(2)}, u32[]{:S(2)}) collective-permute-start(bf16[768,384]{0,1:T(8,128)(2,1)} %fusion.10), channel_id=1, source_target_pairs={{0,5},{1,4},{2,7},{3,6},{4,1},{5,0},{6,3},{7,2},{8,13},{9,12},{10,... | collective-permute-start | bytes 1769480 | tf_op jit(solution)/shard_map/ppermute | solution.py:23
  130.8 14.1 %copy-start.16 = (f32[768]{0:T(1024)S(1)}, f32[768]{0:T(1024)}, u32[]{:S(2)}) copy-start(f32[768]{0:T(1024)} %mul.276) | copy-start | bytes 9220
  130.8 22.0 %copy-start.15 = (f32[768]{0:T(1024)S(1)}, f32[768]{0:T(1024)}, u32[]{:S(2)}) copy-start(f32[768]{0:T(1024)} %mul.280) | copy-start | bytes 9220
  130.8 49.7 %collective-permute-start.1 = (bf16[768,384]{0,1:T(8,128)(2,1)}, bf16[768,384]{0,1:T(8,128)(2,1)S(1)}, u32[]{:S(2)}, u32[]{:S(2)}) collective-permute-start(bf16[768,384]{0,1:T(8,128)(2,1)} %fusion.6), channel_id=1, source_target_pairs={{0,1},{1,0},{2,3},{3,2},{4,5},{5,4},{6,7},{7,6},{8,9},{9,8},{10,11... | collective-permute-start | bytes 1769480 | tf_op jit(solution)/shard_map/ppermute | solution.py:23
  130.8 50.2 %collective-permute-start.3 = (bf16[768,384]{0,1:T(8,128)(2,1)}, bf16[768,384]{0,1:T(8,128)(2,1)S(1)}, u32[]{:S(2)}, u32[]{:S(2)}) collective-permute-start(bf16[768,384]{0,1:T(8,128)(2,1)} %fusion.7), channel_id=1, source_target_pairs={{0,2},{1,3},{2,0},{3,1},{4,6},{5,7},{6,4},{7,5},{8,10},{9,11},{10,... | collective-permute-start | bytes 1769480 | tf_op jit(solution)/shard_map/ppermute | solution.py:23
  141.3 26.9 %collective-permute-start.11 = (bf16[768,384]{0,1:T(8,128)(2,1)}, bf16[768,384]{0,1:T(8,128)(2,1)S(1)}, u32[]{:S(2)}, u32[]{:S(2)}) collective-permute-start(bf16[768,384]{0,1:T(8,128)(2,1)} %fusion.11), channel_id=1, source_target_pairs={{0,6},{1,7},{2,4},{3,5},{4,2},{5,3},{6,0},{7,1},{8,14},{9,15},{10,... | collective-permute-start | bytes 1769480 | tf_op jit(solution)/shard_map/ppermute | solution.py:23
  144.8 35.1 %collective-permute-start.13 = (bf16[768,384]{0,1:T(8,128)(2,1)}, bf16[768,384]{0,1:T(8,128)(2,1)S(1)}, u32[]{:S(2)}, u32[]{:S(2)}) collective-permute-start(bf16[768,384]{0,1:T(8,128)(2,1)} %fusion.12), channel_id=1, source_target_pairs={{0,7},{1,6},{2,5},{3,4},{4,3},{5,2},{6,1},{7,0},{8,15},{9,14},{10,... | collective-permute-start | bytes 1769480 | tf_op jit(solution)/shard_map/ppermute | solution.py:23
  153.3 27.2 %copy-start.10 = (f32[384,384]{1,0:T(8,128)S(1)}, f32[384,384]{1,0:T(8,128)}, u32[]{:S(2)}) copy-start(f32[384,384]{1,0:T(8,128)} %fusion.51) | copy-start | bytes 1769476
  182.4 21.8 %collective-permute-start.14 = (f32[384,384]{1,0:T(8,128)}, f32[384,384]{1,0:T(8,128)}, u32[]{:S(2)}, u32[]{:S(2)}) collective-permute-start(f32[384,384]{1,0:T(8,128)} %fusion.5), channel_id=1, source_target_pairs={{0,8},{8,0},{16,24},{24,16},{1,9},{9,1},{17,25},{25,17},{2,10},{10... | collective-permute-start | bytes 1769480 | tf_op jit(solution)/shard_map/chol_sum/ppermute | solution.py:23
  196.1 3.4 %copy-start.6 = (bf16[768,384]{0,1:T(8,128)(2,1)S(1)}, bf16[768,384]{0,1:T(8,128)(2,1)}, u32[]{:S(2)}) copy-start(bf16[768,384]{0,1:T(8,128)(2,1)} %copy-done.5) | copy-start | bytes 1769476
  200.9 8.1 %copy-start.4 = (f32[4,384,384]{2,1,0:T(8,128)S(1)}, f32[4,384,384]{2,1,0:T(8,128)}, u32[]{:S(2)}) copy-start(f32[4,384,384]{2,1,0:T(8,128)} %fusion.75) | copy-start | bytes 7077892
  200.9 8.1 %copy-start.9 = (bf16[768,384]{1,0:T(8,128)(2,1)S(1)}, bf16[768,384]{1,0:T(8,128)(2,1)}, u32[]{:S(2)}) copy-start(bf16[768,384]{1,0:T(8,128)(2,1)} %copy.56) | copy-start | bytes 1769476
  202.5 6.5 %copy-start.2 = (f32[4,384,384]{2,1,0:T(8,128)S(1)}, f32[4,384,384]{2,1,0:T(8,128)}, u32[]{:S(2)}) copy-start(f32[4,384,384]{2,1,0:T(8,128)} %fusion.85) | copy-start | bytes 7077892
  202.6 6.4 %copy-start.3 = (f32[4,384,384]{2,1,0:T(8,128)S(1)}, f32[4,384,384]{2,1,0:T(8,128)}, u32[]{:S(2)}) copy-start(f32[4,384,384]{2,1,0:T(8,128)} %fusion.73) | copy-start | bytes 7077892
  206.4 28.8 %collective-permute-start.15 = (f32[384,384]{1,0:T(8,128)}, f32[384,384]{1,0:T(8,128)}, u32[]{:S(2)}, u32[]{:S(2)}) collective-permute-start(f32[384,384]{1,0:T(8,128)} %add.339), channel_id=1, source_target_pairs={{0,16},{8,24},{16,0},{24,8},{1,17},{9,25},{17,1},{25,9},{2,18},{10... | collective-permute-start | bytes 1769480 | tf_op jit(solution)/shard_map/chol_sum/ppermute | solution.py:23
  209.0 28.2 %copy-start.1 = (bf16[4,192,1536]{2,1,0:T(8,128)(2,1)S(1)}, bf16[4,192,1536]{2,1,0:T(8,128)(2,1)}, u32[]{:S(2)}) copy-start(bf16[4,192,1536]{2,1,0:T(8,128)(2,1)} %param.8) | copy-start | bytes 7077892
  (20 other events, 46.7 us)

commit v5 on v3

v5 whole, which is shorter than its diff:
```python
import math

import jax
import jax.numpy as jnp
from jax import lax
from jax.sharding import PartitionSpec as P


def split_bf16(x):
    hi = lax.reduce_precision(x, exponent_bits=8, mantissa_bits=7)
    rest = x - hi
    mid = lax.reduce_precision(rest, exponent_bits=8, mantissa_bits=7)
    lo = rest - mid
    return jnp.stack([hi, mid, lo]).astype(jnp.bfloat16)


def join_bf16(parts):
    parts = parts.astype(jnp.float32)
    return (parts[0] + parts[1]) + parts[2]


def per_device(chol_vec, env_weight, lno_coef, domain, block_fill, lno_count):
    chol_local, orb_rows, orb_total = chol_vec.shape
    frag_total, slot_total = domain.shape
    group_count = block_fill.shape[1]
    group_width = slot_total // group_count
    lno_width = lno_coef.shape[2]
    chol_size = lax.axis_size("chol")
    orb_size = lax.axis_size("orb")
    my_index = lax.axis_index("orb")
    norm_factor = 1.0 / math.sqrt(chol_local * chol_size * orb_total)
    chunks = lno_width // 128 if lno_width % 128 == 0 else 1
    width = lno_width // chunks

    slot_index = jnp.arange(slot_total, dtype=jnp.int32)
    slot_ok = (slot_index % group_width)[None, :] < jnp.repeat(block_fill, group_width, axis=1)
    column_ok = jnp.arange(lno_width, dtype=jnp.int32)[None, :] < lno_count[:, None]

    weight_rows = -(-3 * orb_rows // lno_width)
    pad_rows = -(-weight_rows // 8) * 8
    weight_parts = split_bf16(env_weight).reshape(-1)
    weight_parts = jnp.pad(weight_parts, (0, pad_rows * lno_width - weight_parts.shape[0]))
    payload = jnp.concatenate([lno_coef, weight_parts.reshape(1, pad_rows, lno_width)], axis=1)
    gathered = lax.all_gather(payload, "orb", axis=0, tiled=True)

    with jax.named_scope("pick_columns"):
        chol_t = chol_vec.reshape(chol_local * orb_rows, orb_total).T
        picked = jnp.take(chol_t, domain, axis=0)
        picked = jnp.where(slot_ok[:, :, None], picked, jnp.zeros_like(picked))

    with jax.named_scope("own_placement"):
        own_groups = lax.dynamic_index_in_dim(domain, my_index, 0, keepdims=False)
        own_groups = own_groups.reshape(group_count, group_width)
        own_fill = lax.dynamic_index_in_dim(slot_ok, my_index, 0, keepdims=False)
        own_fill = own_fill.reshape(group_count, group_width)
        own_cols = lax.dynamic_index_in_dim(column_ok, my_index, 0, keepdims=False)
        block_ids = jnp.arange(orb_size, dtype=jnp.int32)
        sel = (own_groups[:, 0] // orb_rows)[None, :] == block_ids[:, None]
        present = jnp.any(sel, axis=1)
        group_of_block = jnp.argmax(sel, axis=1).astype(jnp.int32)
        local = jnp.take(own_groups, group_of_block, axis=0) - block_ids[:, None] * orb_rows
        fill = jnp.take(own_fill, group_of_block, axis=0) & present[:, None]
        row_ids = jnp.arange(orb_rows, dtype=jnp.int32)
        onehot = ((local[:, None, :] == row_ids[None, :, None]) & fill[:, None, :]).astype(jnp.bfloat16)
        own_coef = jnp.take(lno_coef[0].reshape(group_count, group_width, lno_width), group_of_block, axis=0)
        own_w = jnp.einsum("brs,bsa->bra", onehot, own_coef, preferred_element_type=jnp.float32)
        own_w = jnp.where(own_cols[None, None, :], own_w, 0.0).astype(jnp.bfloat16)

    all_coef = gathered[:, :slot_total]
    weight_all = join_bf16(
        gathered[:, slot_total:]
        .reshape(orb_size, -1)[:, : 3 * orb_rows]
        .reshape(orb_size, 3, orb_rows)
        .transpose(1, 0, 2)
    )

    received = []
    weighted = []
    rot_parts = []
    blocks = {}
    for k in range(chunks):
        cols = slice(k * width, (k + 1) * width)
        with jax.named_scope("half"):
            half = jnp.einsum(
                "fsk,fsa->fka", picked, all_coef[:, :, cols], preferred_element_type=jnp.float32
            )
            half = jnp.where(column_ok[:, None, cols], half, 0.0).astype(jnp.bfloat16)
            half = half.reshape(frag_total, chol_local, orb_rows, width)
        recv = lax.all_to_all(half, "orb", split_axis=0, concat_axis=0, tiled=True)
        with jax.named_scope("dressing"):
            wtd = (recv.astype(jnp.float32) * weight_all.reshape(orb_size, 1, orb_rows, 1)).astype(jnp.bfloat16)
            received.append(recv.reshape(-1, width))
            weighted.append(wtd.reshape(-1, width))
            pairs = [(k, k)] + [p for j in range(k) for p in ((k, j), (j, k))]
            for a_i, b_i in pairs:
                blocks[(a_i, b_i)] = lax.dot_general(
                    weighted[a_i], received[b_i], (((0,), (0,)), ((), ())),
                    preferred_element_type=jnp.float32,
                )
        with jax.named_scope("rotated"):
            rot_parts.append(
                jnp.einsum(
                    "ora,ogrb->gab", own_w, recv, preferred_element_type=jnp.float32
                ).astype(jnp.bfloat16)
            )

    with jax.named_scope("dressing"):
        dressing_part = jnp.concatenate(
            [jnp.concatenate([blocks[(i, j)] for j in range(chunks)], axis=1) for i in range(chunks)], axis=0
        )
        dressing = (lax.psum(dressing_part, "chol") * norm_factor).astype(jnp.bfloat16)
    rotated = jnp.concatenate(rot_parts, axis=2)[:, None]
    return (rotated, dressing[None])


def solution(mesh):
    return jax.shard_map(
        per_device,
        mesh=mesh,
        in_specs=(P("chol", "orb", None), P("orb"), P("orb", None, None), P(), P(), P()),
        out_specs=(P("chol", "orb", None, None), P("orb", None, None)),
        check_vma=False,
    )
```

time: 235 us -> 218 us (0.928)
  waiting for transfers between devices: 104 us -> 65.1 us
  local copies, waits for them, and re-layouts: 33 us -> 59.4 us
  matrix products: 60.5 us -> 57.9 us
  other arithmetic: 8.66 us -> 6.29 us
    all_gather x3 -> x1, waiting for transfers between devices: 60.8 us -> 0.02 us  [per_device(): gathered = lax.all_gather(payload, 'orb', axis=0, tiled=True)]
    gather x8 -> x5, local copies, waits for them, and re-layouts: 14.5 us -> 53.1 us  [the longest x2 51.2 us: per_device(): picked = jnp.take(chol_t, domain, axis=0)]
    all_to_all x3, waiting for transfers between devices: 10.9 us -> 33.7 us  [per_device(): recv = lax.all_to_all(half, 'orb', split_axis=0, concat_axis=0, tiled=True)]
    convert_element_type x3 -> x0, local copies, waits for them, and re-layouts: 7.88 us -> none  [per_device(): half.astype(jnp.bfloat16).reshape(frag_total, chol_local, orb_rows, width)]
    dot_general x9, matrix products: 28.6 us -> 22.2 us  [per_device(): lax.dot_general(weighted[a_i], received[b_i], (((0,), (0,)), ((), ())), p...]
    slice x3 -> x1, local copies, waits for them, and re-layouts: 5.78 us -> 0.01 us  [per_device(): half = jnp.where(column_ok[:, None, cols], half, 0.0).astype(jnp.bfloat16)]
    dot_general x10 -> x7, matrix products: 31.9 us -> 35.7 us  [the longest x3 29.3 us: per_device(): jnp.einsum('fsk,fsa->fka', picked, all_coef[:, :, cols], preferred_elemen...]
    reshape x1 -> x2, local copies, waits for them, and re-layouts: 0.01 us -> 2.86 us  [the longest x1 2.84 us: per_device(): chol_t = chol_vec.reshape(chol_local * orb_rows, orb_total).T]
  transfers between devices with their start and end apart: 7 -> 5, of which waited for: 6 -> 4; matrix products, arithmetic and copies ran while one was open for 35% -> 44% of each run, Pallas kernels for 0% -> 0%
where the time goes in v5:
time: 218 us; the launch traced here: 217 us
  waiting for transfers between devices  65.1 us (30%)
  local copies, waits for them, and re-layouts  59.4 us (27%)
  matrix products  57.9 us (27%)
  between operations  14.3 us (7%)
  starting transfers between devices  14 us (6%)
  other arithmetic  6.29 us (3%)
    gather x2, local copies, waits for them, and re-layouts, per_device(): picked = jnp.take(chol_t, domain, axis=0)  51.2 us
    all_to_all x3, waiting for transfers between devices, per_device(): recv = lax.all_to_all(half, 'orb', split_axis=0, concat_axis=0, tiled=True)  33.7 us
    psum x1, waiting for transfers between devices, per_device(): lax.psum(dressing_part, 'chol') * norm_factor  31.3 us
    dot_general x3, matrix products, per_device(): jnp.einsum('fsk,fsa->fka', picked, all_coef[:, :, cols], preferred_elemen...  29.3 us
    dot_general x9, matrix products, per_device(): lax.dot_general(weighted[a_i], received[b_i], (((0,), (0,)), ((), ())), p...  22.2 us
    all_to_all x3, starting transfers between devices, per_device(): recv = lax.all_to_all(half, 'orb', split_axis=0, concat_axis=0, tiled=True)  13.8 us
    dot_general x3, matrix products, per_device(): jnp.einsum('ora,ogrb->gab', own_w, recv, preferred_element_type=jnp.float32)  5.85 us
  transfers between devices with their start and end apart: 5, of which 4 were waited for; matrix products, arithmetic and copies ran while one was open for 44% of the time, Pallas kernels for 0%

profile of v5, /device:TPU:0, one launch (start us, length us, event | category | flops | bytes accessed | tf_op | source)
XLA Modules:
  0.0 217.0 jit_solution(16732784904637263219)
XLA Ops:
  8.0 2.1 pad_maximum_fusion
  10.2 2.8 %copy.70 = bf16[768,1536]{0,1:T(8,128)(2,1)S(1)} copy(bf16[768,1536]{1,0:T(8,128)(2,1)} %bitcast.108) | data formatting | bytes 4718592 | tf_op jit(solution)/shard_map/pick_columns/reshape | solution.py:47
  13.1 34.5 %gather_fusion = bf16[8192,768]{1,0:T(8,128)(2,1)} fusion(bf16[1536,768]{1,0:T(8,128)(2,1)S(1)} %bitcast.105, s32[8192]{0:T(1024)S(1)} %bitcast_clamp_fusion), kind=kCustom, calls=%fused_computation | custom fusion | bytes 25198592 | tf_op jit(solution)/shard_map/pick_columns/jit(_take)/gather | solution.py:48
  47.6 16.7 %copy.71 = bf16[8,1024,768]{1,2,0:T(8,128)(2,1)} copy(bf16[8,1024,768]{2,1,0:T(8,128)(2,1)} %bitcast.106) | data formatting | bytes 25165824 | tf_op jit(solution)/shard_map/pick_columns/jit(_take)/gather | solution.py:48
  65.9 0.7 gather_fusion.3
  68.3 9.8 %select_convert_fusion = bf16[8,768,128]{2,1,0:T(8,128)(2,1)} fusion(pred[8,128]{1,0:T(8,128)(4,1)S(1)} %get-tuple-element.13, bf16[8,1032,384]{2,1,0:T(8,128)(2,1)} %all-gather.2.cloned.1.call-done, bf16[8,1024,768]{1,2,0:T(8,128)(2,1)} %copy.71, pred[8,1024]{1,0:T(8,128)(4,1)S(1)} %get-tuple-element.19, pred[8,1024]{1,0:T(8,128)(4,1)S(1)} %get-tuple-element.18), kind=kOutput, calls=%fused_computation.17 | convolution fusion | flops 1624768512 | bytes 16270336 | tf_op jit(solution)/shard_map/half/fsk,fsa->fka/dot_general | solution.py:84
  78.1 5.2 %all-to-all-start.2 = ((bf16[8,4,192,128]{3,2,1,0:T(8,128)(2,1)}), bf16[8,4,192,128]{3,2,1,0:T(8,128)(2,1)S(1)}, u32[]{:S(2)}, u32[]{:S(2)}) async-start(bf16[8,4,192,128]{3,2,1,0:T(8,128)(2,1)} %bitcast.111), calls=%async_computation.2 | async-start | bytes 3145728 | tf_op jit(solution)/shard_map/all_to_all | solution.py:89
  83.2 0.8 slice_bitcast_fusion
  84.1 9.7 %select_convert_fusion.1 = bf16[8,768,128]{2,1,0:T(8,128)(2,1)} fusion(pred[8,128]{1,0:T(8,128)(4,1)S(1)} %get-tuple-element.14, bf16[8,1032,384]{2,1,0:T(8,128)(2,1)} %all-gather.2.cloned.1.call-done, bf16[8,1024,768]{1,2,0:T(8,128)(2,1)} %copy.71, pred[8,1024]{1,0:T(8,128)(4,1)S(1)} %get-tuple-element.19, pred[8,1024]{1,0:T(8,128)(4,1)S(1)} %get-tuple-element.18), kind=kOutput, calls=%fused_computation.18 | convolution fusion | flops 1624768512 | bytes 16270336 | tf_op jit(solution)/shard_map/half/fsk,fsa->fka/dot_general | solution.py:84
  93.8 10.5 %all-to-all-done.2 = bf16[8,4,192,128]{3,2,1,0:T(8,128)(2,1)S(1)} async-done(((bf16[8,4,192,128]{3,2,1,0:T(8,128)(2,1)}), bf16[8,4,192,128]{3,2,1,0:T(8,128)(2,1)S(1)}, u32[]{:S(2)}, u32[]{:S(2)}) %all-to-all-start.2) | async-done | bytes 1572896 | tf_op jit(solution)/shard_map/all_to_all | solution.py:89
  104.3 4.3 %all-to-all-start.1 = ((bf16[8,4,192,128]{3,2,1,0:T(8,128)(2,1)}), bf16[8,4,192,128]{3,2,1,0:T(8,128)(2,1)}, u32[]{:S(2)}, u32[]{:S(2)}) async-start(bf16[8,4,192,128]{3,2,1,0:T(8,128)(2,1)} %bitcast.110), calls=%async_computation.1 | async-start | bytes 3145728 | tf_op jit(solution)/shard_map/all_to_all | solution.py:89
  108.6 9.7 %select_convert_fusion.2 = bf16[8,768,128]{2,1,0:T(8,128)(2,1)} fusion(pred[8,128]{1,0:T(8,128)(4,1)S(1)} %get-tuple-element.12, bf16[8,1032,384]{2,1,0:T(8,128)(2,1)} %all-gather.2.cloned.1.call-done, bf16[8,1024,768]{1,2,0:T(8,128)(2,1)} %copy.71, pred[8,1024]{1,0:T(8,128)(4,1)S(1)} %get-tuple-element.19, pred[8,1024]{1,0:T(8,128)(4,1)S(1)} %get-tuple-element.18), kind=kOutput, calls=%fused_computation.19 | convolution fusion | flops 1624768512 | bytes 16270336 | tf_op jit(solution)/shard_map/half/fsk,fsa->fka/dot_general | solution.py:84
  118.3 11.3 %all-to-all-done.1 = bf16[8,4,192,128]{3,2,1,0:T(8,128)(2,1)} async-done(((bf16[8,4,192,128]{3,2,1,0:T(8,128)(2,1)}), bf16[8,4,192,128]{3,2,1,0:T(8,128)(2,1)}, u32[]{:S(2)}, u32[]{:S(2)}) %all-to-all-start.1) | async-done | bytes 1572896 | tf_op jit(solution)/shard_map/all_to_all | solution.py:89
  129.6 4.3 %all-to-all-start = ((bf16[8,4,192,128]{3,2,1,0:T(8,128)(2,1)}), bf16[8,4,192,128]{3,2,1,0:T(8,128)(2,1)}, u32[]{:S(2)}, u32[]{:S(2)}) async-start(bf16[8,4,192,128]{3,2,1,0:T(8,128)(2,1)} %bitcast.109), calls=%async_computation | async-start | bytes 3145728 | tf_op jit(solution)/shard_map/all_to_all | solution.py:89
  134.3 1.0 fusion.45
  135.3 2.4 %fusion.44 = f32[128,128]{0,1:T(8,128)S(1)} fusion(bf16[8,4,192,128]{3,2,1,0:T(8,128)(2,1)} %all-to-all-done.1, bf16[8,4,192,128]{3,2,1,0:T(8,128)(2,1)S(1)} %all-to-all-done.2, f32[8,192]{1,0:T(8,128)S(1)} %bitcast.119), kind=kOutput, calls=%fused_computation.54 | convolution fusion | flops 203685888 | bytes 3217408 | tf_op jit(solution)/shard_map/dressing/dot_general | solution.py:96
  137.7 2.4 %fusion.48 = f32[128,128]{0,1:T(8,128)S(1)} fusion(bf16[8,4,192,128]{3,2,1,0:T(8,128)(2,1)S(1)} %all-to-all-done.2, bf16[8,4,192,128]{3,2,1,0:T(8,128)(2,1)} %all-to-all-done.1, f32[8,192]{1,0:T(8,128)S(1)} %bitcast.120), kind=kOutput, calls=%fused_computation.58 | convolution fusion | flops 203685888 | bytes 3217408 | tf_op jit(solution)/shard_map/dressing/dot_general | solution.py:96
  140.1 2.9 %fusion.47 = f32[128,128]{0,1:T(8,128)S(1)} fusion(bf16[8,4,192,128]{3,2,1,0:T(8,128)(2,1)} %all-to-all-done.1, f32[8,192]{1,0:T(8,128)S(1)} %bitcast.121), kind=kOutput, calls=%fused_computation.57 | convolution fusion | flops 203685888 | bytes 1644544 | tf_op jit(solution)/shard_map/dressing/dot_general | solution.py:96
  143.0 12.0 %all-to-all-done = bf16[8,4,192,128]{3,2,1,0:T(8,128)(2,1)} async-done(((bf16[8,4,192,128]{3,2,1,0:T(8,128)(2,1)}), bf16[8,4,192,128]{3,2,1,0:T(8,128)(2,1)}, u32[]{:S(2)}, u32[]{:S(2)}) %all-to-all-start) | async-done | bytes 1572896 | tf_op jit(solution)/shard_map/all_to_all | solution.py:89
  155.0 2.4 %fusion.43 = f32[128,128]{0,1:T(8,128)S(1)} fusion(bf16[8,4,192,128]{3,2,1,0:T(8,128)(2,1)} %all-to-all-done, bf16[8,4,192,128]{3,2,1,0:T(8,128)(2,1)S(1)} %all-to-all-done.2, f32[8,192]{1,0:T(8,128)S(1)} %bitcast.122), kind=kOutput, calls=%fused_computation.53 | convolution fusion | flops 203685888 | bytes 3217408 | tf_op jit(solution)/shard_map/dressing/dot_general | solution.py:96
  157.4 2.9 %fusion.46 = f32[128,128]{0,1:T(8,128)S(1)} fusion(bf16[8,4,192,128]{3,2,1,0:T(8,128)(2,1)} %all-to-all-done, bf16[8,4,192,128]{3,2,1,0:T(8,128)(2,1)} %all-to-all-done.1, f32[8,192]{1,0:T(8,128)S(1)} %bitcast.123), kind=kOutput, calls=%fused_computation.56 | convolution fusion | flops 203685888 | bytes 3217408 | tf_op jit(solution)/shard_map/dressing/dot_general | solution.py:96
  160.3 2.4 %fusion.51 = f32[128,128]{0,1:T(8,128)S(1)} fusion(bf16[8,4,192,128]{3,2,1,0:T(8,128)(2,1)S(1)} %all-to-all-done.2, bf16[8,4,192,128]{3,2,1,0:T(8,128)(2,1)} %all-to-all-done, f32[8,192]{1,0:T(8,128)S(1)} %bitcast.124), kind=kOutput, calls=%fused_computation.61 | convolution fusion | flops 203685888 | bytes 3217408 | tf_op jit(solution)/shard_map/dressing/dot_general | solution.py:96
  162.7 2.9 %fusion.50 = f32[128,128]{0,1:T(8,128)S(1)} fusion(bf16[8,4,192,128]{3,2,1,0:T(8,128)(2,1)} %all-to-all-done.1, bf16[8,4,192,128]{3,2,1,0:T(8,128)(2,1)} %all-to-all-done, f32[8,192]{1,0:T(8,128)S(1)} %bitcast.125), kind=kOutput, calls=%fused_computation.60 | convolution fusion | flops 203685888 | bytes 3217408 | tf_op jit(solution)/shard_map/dressing/dot_general | solution.py:96
  165.6 2.9 %fusion.49 = f32[128,128]{0,1:T(8,128)S(1)} fusion(bf16[8,4,192,128]{3,2,1,0:T(8,128)(2,1)} %all-to-all-done, f32[8,192]{1,0:T(8,128)S(1)} %bitcast.126), kind=kOutput, calls=%fused_computation.59 | convolution fusion | flops 203685888 | bytes 1644544 | tf_op jit(solution)/shard_map/dressing/dot_general | solution.py:96
  168.5 0.9 maximum_maximum_fusion
  169.4 1.0 fusion.40
  170.4 2.4 %fusion.41 = bf16[4,384,128]{1,2,0:T(8,128)(2,1)S(1)} fusion(bf16[8,4,192,128]{3,2,1,0:T(8,128)(2,1)} %all-to-all-done.1, bf16[8,192,384,1]{2,1,3,0:T(8,128)(2,1)S(1)} %fusion.30), kind=kOutput, calls=%fused_computation.50 | convolution fusion | flops 604176384 | bytes 3145728 | tf_op jit(solution)/shard_map/rotated/ora,ogrb->gab/dot_general | solution.py:102
  172.8 2.4 %fusion.42 = bf16[4,384,128]{1,2,0:T(8,128)(2,1)S(1)} fusion(bf16[8,4,192,128]{3,2,1,0:T(8,128)(2,1)} %all-to-all-done, bf16[8,192,384,1]{2,1,3,0:T(8,128)(2,1)S(1)} %fusion.30), kind=kOutput, calls=%fused_computation.51 | convolution fusion | flops 604176384 | bytes 3145728 | tf_op jit(solution)/shard_map/rotated/ora,ogrb->gab/dot_general | solution.py:102
  175.4 1.5 copy.72
  176.8 31.3 %all-reduce.3.cloned.1.call-done = f32[384,384]{0,1:T(8,128)} async-done(((f32[384,384]{0,1:T(8,128)}), f32[384,384]{0,1:T(8,128)}) %all-reduce.3.cloned.1.call-update) | async-done | bytes 589840 | tf_op jit(solution)/shard_map/dressing/psum | solution.py:111
  208.2 1.1 fusion.59
  209.3 0.9 copy.73
  (51 shorter events, 4.6 us)
Async XLA Ops:
  7.2 61.1 %all-gather.2.cloned.1.call-start = ((), (), s32[]{:S(2)}) async-start(), calls=%async_computation.3 | async-start | bytes 7133184 | tf_op jit(solution)/shard_map/all_gather | solution.py:44
  10.2 2.9 %copy-start.1 = (s32[8,1024]{1,0:T(8,128)S(1)}, s32[8,1024]{1,0:T(8,128)}, u32[]{:S(2)}) copy-start(s32[8,1024]{1,0:T(8,128)} %param.9) | copy-start | bytes 98308
  47.6 16.7 %copy-start.2 = (s32[8,8]{1,0:T(8,128)S(1)}, s32[8,8]{1,0:T(8,128)}, u32[]{:S(2)}) copy-start(s32[8,8]{1,0:T(8,128)} %param.10) | copy-start | bytes 772
  47.6 18.3 %copy-start = (bf16[1,1024,384]{2,1,0:T(8,128)(2,1)S(1)}, bf16[1,1024,384]{2,1,0:T(8,128)(2,1)}, u32[]{:S(2)}) copy-start(bf16[1,1024,384]{2,1,0:T(8,128)(2,1)} %param.8) | copy-start | bytes 2359300
  64.3 3.0 %copy-start.3 = (s32[8]{0:T(128)S(1)}, s32[8]{0:T(128)}, u32[]{:S(2)}) copy-start(s32[8]{0:T(128)} %param.11) | copy-start | bytes 100
  78.1 26.2 %all-to-all-start.2 = ((bf16[8,4,192,128]{3,2,1,0:T(8,128)(2,1)}), bf16[8,4,192,128]{3,2,1,0:T(8,128)(2,1)S(1)}, u32[]{:S(2)}, u32[]{:S(2)}) async-start(bf16[8,4,192,128]{3,2,1,0:T(8,128)(2,1)} %bitcast.111), calls=%async_computation.2 | async-start | bytes 3145728 | tf_op jit(solution)/shard_map/all_to_all | solution.py:89
  104.3 25.4 %all-to-all-start.1 = ((bf16[8,4,192,128]{3,2,1,0:T(8,128)(2,1)}), bf16[8,4,192,128]{3,2,1,0:T(8,128)(2,1)}, u32[]{:S(2)}, u32[]{:S(2)}) async-start(bf16[8,4,192,128]{3,2,1,0:T(8,128)(2,1)} %bitcast.110), calls=%async_computation.1 | async-start | bytes 3145728 | tf_op jit(solution)/shard_map/all_to_all | solution.py:89
  129.6 25.3 %all-to-all-start = ((bf16[8,4,192,128]{3,2,1,0:T(8,128)(2,1)}), bf16[8,4,192,128]{3,2,1,0:T(8,128)(2,1)}, u32[]{:S(2)}, u32[]{:S(2)}) async-start(bf16[8,4,192,128]{3,2,1,0:T(8,128)(2,1)} %bitcast.109), calls=%async_computation | async-start | bytes 3145728 | tf_op jit(solution)/shard_map/all_to_all | solution.py:89
  133.9 74.2 %all-reduce.3.cloned.1.call-start = ((), (), s32[]{:S(2)}) async-start(), calls=%async_computation.4 | async-start | bytes 1179648 | tf_op jit(solution)/shard_map/dressing/psum | solution.py:111
Sparse Core Ops, SparseCore 0:
  10.5 48.4 all-gather.1
  169.5 38.6 all-reduce.2

commit v6 on v5

--- a/solution.py
+++ b/solution.py
@@ -29,8 +29,6 @@
     orb_size = lax.axis_size("orb")
     my_index = lax.axis_index("orb")
     norm_factor = 1.0 / math.sqrt(chol_local * chol_size * orb_total)
-    chunks = lno_width // 128 if lno_width % 128 == 0 else 1
-    width = lno_width // chunks
 
     slot_index = jnp.arange(slot_total, dtype=jnp.int32)
     slot_ok = (slot_index % group_width)[None, :] < jnp.repeat(block_fill, group_width, axis=1)
@@ -74,42 +72,29 @@
         .transpose(1, 0, 2)
     )
 
-    received = []
-    weighted = []
-    rot_parts = []
-    blocks = {}
-    for k in range(chunks):
-        cols = slice(k * width, (k + 1) * width)
-        with jax.named_scope("half"):
-            half = jnp.einsum(
-                "fsk,fsa->fka", picked, all_coef[:, :, cols], preferred_element_type=jnp.float32
-            )
-            half = jnp.where(column_ok[:, None, cols], half, 0.0).astype(jnp.bfloat16)
-            half = half.reshape(frag_total, chol_local, orb_rows, width)
-        recv = lax.all_to_all(half, "orb", split_axis=0, concat_axis=0, tiled=True)
-        with jax.named_scope("dressing"):
-            wtd = (recv.astype(jnp.float32) * weight_all.reshape(orb_size, 1, orb_rows, 1)).astype(jnp.bfloat16)
-            received.append(recv.reshape(-1, width))
-            weighted.append(wtd.reshape(-1, width))
-            pairs = [(k, k)] + [p for j in range(k) for p in ((k, j), (j, k))]
-            for a_i, b_i in pairs:
-                blocks[(a_i, b_i)] = lax.dot_general(
-                    weighted[a_i], received[b_i], (((0,), (0,)), ((), ())),
-                    preferred_element_type=jnp.float32,
-                )
-        with jax.named_scope("rotated"):
-            rot_parts.append(
-                jnp.einsum(
-                    "ora,ogrb->gab", own_w, recv, preferred_element_type=jnp.float32
-                ).astype(jnp.bfloat16)
-            )
+    with jax.named_scope("half"):
+        half = jnp.einsum("fsk,fsa->fka", picked, all_coef, preferred_element_type=jnp.float32)
+        half = jnp.where(column_ok[:, None, :], half, 0.0).astype(jnp.bfloat16)
+        half = half.reshape(frag_total, chol_local, orb_rows, lno_width)
+
+    received = lax.all_to_all(half, "orb", split_axis=0, concat_axis=0, tiled=True)
 
     with jax.named_scope("dressing"):
-        dressing_part = jnp.concatenate(
-            [jnp.concatenate([blocks[(i, j)] for j in range(chunks)], axis=1) for i in range(chunks)], axis=0
+        weighted = (
+            received.astype(jnp.float32) * weight_all.reshape(orb_size, 1, orb_rows, 1)
+        ).astype(jnp.bfloat16)
+        dressing_part = lax.dot_general(
+            weighted.reshape(-1, lno_width),
+            received.reshape(-1, lno_width),
+            (((0,), (0,)), ((), ())),
+            preferred_element_type=jnp.float32,
         )
         dressing = (lax.psum(dressing_part, "chol") * norm_factor).astype(jnp.bfloat16)
-    rotated = jnp.concatenate(rot_parts, axis=2)[:, None]
+
+    with jax.named_scope("rotated"):
+        rotated = jnp.einsum(
+            "ora,ogrb->gab", own_w, received, preferred_element_type=jnp.float32
+        ).astype(jnp.bfloat16)[:, None]
     return (rotated, dressing[None])
 
 

time: 218 us -> 194 us (0.89)
  matrix products: 57.9 us -> 25.5 us
  waiting for transfers between devices: 65.1 us -> 83.6 us
  starting transfers between devices: 14 us -> 5.37 us
    dot_general x16 -> x3, matrix products: 57.9 us -> 25.5 us  [the longest x1 12.9 us: per_device(): jnp.einsum('fsk,fsa->fka', picked, all_coef, preferred_element_type=jnp.f...]
    all_to_all x3 -> x1, waiting for transfers between devices: 33.7 us -> 50.7 us  [per_device(): lax.all_to_all(half, 'orb', split_axis=0, concat_axis=0, tiled=True)]
    all_to_all x3 -> x1, starting transfers between devices: 13.8 us -> 5.29 us  [per_device(): lax.all_to_all(half, 'orb', split_axis=0, concat_axis=0, tiled=True)]
  transfers between devices with their start and end apart: 5 -> 3, of which waited for: 4 -> 2; matrix products, arithmetic and copies ran while one was open for 44% -> 34% of each run, Pallas kernels for 0% -> 0%
where the time goes in v6:
time: 194 us; the launch traced here: 193 us
  waiting for transfers between devices  83.6 us (43%)
  local copies, waits for them, and re-layouts  58.5 us (30%)
  matrix products  25.5 us (13%)
  between operations  14.2 us (7%)
  other arithmetic  6 us (3%)
  starting transfers between devices  5.37 us (3%)
    gather x2, local copies, waits for them, and re-layouts, per_device(): picked = jnp.take(chol_t, domain, axis=0)  51.2 us
    all_to_all x1, waiting for transfers between devices, per_device(): lax.all_to_all(half, 'orb', split_axis=0, concat_axis=0, tiled=True)  50.7 us
    psum x1, waiting for transfers between devices, per_device(): lax.psum(dressing_part, 'chol') * norm_factor  32.9 us
    dot_general x1, matrix products, per_device(): jnp.einsum('fsk,fsa->fka', picked, all_coef, preferred_element_type=jnp.f...  12.9 us
    dot_general x1, matrix products, per_device(): lax.dot_general(weighted.reshape(-1, lno_width), received.reshape(-1, lno...  7.31 us
    dot_general x1, matrix products, per_device(): jnp.einsum('ora,ogrb->gab', own_w, received, preferred_element_type=jnp.f...  5.34 us
    all_to_all x1, starting transfers between devices, per_device(): lax.all_to_all(half, 'orb', split_axis=0, concat_axis=0, tiled=True)  5.29 us
  transfers between devices with their start and end apart: 3, of which 2 were waited for; matrix products, arithmetic and copies ran while one was open for 34% of the time, Pallas kernels for 0%

profile of v6, /device:TPU:0, one launch (start us, length us, event | category | flops | bytes accessed | tf_op | source)
XLA Modules:
  0.0 193.2 jit_solution(15472110756404141395)
XLA Ops:
  7.2 0.0 all-gather.2.cloned.1.call-start
  7.2 0.7 reduce-precision_convert_fusion.1
  7.9 0.1 convert_element_type.38
  8.1 2.1 %pad_maximum_fusion = bf16[1,1032,384]{2,1,0:T(8,128)(2,1)} fusion(bf16[1,8,384]{2,1,0:T(8,128)(2,1)S(1)} %reshape.191, bf16[1,1024,384]{2,1,0:T(8,128)(2,1)} %param.8), kind=kLoop, calls=%fused_computation.21 | loop fusion | flops 1585152 | bytes 1585152 | tf_op jit(solution)/shard_map/concatenate | solution.py:41
  10.2 0.0 all-gather.2.cloned.1.call-update
  10.2 2.8 %copy.29 = bf16[768,1536]{0,1:T(8,128)(2,1)S(1)} copy(bf16[768,1536]{1,0:T(8,128)(2,1)} %bitcast.46) | data formatting | bytes 4718592 | tf_op jit(solution)/shard_map/pick_columns/reshape | solution.py:45
  13.1 34.5 %gather_fusion = bf16[8192,768]{1,0:T(8,128)(2,1)} fusion(bf16[1536,768]{1,0:T(8,128)(2,1)S(1)} %bitcast.42, s32[8192]{0:T(1024)S(1)} %bitcast_clamp_fusion), kind=kCustom, calls=%fused_computation | custom fusion | bytes 25198592 | tf_op jit(solution)/shard_map/pick_columns/jit(_take)/gather | solution.py:46
  47.6 16.7 %copy.30 = bf16[8,1024,768]{1,2,0:T(8,128)(2,1)} copy(bf16[8,1024,768]{2,1,0:T(8,128)(2,1)} %bitcast.43) | data formatting | bytes 25165824 | tf_op jit(solution)/shard_map/pick_columns/jit(_take)/gather | solution.py:46
  64.2 0.1 copy.28
  64.3 0.1 iota_compare_fusion.1
  64.4 0.1 bitcast_compare_fusion
  64.5 12.9 %select_convert_fusion = bf16[8,768,384]{2,1,0:T(8,128)(2,1)} fusion(pred[8,384]{1,0:T(8,128)(4,1)S(1)} %iota_compare_fusion.1, bf16[8,1032,384]{2,1,0:T(8,128)(2,1)} %all-gather.2.cloned.1.call-done, bf16[8,1024,768]{1,2,0:T(8,128)(2,1)} %copy.30, pred[8,1024]{1,0:T(8,128)(4,1)S(1)} %get-tuple-element.16, pred[8,1024]{1,0:T(8,128)(4,1)S(1)} %get-tuple-element.15), kind=kOutput, calls=%fused_computation.10 | convolution fusion | flops 4849139712 | bytes 23612416 | tf_op jit(solution)/shard_map/half/fsk,fsa->fka/dot_general | solution.py:76
  77.4 5.3 %all-to-all-start = ((bf16[8,4,192,384]{3,2,1,0:T(8,128)(2,1)}), bf16[8,4,192,384]{3,2,1,0:T(8,128)(2,1)}, u32[]{:S(2)}, u32[]{:S(2)}) async-start(bf16[8,4,192,384]{3,2,1,0:T(8,128)(2,1)} %bitcast.44), calls=%async_computation | async-start | bytes 9437184 | tf_op jit(solution)/shard_map/all_to_all | solution.py:80
  82.7 0.0 all-reduce.3.cloned.1.call-start
  82.7 0.1 fusion.37
  82.9 0.1 divide_reduce_fusion
  83.0 0.6 iota_reduce_fusion
  83.6 0.6 gather_fusion.1
  84.2 0.7 gather_fusion.3
  85.0 0.6 gather_fusion.2
  85.6 0.1 fusion.32
  85.7 0.1 select_and_fusion
  85.8 0.1 select_subtract_fusion
  85.8 0.8 slice_bitcast_fusion
  86.7 0.1 reshape.196
  86.8 50.7 %all-to-all-done = bf16[8,4,192,384]{3,2,1,0:T(8,128)(2,1)} async-done(((bf16[8,4,192,384]{3,2,1,0:T(8,128)(2,1)}), bf16[8,4,192,384]{3,2,1,0:T(8,128)(2,1)}, u32[]{:S(2)}, u32[]{:S(2)}) %all-to-all-start) | async-done | bytes 4718624 | tf_op jit(solution)/shard_map/all_to_all | solution.py:80
  137.5 7.3 %fusion.16 = f32[384,384]{1,0:T(8,128)} fusion(bf16[8,4,192,384]{3,2,1,0:T(8,128)(2,1)} %all-to-all-done, f32[8,192]{1,0:T(8,128)S(1)} %bitcast.53), kind=kOutput, calls=%fused_computation.20 | convolution fusion | flops 1819017216 | bytes 5314560 | tf_op jit(solution)/shard_map/dressing/dot_general | solution.py:86
  144.8 0.0 all-reduce.3.cloned.1.call-update
  144.9 5.3 %fusion.15 = bf16[4,1,384,384]{2,3,0,1:T(8,128)(2,1)S(1)} fusion(bf16[8,4,192,384]{3,2,1,0:T(8,128)(2,1)} %all-to-all-done, pred[384]{0:T(512)(128)(4,1)S(1)} %dynamic-slice_reduce_fusion.1, bf16[8,128,384]{2,1,0:T(8,128)(2,1)S(1)} %gather_fusion.3, pred[8]{0:T(512)(128)(4,1)S(1)} %compare_and_fusion.1, s32[8,128]{1,0:T(8,128)S(1)} %select_subtract_fusion, ...), kind=kOutput, calls=%fused_computation.19 | convolution fusion | flops 1965490176 | bytes 6690184 | tf_op jit(solution)/shard_map/rotated/ora,ogrb->gab/dot_general | solution.py:95
  150.2 1.5 copy.31
  151.7 32.9 %all-reduce.3.cloned.1.call-done = f32[384,384]{1,0:T(8,128)} async-done(((f32[384,384]{1,0:T(8,128)}), f32[384,384]{1,0:T(8,128)}) %all-reduce.3.cloned.1.call-update) | async-done | bytes 589840 | tf_op jit(solution)/shard_map/dressing/psum | solution.py:92
  184.5 1.8 fusion.30
  (30 shorter events, 0.2 us)
Async XLA Ops:
  7.2 5.9 %copy-start.1 = (s32[8,1024]{1,0:T(8,128)S(1)}, s32[8,1024]{1,0:T(8,128)}, u32[]{:S(2)}) copy-start(s32[8,1024]{1,0:T(8,128)} %param.9) | copy-start | bytes 98308
  7.2 57.3 %all-gather.2.cloned.1.call-start = ((), (), s32[]{:S(2)}) async-start(), calls=%async_computation.1 | async-start | bytes 7133184 | tf_op jit(solution)/shard_map/all_gather | solution.py:42
  47.6 16.7 %copy-start.2 = (s32[8,8]{1,0:T(8,128)S(1)}, s32[8,8]{1,0:T(8,128)}, u32[]{:S(2)}) copy-start(s32[8,8]{1,0:T(8,128)} %param.10) | copy-start | bytes 772
  47.6 16.8 %copy-start.3 = (s32[8]{0:T(128)S(1)}, s32[8]{0:T(128)}, u32[]{:S(2)}) copy-start(s32[8]{0:T(128)} %param.11) | copy-start | bytes 100
  77.4 6.8 %copy-start = (bf16[1,1024,384]{2,1,0:T(8,128)(2,1)S(1)}, bf16[1,1024,384]{2,1,0:T(8,128)(2,1)}, u32[]{:S(2)}) copy-start(bf16[1,1024,384]{2,1,0:T(8,128)(2,1)} %param.8) | copy-start | bytes 2359300
  77.4 60.1 %all-to-all-start = ((bf16[8,4,192,384]{3,2,1,0:T(8,128)(2,1)}), bf16[8,4,192,384]{3,2,1,0:T(8,128)(2,1)}, u32[]{:S(2)}, u32[]{:S(2)}) async-start(bf16[8,4,192,384]{3,2,1,0:T(8,128)(2,1)} %bitcast.44), calls=%async_computation | async-start | bytes 9437184 | tf_op jit(solution)/shard_map/all_to_all | solution.py:80
  82.7 101.8 %all-reduce.3.cloned.1.call-start = ((), (), s32[]{:S(2)}) async-start(), calls=%async_computation.2 | async-start | bytes 1179648 | tf_op jit(solution)/shard_map/dressing/psum | solution.py:92
Sparse Core Ops, SparseCore 0:
  10.5 48.4 all-gather.1
  145.0 39.4 all-reduce.2

commit v7 on v6

--- a/solution.py
+++ b/solution.py
@@ -89,7 +89,15 @@
             (((0,), (0,)), ((), ())),
             preferred_element_type=jnp.float32,
         )
-        dressing = (lax.psum(dressing_part, "chol") * norm_factor).astype(jnp.bfloat16)
+    with jax.named_scope("chol_sum"):
+        hi = lax.reduce_precision(dressing_part, exponent_bits=8, mantissa_bits=7)
+        parts = jnp.stack([hi, dressing_part - hi]).astype(jnp.bfloat16)
+        every = lax.all_gather(parts, "chol", axis=0, tiled=False).astype(jnp.float32)
+        terms = every[:, 0] + every[:, 1]
+        total = terms[0]
+        for c in range(1, chol_size):
+            total = total + terms[c]
+        dressing = (total * norm_factor).astype(jnp.bfloat16)
 
     with jax.named_scope("rotated"):
         rotated = jnp.einsum(

time: 194 us -> 207 us (1.067)
  waiting for transfers between devices: 83.6 us -> 94.9 us
  other arithmetic: 6 us -> 8.09 us
    all_gather x0 -> x1, waiting for transfers between devices: none -> 41 us  [per_device(): lax.all_gather(parts, 'chol', axis=0, tiled=False).astype(jnp.float32)]
    psum x1 -> x0, waiting for transfers between devices: 32.9 us -> none  [per_device(): lax.psum(dressing_part, 'chol') * norm_factor]
    all_to_all x1, waiting for transfers between devices: 50.7 us -> 53.8 us  [per_device(): lax.all_to_all(half, 'orb', split_axis=0, concat_axis=0, tiled=True)]
    convert_element_type x0 -> x2, other arithmetic: none -> 2.81 us  [the longest x1 1.98 us: per_device(): lax.all_gather(parts, 'chol', axis=0, tiled=False).astype(jnp.float32)]
  transfers between devices with their start and end apart: 3 -> 3, of which waited for: 2 -> 2; matrix products, arithmetic and copies ran while one was open for 34% -> 32% of each run, Pallas kernels for 0% -> 0%
where the time goes in v7:
time: 207 us; the launch traced here: 206 us
  waiting for transfers between devices  94.9 us (46%)
  local copies, waits for them, and re-layouts  58.5 us (28%)
  matrix products  24.8 us (12%)
  between operations  14.2 us (7%)
  other arithmetic  8.09 us (4%)
  starting transfers between devices  5.24 us (3%)
    all_to_all x1, waiting for transfers between devices, per_device(): lax.all_to_all(half, 'orb', split_axis=0, concat_axis=0, tiled=True)  53.8 us
    gather x2, local copies, waits for them, and re-layouts, per_device(): picked = jnp.take(chol_t, domain, axis=0)  51.2 us
    all_gather x1, waiting for transfers between devices, per_device(): lax.all_gather(parts, 'chol', axis=0, tiled=False).astype(jnp.float32)  41 us
    dot_general x1, matrix products, per_device(): jnp.einsum('fsk,fsa->fka', picked, all_coef, preferred_element_type=jnp.f...  12.9 us
    dot_general x1, matrix products, per_device(): lax.dot_general(weighted.reshape(-1, lno_width), received.reshape(-1, lno...  6.54 us
    dot_general x1, matrix products, per_device(): jnp.einsum('ora,ogrb->gab', own_w, received, preferred_element_type=jnp.f...  5.34 us
    all_to_all x1, starting transfers between devices, per_device(): lax.all_to_all(half, 'orb', split_axis=0, concat_axis=0, tiled=True)  5.16 us
  transfers between devices with their start and end apart: 3, of which 2 were waited for; matrix products, arithmetic and copies ran while one was open for 32% of the time, Pallas kernels for 0%

profile of v7, /device:TPU:0, one launch (start us, length us, event | category | flops | bytes accessed | tf_op | source)
XLA Modules:
  0.0 205.6 jit_solution(3772079139776102653)
XLA Ops:
  7.2 0.0 all-gather.3.cloned.1.call-start
  7.2 0.7 reduce-precision_convert_fusion.2
  7.9 0.1 convert_element_type.50
  8.1 2.1 %pad_maximum_fusion = bf16[1,1032,384]{2,1,0:T(8,128)(2,1)} fusion(bf16[1,8,384]{2,1,0:T(8,128)(2,1)S(1)} %reshape.232, bf16[1,1024,384]{2,1,0:T(8,128)(2,1)} %param.8), kind=kLoop, calls=%fused_computation.24 | loop fusion | flops 1585152 | bytes 1585152 | tf_op jit(solution)/shard_map/concatenate | solution.py:41
  10.2 2.8 %copy.29 = bf16[768,1536]{0,1:T(8,128)(2,1)S(1)} copy(bf16[768,1536]{1,0:T(8,128)(2,1)} %bitcast.52) | data formatting | bytes 4718592 | tf_op jit(solution)/shard_map/pick_columns/reshape | solution.py:45
  13.1 34.5 %gather_fusion = bf16[8192,768]{1,0:T(8,128)(2,1)} fusion(bf16[1536,768]{1,0:T(8,128)(2,1)S(1)} %bitcast.48, s32[8192]{0:T(1024)S(1)} %bitcast_clamp_fusion), kind=kCustom, calls=%fused_computation | custom fusion | bytes 25198592 | tf_op jit(solution)/shard_map/pick_columns/jit(_take)/gather | solution.py:46
  47.6 16.7 %copy.30 = bf16[8,1024,768]{1,2,0:T(8,128)(2,1)} copy(bf16[8,1024,768]{2,1,0:T(8,128)(2,1)} %bitcast.49) | data formatting | bytes 25165824 | tf_op jit(solution)/shard_map/pick_columns/jit(_take)/gather | solution.py:46
  64.2 0.1 copy.28
  64.3 0.1 iota_compare_fusion.1
  64.4 0.1 bitcast_compare_fusion
  64.5 12.9 %select_convert_fusion = bf16[8,768,384]{2,1,0:T(8,128)(2,1)} fusion(pred[8,384]{1,0:T(8,128)(4,1)S(1)} %iota_compare_fusion.1, bf16[8,1032,384]{2,1,0:T(8,128)(2,1)} %all-gather.3.cloned.1.call-done, bf16[8,1024,768]{1,2,0:T(8,128)(2,1)} %copy.30, pred[8,1024]{1,0:T(8,128)(4,1)S(1)} %get-tuple-element.18, pred[8,1024]{1,0:T(8,128)(4,1)S(1)} %get-tuple-element.17), kind=kOutput, calls=%fused_computation.10 | convolution fusion | flops 4849139712 | bytes 23612416 | tf_op jit(solution)/shard_map/half/fsk,fsa->fka/dot_general | solution.py:76
  77.4 5.2 %all-to-all-start = ((bf16[8,4,192,384]{3,2,1,0:T(8,128)(2,1)}), bf16[8,4,192,384]{3,2,1,0:T(8,128)(2,1)}, u32[]{:S(2)}, u32[]{:S(2)}) async-start(bf16[8,4,192,384]{3,2,1,0:T(8,128)(2,1)} %bitcast.50), calls=%async_computation | async-start | bytes 9437184 | tf_op jit(solution)/shard_map/all_to_all | solution.py:80
  82.6 0.8 slice_bitcast_fusion
  83.4 0.1 reshape.240
  83.5 53.8 %all-to-all-done = bf16[8,4,192,384]{3,2,1,0:T(8,128)(2,1)} async-done(((bf16[8,4,192,384]{3,2,1,0:T(8,128)(2,1)}), bf16[8,4,192,384]{3,2,1,0:T(8,128)(2,1)}, u32[]{:S(2)}, u32[]{:S(2)}) %all-to-all-start) | async-done | bytes 4718624 | tf_op jit(solution)/shard_map/all_to_all | solution.py:80
  137.4 6.5 %fusion.35 = (bf16[1,1,384,384]{3,2,1,0:T(8,128)(2,1)S(1)}, bf16[1,1,384,384]{3,2,1,0:T(8,128)(2,1)S(1)}) fusion(bf16[8,4,192,384]{3,2,1,0:T(8,128)(2,1)} %all-to-all-done, f32[8,192]{1,0:T(8,128)S(1)} %bitcast.59), kind=kOutput, calls=%fused_computation.41 | convolution fusion | flops 1819607040 | bytes 5314560 | tf_op jit(solution)/shard_map/dressing/dot_general | solution.py:86
  143.9 0.9 pad_maximum_fusion.1
  144.9 0.1 fusion.42
  145.0 0.1 divide_reduce_fusion
  145.1 0.6 iota_reduce_fusion
  145.8 0.6 gather_fusion.1
  146.3 0.7 gather_fusion.3
  147.1 0.6 gather_fusion.2
  147.7 0.1 fusion.37
  147.8 0.1 select_and_fusion
  147.9 0.1 select_subtract_fusion
  148.0 5.3 %fusion.15 = bf16[4,1,384,384]{2,3,0,1:T(8,128)(2,1)S(1)} fusion(bf16[8,4,192,384]{3,2,1,0:T(8,128)(2,1)} %all-to-all-done, pred[384]{0:T(512)(128)(4,1)S(1)} %dynamic-slice_reduce_fusion.1, bf16[8,128,384]{2,1,0:T(8,128)(2,1)S(1)} %gather_fusion.3, pred[8]{0:T(512)(128)(4,1)S(1)} %compare_and_fusion.1, s32[8,128]{1,0:T(8,128)S(1)} %select_subtract_fusion, ...), kind=kOutput, calls=%fused_computation.20 | convolution fusion | flops 1965490176 | bytes 6690184 | tf_op jit(solution)/shard_map/rotated/ora,ogrb->gab/dot_general | solution.py:103
  153.3 1.5 copy.31
  154.8 41.0 %all-gather.5.cloned.1.call-done = bf16[4,2,384,384]{3,2,1,0:T(8,128)(2,1)} async-done(((bf16[1,2,384,384]{3,2,1,0:T(8,128)(2,1)}), bf16[4,2,384,384]{3,2,1,0:T(8,128)(2,1)}) %all-gather.5.cloned.1.call-update) | async-done | bytes 2359312 | tf_op jit(solution)/shard_map/chol_sum/all_gather | solution.py:95
  195.7 2.0 convert_element_type.60
  197.7 0.2 slice_add_fusion
  197.9 0.8 fusion.33
  (33 shorter events, 0.3 us)
Async XLA Ops:
  7.2 5.9 %copy-start.1 = (s32[8,1024]{1,0:T(8,128)S(1)}, s32[8,1024]{1,0:T(8,128)}, u32[]{:S(2)}) copy-start(s32[8,1024]{1,0:T(8,128)} %param.9) | copy-start | bytes 98308
  7.2 57.3 %all-gather.3.cloned.1.call-start = ((), (), s32[]{:S(2)}) async-start(), calls=%async_computation.1 | async-start | bytes 7133184 | tf_op jit(solution)/shard_map/all_gather | solution.py:42
  47.6 16.7 %copy-start.2 = (s32[8,8]{1,0:T(8,128)S(1)}, s32[8,8]{1,0:T(8,128)}, u32[]{:S(2)}) copy-start(s32[8,8]{1,0:T(8,128)} %param.10) | copy-start | bytes 772
  47.6 16.8 %copy-start.3 = (s32[8]{0:T(128)S(1)}, s32[8]{0:T(128)}, u32[]{:S(2)}) copy-start(s32[8]{0:T(128)} %param.11) | copy-start | bytes 100
  77.4 60.0 %all-to-all-start = ((bf16[8,4,192,384]{3,2,1,0:T(8,128)(2,1)}), bf16[8,4,192,384]{3,2,1,0:T(8,128)(2,1)}, u32[]{:S(2)}, u32[]{:S(2)}) async-start(bf16[8,4,192,384]{3,2,1,0:T(8,128)(2,1)} %bitcast.50), calls=%async_computation | async-start | bytes 9437184 | tf_op jit(solution)/shard_map/all_to_all | solution.py:80
  82.5 113.2 %all-gather.5.cloned.1.call-start = ((), (), s32[]{:S(2)}) async-start(), calls=%async_computation.2 | async-start | bytes 2949120 | tf_op jit(solution)/shard_map/chol_sum/all_gather | solution.py:95
  137.4 8.9 %copy-start = (bf16[1,1024,384]{2,1,0:T(8,128)(2,1)S(1)}, bf16[1,1024,384]{2,1,0:T(8,128)(2,1)}, u32[]{:S(2)}) copy-start(bf16[1,1024,384]{2,1,0:T(8,128)(2,1)} %param.8) | copy-start | bytes 2359300
Sparse Core Ops, SparseCore 0:
  10.5 48.4 all-gather.2
  145.0 50.7 all-gather.4

commit v8 on v6

--- a/solution.py
+++ b/solution.py
@@ -34,46 +34,55 @@
     slot_ok = (slot_index % group_width)[None, :] < jnp.repeat(block_fill, group_width, axis=1)
     column_ok = jnp.arange(lno_width, dtype=jnp.int32)[None, :] < lno_count[:, None]
 
+    with jax.named_scope("placement"):
+        groups = domain.reshape(frag_total, group_count, group_width)
+        group_block = groups[:, :, 0] // orb_rows
+        block_ids = jnp.arange(orb_size, dtype=jnp.int32)
+        sel = group_block[:, None, :] == block_ids[None, :, None]
+        present = jnp.any(sel, axis=2)
+        group_of_block = jnp.argmax(sel, axis=2).astype(jnp.int32)
+        local = jnp.take_along_axis(groups, group_of_block[:, :, None], axis=1)
+        local = local - block_ids[None, :, None] * orb_rows
+        fill = jnp.take_along_axis(
+            slot_ok.reshape(frag_total, group_count, group_width), group_of_block[:, :, None], axis=1
+        ) & present[:, :, None]
+        row_ids = jnp.arange(orb_rows, dtype=jnp.int32)
+        onehot = ((local[:, :, None, :] == row_ids[None, None, :, None]) & fill[:, :, None, :]).astype(jnp.bfloat16)
+
+    own_pick = lax.dynamic_index_in_dim(group_of_block, my_index, 0, keepdims=False)
+    own_perm = jnp.take(lno_coef[0].reshape(group_count, group_width, lno_width), own_pick, axis=0)
     weight_rows = -(-3 * orb_rows // lno_width)
     pad_rows = -(-weight_rows // 8) * 8
     weight_parts = split_bf16(env_weight).reshape(-1)
     weight_parts = jnp.pad(weight_parts, (0, pad_rows * lno_width - weight_parts.shape[0]))
-    payload = jnp.concatenate([lno_coef, weight_parts.reshape(1, pad_rows, lno_width)], axis=1)
+    block_slots = orb_size * group_width
+    payload = jnp.concatenate(
+        [own_perm.reshape(1, block_slots, lno_width), weight_parts.reshape(1, pad_rows, lno_width)], axis=1
+    )
     gathered = lax.all_gather(payload, "orb", axis=0, tiled=True)
 
     with jax.named_scope("pick_columns"):
-        chol_t = chol_vec.reshape(chol_local * orb_rows, orb_total).T
-        picked = jnp.take(chol_t, domain, axis=0)
-        picked = jnp.where(slot_ok[:, :, None], picked, jnp.zeros_like(picked))
+        chol_blocks = chol_vec.reshape(chol_local * orb_rows, orb_size, orb_rows)
+        picked = jnp.einsum(
+            "kor,forc->fkoc", chol_blocks, onehot, preferred_element_type=jnp.float32
+        ).astype(jnp.bfloat16).reshape(frag_total, chol_local * orb_rows, block_slots)
 
     with jax.named_scope("own_placement"):
-        own_groups = lax.dynamic_index_in_dim(domain, my_index, 0, keepdims=False)
-        own_groups = own_groups.reshape(group_count, group_width)
-        own_fill = lax.dynamic_index_in_dim(slot_ok, my_index, 0, keepdims=False)
-        own_fill = own_fill.reshape(group_count, group_width)
+        own_hot = lax.dynamic_index_in_dim(onehot, my_index, 0, keepdims=False)
         own_cols = lax.dynamic_index_in_dim(column_ok, my_index, 0, keepdims=False)
-        block_ids = jnp.arange(orb_size, dtype=jnp.int32)
-        sel = (own_groups[:, 0] // orb_rows)[None, :] == block_ids[:, None]
-        present = jnp.any(sel, axis=1)
-        group_of_block = jnp.argmax(sel, axis=1).astype(jnp.int32)
-        local = jnp.take(own_groups, group_of_block, axis=0) - block_ids[:, None] * orb_rows
-        fill = jnp.take(own_fill, group_of_block, axis=0) & present[:, None]
-        row_ids = jnp.arange(orb_rows, dtype=jnp.int32)
-        onehot = ((local[:, None, :] == row_ids[None, :, None]) & fill[:, None, :]).astype(jnp.bfloat16)
-        own_coef = jnp.take(lno_coef[0].reshape(group_count, group_width, lno_width), group_of_block, axis=0)
-        own_w = jnp.einsum("brs,bsa->bra", onehot, own_coef, preferred_element_type=jnp.float32)
+        own_w = jnp.einsum("orc,oca->ora", own_hot, own_perm, preferred_element_type=jnp.float32)
         own_w = jnp.where(own_cols[None, None, :], own_w, 0.0).astype(jnp.bfloat16)
 
-    all_coef = gathered[:, :slot_total]
+    all_coef = gathered[:, :block_slots]
     weight_all = join_bf16(
-        gathered[:, slot_total:]
+        gathered[:, block_slots:]
         .reshape(orb_size, -1)[:, : 3 * orb_rows]
         .reshape(orb_size, 3, orb_rows)
         .transpose(1, 0, 2)
     )
 
     with jax.named_scope("half"):
-        half = jnp.einsum("fsk,fsa->fka", picked, all_coef, preferred_element_type=jnp.float32)
+        half = jnp.einsum("fks,fsa->fka", picked, all_coef, preferred_element_type=jnp.float32)
         half = jnp.where(column_ok[:, None, :], half, 0.0).astype(jnp.bfloat16)
         half = half.reshape(frag_total, chol_local, orb_rows, lno_width)
 

time: 194 us -> 188 us (0.969)
  local copies, waits for them, and re-layouts: 58.5 us -> 18.5 us
  waiting for transfers between devices: 83.6 us -> 107 us
  matrix products: 25.5 us -> 36.1 us
    gather x5 -> x4, local copies, waits for them, and re-layouts: 53 us -> 2.37 us  [the longest x2 0.84 us: per_device(): local = jnp.take_along_axis(groups, group_of_block[:, :, None], axis=1)]
    all_gather x1, waiting for transfers between devices: 0.02 us -> 25.3 us  [per_device(): gathered = lax.all_gather(payload, 'orb', axis=0, tiled=True)]
    dot_general x1 -> x2, matrix products: 12.9 us -> 22.4 us  [the longest x1 13 us: per_device(): jnp.einsum('fks,fsa->fka', picked, all_coef, preferred_element_type=jnp.f...]
    convert_element_type x0 -> x1, local copies, waits for them, and re-layouts: none -> 5.63 us  [per_device(): picked = jnp.einsum('kor,forc->fkoc', chol_blocks, onehot, preferred_elem...]
    psum x1, waiting for transfers between devices: 32.9 us -> 29.6 us  [per_device(): lax.psum(dressing_part, 'chol') * norm_factor]
    reshape x1, local copies, waits for them, and re-layouts: 2.84 us -> 5.96 us  [per_device(): chol_blocks = chol_vec.reshape(chol_local * orb_rows, orb_size, orb_rows)]
    unnamed x13 -> x12, local copies, waits for them, and re-layouts: 2.36 us -> 4.16 us
  transfers between devices with their start and end apart: 3 -> 3, of which waited for: 2 -> 3; matrix products, arithmetic and copies ran while one was open for 34% -> 18% of each run, Pallas kernels for 0% -> 0%
where the time goes in v8:
time: 188 us; the launch traced here: 187 us
  waiting for transfers between devices  107 us (57%)
  matrix products  36.1 us (19%)
  local copies, waits for them, and re-layouts  18.5 us (10%)
  between operations  14.2 us (8%)
  other arithmetic  6.9 us (4%)
  starting transfers between devices  4.85 us (3%)
    all_to_all x1, waiting for transfers between devices, per_device(): lax.all_to_all(half, 'orb', split_axis=0, concat_axis=0, tiled=True)  51.9 us
    psum x1, waiting for transfers between devices, per_device(): lax.psum(dressing_part, 'chol') * norm_factor  29.6 us
    all_gather x1, waiting for transfers between devices, per_device(): gathered = lax.all_gather(payload, 'orb', axis=0, tiled=True)  25.3 us
    dot_general x1, matrix products, per_device(): jnp.einsum('fks,fsa->fka', picked, all_coef, preferred_element_type=jnp.f...  13 us
    dot_general x1, matrix products, per_device(): jnp.einsum('kor,forc->fkoc', chol_blocks, onehot, preferred_element_type=...  9.4 us
    dot_general x1, matrix products, per_device(): lax.dot_general(weighted.reshape(-1, lno_width), received.reshape(-1, lno...  7.31 us
    dot_general x1, matrix products, per_device(): jnp.einsum('ora,ogrb->gab', own_w, received, preferred_element_type=jnp.f...  6.41 us
    reshape x1, local copies, waits for them, and re-layouts, per_device(): chol_blocks = chol_vec.reshape(chol_local * orb_rows, orb_size, orb_rows)  5.96 us
  transfers between devices with their start and end apart: 3, of which 3 were waited for; matrix products, arithmetic and copies ran while one was open for 18% of the time, Pallas kernels for 0%

profile of v8, /device:TPU:0, one launch (start us, length us, event | category | flops | bytes accessed | tf_op | source)
XLA Modules:
  0.0 187.4 jit_solution(15248110825288862906)
XLA Ops:
  7.2 0.8 copy.70
  8.1 0.1 copy.63
  8.2 0.9 iota_reduce_fusion
  9.2 0.7 reduce-precision_convert_fusion.1
  9.9 0.1 convert_element_type.46
  10.0 0.1 broadcast_bitcast_fusion
  10.1 0.7 gather_fusion
  10.8 0.2 bitcast_select_fusion
  11.0 1.0 pad_maximum_fusion
  12.0 6.0 %reshape.200 = bf16[768,8,192]{2,1,0:T(8,128)(2,1)} reshape(bf16[4,192,1536]{2,1,0:T(8,128)(2,1)} %param.6) | data formatting | bytes 4718592 | tf_op jit(solution)/shard_map/pick_columns/reshape | solution.py:65
  18.0 0.1 reshape.214
  18.1 0.8 gather_fusion.1
  18.9 0.1 fusion.22
  19.0 0.1 broadcast_compare_fusion
  19.1 0.8 gather_fusion.2
  19.9 0.2 fusion.23
  20.1 0.1 fusion.24
  20.2 9.4 %convert_bitcast_fusion = bf16[8,768,8,128]{1,3,0,2:T(8,128)(2,1)S(1)} fusion(bf16[768,8,192,1]{2,1,0,3:T(8,128)(2,1)} %bitcast.80, s32[8,8,128]{2,0,1:T(8,128)S(1)} %copy.50, pred[8,8,128]{2,0,1:T(8,128)(4,1)S(1)} %copy.51), kind=kOutput, calls=%fused_computation.3 | convolution fusion | flops 2425356288 | bytes 14983168 | tf_op jit(solution)/shard_map/pick_columns/kor,forc->fkoc/dot_general | solution.py:66
  29.6 5.6 %copy.53 = bf16[8,768,8,128]{1,3,2,0:T(8,128)(2,1)} copy(bf16[8,768,8,128]{1,3,0,2:T(8,128)(2,1)S(1)} %convert_bitcast_fusion) | data formatting | bytes 25165824 | tf_op jit(solution)/shard_map/pick_columns/convert_element_type | solution.py:68
  35.3 25.3 %all-gather.2.cloned.1.call-done = bf16[8,1032,384]{2,1,0:T(8,128)(2,1)} async-done(((bf16[1,1032,384]{2,1,0:T(8,128)(2,1)}), bf16[8,1032,384]{2,1,0:T(8,128)(2,1)}) %all-gather.2.cloned.1.call-update) | async-done | bytes 6340624 | tf_op jit(solution)/shard_map/all_gather | solution.py:62
  60.6 13.0 %select_convert_fusion = bf16[8,768,384]{2,1,0:T(8,128)(2,1)} fusion(pred[8,384]{1,0:T(8,128)(4,1)S(1)} %iota_compare_fusion.2, bf16[8,768,1024]{1,2,0:T(8,128)(2,1)} %bitcast.75, bf16[8,1032,384]{2,1,0:T(8,128)(2,1)} %all-gather.2.cloned.1.call-done), kind=kOutput, calls=%fused_computation.5 | convolution fusion | flops 4836556800 | bytes 23596032 | tf_op jit(solution)/shard_map/half/fks,fsa->fka/dot_general | solution.py:85
  73.6 4.6 %all-to-all-start = ((bf16[8,4,192,384]{3,2,1,0:T(8,128)(2,1)}), bf16[8,4,192,384]{3,2,1,0:T(8,128)(2,1)}, u32[]{:S(2)}, u32[]{:S(2)}) async-start(bf16[8,4,192,384]{3,2,1,0:T(8,128)(2,1)} %bitcast.76), calls=%async_computation | async-start | bytes 9437184 | tf_op jit(solution)/shard_map/all_to_all | solution.py:89
  78.2 0.2 all-reduce.3.cloned.1.call-start
  78.5 1.6 fusion.3
  80.1 0.8 slice_bitcast_fusion
  81.0 0.1 reshape.205
  81.1 51.9 %all-to-all-done = bf16[8,4,192,384]{3,2,1,0:T(8,128)(2,1)} async-done(((bf16[8,4,192,384]{3,2,1,0:T(8,128)(2,1)}), bf16[8,4,192,384]{3,2,1,0:T(8,128)(2,1)}, u32[]{:S(2)}, u32[]{:S(2)}) %all-to-all-start) | async-done | bytes 4718624 | tf_op jit(solution)/shard_map/all_to_all | solution.py:89
  133.0 7.3 %fusion.10 = f32[384,384]{1,0:T(8,128)} fusion(bf16[8,4,192,384]{3,2,1,0:T(8,128)(2,1)} %all-to-all-done, f32[8,192]{1,0:T(8,128)S(1)} %bitcast.84), kind=kOutput, calls=%fused_computation.17 | convolution fusion | flops 1819017216 | bytes 5314560 | tf_op jit(solution)/shard_map/dressing/dot_general | solution.py:95
  140.3 6.4 %fusion.9 = bf16[4,1,384,384]{2,3,0,1:T(8,128)(2,1)} fusion(bf16[8,4,192,384]{3,2,1,0:T(8,128)(2,1)} %all-to-all-done, pred[384]{0:T(512)(128)(4,1)S(1)} %dynamic-slice_reduce_fusion, bf16[8,128,384]{2,1,0:T(8,128)(2,1)S(1)} %gather_fusion, pred[8]{0:T(512)(128)(4,1)S(1)} %compare_and_fusion.1, pred[8,8,192,128]{3,2,0,1:T(32,128)(4,1)S(1)} %fusion.3, ...), kind=kOutput, calls=%fused_computation.16 | convolution fusion | flops 1965096960 | bytes 6882308 | tf_op jit(solution)/shard_map/rotated/ora,ogrb->gab/dot_general | solution.py:104
  146.7 2.4 %copy.55 = bf16[4,1,384,384]{3,2,1,0:T(8,128)(2,1)} copy(bf16[4,1,384,384]{2,3,0,1:T(8,128)(2,1)} %fusion.9) | data formatting | bytes 2359296
  149.1 29.6 %all-reduce.3.cloned.1.call-done = f32[384,384]{1,0:T(8,128)} async-done(((f32[384,384]{1,0:T(8,128)}), f32[384,384]{1,0:T(8,128)}) %all-reduce.3.cloned.1.call-update) | async-done | bytes 589840 | tf_op jit(solution)/shard_map/dressing/psum | solution.py:101
  178.7 1.8 fusion.21
  (31 shorter events, 0.4 us)
Async XLA Ops:
  7.2 2.9 %copy-start = (bf16[1,1024,384]{2,1,0:T(8,128)(2,1)S(1)}, bf16[1,1024,384]{2,1,0:T(8,128)(2,1)}, u32[]{:S(2)}) copy-start(bf16[1,1024,384]{2,1,0:T(8,128)(2,1)} %param.8) | copy-start | bytes 2359300
  7.2 53.5 %all-gather.2.cloned.1.call-start = ((), (), s32[]{:S(2)}) async-start(), calls=%async_computation.1 | async-start | bytes 7133184 | tf_op jit(solution)/shard_map/all_gather | solution.py:62
  10.8 8.2 %copy-start.1 = (s32[8,8]{1,0:T(8,128)S(1)}, s32[8,8]{1,0:T(8,128)}, u32[]{:S(2)}) copy-start(s32[8,8]{1,0:T(8,128)} %param.10) | copy-start | bytes 772
  29.6 5.6 %copy-start.2 = (s32[8]{0:T(128)S(1)}, s32[8]{0:T(128)}, u32[]{:S(2)}) copy-start(s32[8]{0:T(128)} %param.11) | copy-start | bytes 100
  73.6 59.3 %all-to-all-start = ((bf16[8,4,192,384]{3,2,1,0:T(8,128)(2,1)}), bf16[8,4,192,384]{3,2,1,0:T(8,128)(2,1)}, u32[]{:S(2)}, u32[]{:S(2)}) async-start(bf16[8,4,192,384]{3,2,1,0:T(8,128)(2,1)} %bitcast.76), calls=%async_computation | async-start | bytes 9437184 | tf_op jit(solution)/shard_map/all_to_all | solution.py:89
  78.2 100.4 %all-reduce.3.cloned.1.call-start = ((), (), s32[]{:S(2)}) async-start(), calls=%async_computation.2 | async-start | bytes 1179648 | tf_op jit(solution)/shard_map/dressing/psum | solution.py:101
Sparse Core Ops, SparseCore 0:
  12.1 48.4 all-gather.1
  140.4 38.2 all-reduce.2

commit v9 on v8

--- a/solution.py
+++ b/solution.py
@@ -50,7 +50,10 @@
         onehot = ((local[:, :, None, :] == row_ids[None, None, :, None]) & fill[:, :, None, :]).astype(jnp.bfloat16)
 
     own_pick = lax.dynamic_index_in_dim(group_of_block, my_index, 0, keepdims=False)
-    own_perm = jnp.take(lno_coef[0].reshape(group_count, group_width, lno_width), own_pick, axis=0)
+    own_slots = lax.dynamic_index_in_dim(slot_ok, my_index, 0, keepdims=False)
+    own_cols = lax.dynamic_index_in_dim(column_ok, my_index, 0, keepdims=False)
+    own_masked = jnp.where(own_slots[:, None] & own_cols[None, :], lno_coef[0], jnp.zeros_like(lno_coef[0]))
+    own_perm = jnp.take(own_masked.reshape(group_count, group_width, lno_width), own_pick, axis=0)
     weight_rows = -(-3 * orb_rows // lno_width)
     pad_rows = -(-weight_rows // 8) * 8
     weight_parts = split_bf16(env_weight).reshape(-1)
@@ -69,9 +72,9 @@
 
     with jax.named_scope("own_placement"):
         own_hot = lax.dynamic_index_in_dim(onehot, my_index, 0, keepdims=False)
-        own_cols = lax.dynamic_index_in_dim(column_ok, my_index, 0, keepdims=False)
-        own_w = jnp.einsum("orc,oca->ora", own_hot, own_perm, preferred_element_type=jnp.float32)
-        own_w = jnp.where(own_cols[None, None, :], own_w, 0.0).astype(jnp.bfloat16)
+        own_w = jnp.einsum(
+            "orc,oca->ora", own_hot, own_perm, preferred_element_type=jnp.float32
+        ).astype(jnp.bfloat16)
 
     all_coef = gathered[:, :block_slots]
     weight_all = join_bf16(
@@ -83,7 +86,7 @@
 
     with jax.named_scope("half"):
         half = jnp.einsum("fks,fsa->fka", picked, all_coef, preferred_element_type=jnp.float32)
-        half = jnp.where(column_ok[:, None, :], half, 0.0).astype(jnp.bfloat16)
+        half = half.astype(jnp.bfloat16)
         half = half.reshape(frag_total, chol_local, orb_rows, lno_width)
 
     received = lax.all_to_all(half, "orb", split_axis=0, concat_axis=0, tiled=True)

time: 188 us -> 192 us (1.021)
  waiting for transfers between devices: 107 us -> 111 us
  other arithmetic: 6.9 us -> 8.96 us
    reshape x1, local copies, waits for them, and re-layouts: 5.96 us -> 3.62 us  [per_device(): chol_blocks = chol_vec.reshape(chol_local * orb_rows, orb_size, orb_rows)]
    psum x1, waiting for transfers between devices: 29.6 us -> 31.7 us  [per_device(): lax.psum(dressing_part, 'chol') * norm_factor]
    all_gather x1, waiting for transfers between devices: 25.3 us -> 27.2 us  [per_device(): gathered = lax.all_gather(payload, 'orb', axis=0, tiled=True)]
  transfers between devices with their start and end apart: 3 -> 3, of which waited for: 3 -> 3; matrix products, arithmetic and copies ran while one was open for 18% -> 16% of each run, Pallas kernels for 0% -> 0%
where the time goes in v9:
time: 192 us
  waiting for transfers between devices  111 us (58%)
  matrix products  34.8 us (18%)
  local copies, waits for them, and re-layouts  17.8 us (9%)
  between operations  14.2 us (7%)
  other arithmetic  8.96 us (5%)
  starting transfers between devices  4.85 us (3%)
    all_to_all x1, waiting for transfers between devices, per_device(): lax.all_to_all(half, 'orb', split_axis=0, concat_axis=0, tiled=True)  51.9 us
    psum x1, waiting for transfers between devices, per_device(): lax.psum(dressing_part, 'chol') * norm_factor  31.7 us
    all_gather x1, waiting for transfers between devices, per_device(): gathered = lax.all_gather(payload, 'orb', axis=0, tiled=True)  27.2 us
    dot_general x1, matrix products, per_device(): jnp.einsum('fks,fsa->fka', picked, all_coef, preferred_element_type=jnp.f...  13 us
    dot_general x1, matrix products, per_device(): jnp.einsum('kor,forc->fkoc', chol_blocks, onehot, preferred_element_type=...  9.15 us
    dot_general x1, matrix products, per_device(): lax.dot_general(weighted.reshape(-1, lno_width), received.reshape(-1, lno...  7.31 us
    convert_element_type x1, local copies, waits for them, and re-layouts, per_device(): picked = jnp.einsum('kor,forc->fkoc', chol_blocks, onehot, preferred_elem...  5.63 us
    dot_general x1, matrix products, per_device(): jnp.einsum('ora,ogrb->gab', own_w, received, preferred_element_type=jnp.f...  5.34 us
  transfers between devices with their start and end apart: 3, of which 3 were waited for; matrix products, arithmetic and copies ran while one was open for 16% of the time, Pallas kernels for 0%

profile of v9, /device:TPU:0, one launch (start us, length us, event | category | flops | bytes accessed | tf_op | source)
XLA Modules:
  0.0 191.6 jit_solution(16111767947179798101)
XLA Ops:
  7.2 0.8 copy.73
  8.0 0.1 copy.63
  8.1 0.9 iota_reduce_fusion
  9.1 0.7 reduce-precision_convert_fusion.1
  9.8 0.1 convert_element_type.46
  10.0 1.2 dynamic-slice
  11.2 0.7 compare_reduce_fusion.1
  11.9 0.8 broadcast_bitcast_fusion
  12.7 1.4 and_select_fusion
  14.2 0.7 gather_fusion
  14.9 0.2 bitcast_select_fusion
  15.1 1.0 pad_maximum_fusion
  16.1 0.7 copy-done
  16.9 3.6 %reshape.199 = bf16[768,8,192]{2,1,0:T(8,128)(2,1)} reshape(bf16[4,192,1536]{2,1,0:T(8,128)(2,1)S(1)} %copy-done) | data formatting | bytes 4718592 | tf_op jit(solution)/shard_map/pick_columns/reshape | solution.py:68
  20.6 0.8 gather_fusion.1
  21.5 0.8 gather_fusion.2
  22.4 0.2 fusion.25
  22.6 0.1 fusion.26
  22.7 9.2 %convert_bitcast_fusion = bf16[8,768,8,128]{1,3,0,2:T(8,128)(2,1)S(1)} fusion(bf16[768,8,192,1]{2,1,0,3:T(8,128)(2,1)} %bitcast.85, s32[8,8,128]{2,0,1:T(8,128)S(1)} %copy.50, pred[8,8,128]{2,0,1:T(8,128)(4,1)S(1)} %copy.51), kind=kOutput, calls=%fused_computation.3 | convolution fusion | flops 2425356288 | bytes 14983168 | tf_op jit(solution)/shard_map/pick_columns/kor,forc->fkoc/dot_general | solution.py:69
  31.9 5.6 %copy.53 = bf16[8,768,8,128]{1,3,2,0:T(8,128)(2,1)} copy(bf16[8,768,8,128]{1,3,0,2:T(8,128)(2,1)S(1)} %convert_bitcast_fusion) | data formatting | bytes 25165824 | tf_op jit(solution)/shard_map/pick_columns/convert_element_type | solution.py:71
  37.5 27.2 %all-gather.2.cloned.1.call-done = bf16[8,1032,384]{2,1,0:T(8,128)(2,1)} async-done(((bf16[1,1032,384]{2,1,0:T(8,128)(2,1)}), bf16[8,1032,384]{2,1,0:T(8,128)(2,1)}) %all-gather.2.cloned.1.call-update) | async-done | bytes 6340624 | tf_op jit(solution)/shard_map/all_gather | solution.py:65
  64.7 13.0 %fusion.6 = bf16[8,768,384]{2,1,0:T(8,128)(2,1)} fusion(bf16[8,768,1024]{1,2,0:T(8,128)(2,1)} %bitcast.80, bf16[8,1032,384]{2,1,0:T(8,128)(2,1)} %all-gather.2.cloned.1.call-done), kind=kOutput, calls=%fused_computation.12 | convolution fusion | flops 4834197504 | bytes 23592960 | tf_op jit(solution)/shard_map/half/fks,fsa->fka/dot_general | solution.py:88
  77.7 4.6 %all-to-all-start = ((bf16[8,4,192,384]{3,2,1,0:T(8,128)(2,1)}), bf16[8,4,192,384]{3,2,1,0:T(8,128)(2,1)}, u32[]{:S(2)}, u32[]{:S(2)}) async-start(bf16[8,4,192,384]{3,2,1,0:T(8,128)(2,1)} %bitcast.81), calls=%async_computation | async-start | bytes 9437184 | tf_op jit(solution)/shard_map/all_to_all | solution.py:92
  82.3 0.2 all-reduce.3.cloned.1.call-start
  82.5 1.6 fusion.3
  84.2 0.8 slice_bitcast_fusion
  85.1 51.9 %all-to-all-done = bf16[8,4,192,384]{3,2,1,0:T(8,128)(2,1)} async-done(((bf16[8,4,192,384]{3,2,1,0:T(8,128)(2,1)}), bf16[8,4,192,384]{3,2,1,0:T(8,128)(2,1)}, u32[]{:S(2)}, u32[]{:S(2)}) %all-to-all-start) | async-done | bytes 4718624 | tf_op jit(solution)/shard_map/all_to_all | solution.py:92
  137.1 7.3 %fusion.11 = f32[384,384]{1,0:T(8,128)} fusion(bf16[8,4,192,384]{3,2,1,0:T(8,128)(2,1)} %all-to-all-done, f32[8,192]{1,0:T(8,128)S(1)} %bitcast.91), kind=kOutput, calls=%fused_computation.18 | convolution fusion | flops 1819017216 | bytes 5314560 | tf_op jit(solution)/shard_map/dressing/dot_general | solution.py:98
  144.4 5.3 %fusion.10 = bf16[4,1,384,384]{2,3,0,1:T(8,128)(2,1)S(1)} fusion(bf16[8,4,192,384]{3,2,1,0:T(8,128)(2,1)} %all-to-all-done, bf16[8,128,384]{2,1,0:T(8,128)(2,1)S(1)} %gather_fusion, pred[8]{0:T(512)(128)(4,1)S(1)} %compare_and_fusion.1, pred[8,8,192,128]{3,2,0,1:T(32,128)(4,1)S(1)} %fusion.3, s32[]{:T(128)S(6)} %select_n.102), kind=kOutput, calls=%fused_computation.17 | convolution fusion | flops 1964507136 | bytes 6881796 | tf_op jit(solution)/shard_map/rotated/ora,ogrb->gab/dot_general | solution.py:107
  149.7 1.5 copy.55
  151.2 31.7 %all-reduce.3.cloned.1.call-done = f32[384,384]{1,0:T(8,128)} async-done(((f32[384,384]{1,0:T(8,128)}), f32[384,384]{1,0:T(8,128)}) %all-reduce.3.cloned.1.call-update) | async-done | bytes 589840 | tf_op jit(solution)/shard_map/dressing/psum | solution.py:104
  182.9 1.8 fusion.23
  (34 shorter events, 0.7 us)
Async XLA Ops:
  7.2 57.5 %all-gather.2.cloned.1.call-start = ((), (), s32[]{:S(2)}) async-start(), calls=%async_computation.1 | async-start | bytes 7133184 | tf_op jit(solution)/shard_map/all_gather | solution.py:65
  14.9 2.0 %copy-start = (bf16[4,192,1536]{2,1,0:T(8,128)(2,1)S(1)}, bf16[4,192,1536]{2,1,0:T(8,128)(2,1)}, u32[]{:S(2)}) copy-start(bf16[4,192,1536]{2,1,0:T(8,128)(2,1)} %param.6) | copy-start | bytes 7077892
  14.9 6.6 %copy-start.1 = (s32[8,8]{1,0:T(8,128)S(1)}, s32[8,8]{1,0:T(8,128)}, u32[]{:S(2)}) copy-start(s32[8,8]{1,0:T(8,128)} %param.10) | copy-start | bytes 772
  77.7 59.3 %all-to-all-start = ((bf16[8,4,192,384]{3,2,1,0:T(8,128)(2,1)}), bf16[8,4,192,384]{3,2,1,0:T(8,128)(2,1)}, u32[]{:S(2)}, u32[]{:S(2)}) async-start(bf16[8,4,192,384]{3,2,1,0:T(8,128)(2,1)} %bitcast.81), calls=%async_computation | async-start | bytes 9437184 | tf_op jit(solution)/shard_map/all_to_all | solution.py:92
  82.3 100.6 %all-reduce.3.cloned.1.call-start = ((), (), s32[]{:S(2)}) async-start(), calls=%async_computation.2 | async-start | bytes 1179648 | tf_op jit(solution)/shard_map/dressing/psum | solution.py:104
Sparse Core Ops, SparseCore 0:
  16.2 48.4 all-gather.1
  144.5 38.3 all-reduce.2

commit v10 on v8

--- a/solution.py
+++ b/solution.py
@@ -55,17 +55,20 @@
     pad_rows = -(-weight_rows // 8) * 8
     weight_parts = split_bf16(env_weight).reshape(-1)
     weight_parts = jnp.pad(weight_parts, (0, pad_rows * lno_width - weight_parts.shape[0]))
-    block_slots = orb_size * group_width
-    payload = jnp.concatenate(
-        [own_perm.reshape(1, block_slots, lno_width), weight_parts.reshape(1, pad_rows, lno_width)], axis=1
-    )
+    payload = jnp.concatenate([lno_coef, weight_parts.reshape(1, pad_rows, lno_width)], axis=1)
     gathered = lax.all_gather(payload, "orb", axis=0, tiled=True)
 
     with jax.named_scope("pick_columns"):
-        chol_blocks = chol_vec.reshape(chol_local * orb_rows, orb_size, orb_rows)
+        group_rows = groups - group_block[:, :, None] * orb_rows
+        group_hot = (
+            (group_rows[:, :, None, :] == row_ids[None, None, :, None])
+            & slot_ok.reshape(frag_total, group_count, group_width)[:, :, None, :]
+        ).astype(jnp.bfloat16)
+        chol_blocks = chol_vec.reshape(chol_local * orb_rows, orb_size, orb_rows).transpose(1, 0, 2)
+        chol_groups = jnp.take(chol_blocks, group_block, axis=0)
         picked = jnp.einsum(
-            "kor,forc->fkoc", chol_blocks, onehot, preferred_element_type=jnp.float32
-        ).astype(jnp.bfloat16).reshape(frag_total, chol_local * orb_rows, block_slots)
+            "fjkr,fjrc->fkjc", chol_groups, group_hot, preferred_element_type=jnp.float32
+        ).astype(jnp.bfloat16).reshape(frag_total, chol_local * orb_rows, slot_total)
 
     with jax.named_scope("own_placement"):
         own_hot = lax.dynamic_index_in_dim(onehot, my_index, 0, keepdims=False)
@@ -73,9 +76,9 @@
         own_w = jnp.einsum("orc,oca->ora", own_hot, own_perm, preferred_element_type=jnp.float32)
         own_w = jnp.where(own_cols[None, None, :], own_w, 0.0).astype(jnp.bfloat16)
 
-    all_coef = gathered[:, :block_slots]
+    all_coef = gathered[:, :slot_total]
     weight_all = join_bf16(
-        gathered[:, block_slots:]
+        gathered[:, slot_total:]
         .reshape(orb_size, -1)[:, : 3 * orb_rows]
         .reshape(orb_size, 3, orb_rows)
         .transpose(1, 0, 2)

time: 188 us -> 187 us (level)
  waiting for transfers between devices: 107 us -> 99.5 us
  local copies, waits for them, and re-layouts: 18.5 us -> 24.2 us
    gather x0 -> x1, local copies, waits for them, and re-layouts: none -> 8.39 us  [per_device(): chol_groups = jnp.take(chol_blocks, group_block, axis=0)]
    all_gather x1, waiting for transfers between devices: 25.3 us -> 18 us  [per_device(): gathered = lax.all_gather(payload, 'orb', axis=0, tiled=True)]
    convert_element_type x1 -> x0, local copies, waits for them, and re-layouts: 5.63 us -> none  [per_device(): picked = jnp.einsum('kor,forc->fkoc', chol_blocks, onehot, preferred_elem...]
    reshape x1 -> x2, local copies, waits for them, and re-layouts: 5.96 us -> 9.92 us  [per_device(): chol_vec.reshape(chol_local * orb_rows, orb_size, orb_rows)]
    all_to_all x1, waiting for transfers between devices: 51.9 us -> 49.7 us  [per_device(): lax.all_to_all(half, 'orb', split_axis=0, concat_axis=0, tiled=True)]
    psum x1, waiting for transfers between devices: 29.6 us -> 31.7 us  [per_device(): lax.psum(dressing_part, 'chol') * norm_factor]
    unnamed x12 -> x14, local copies, waits for them, and re-layouts: 4.16 us -> 3.18 us
  transfers between devices with their start and end apart: 3 -> 3, of which waited for: 3 -> 3; matrix products, arithmetic and copies ran while one was open for 18% -> 23% of each run, Pallas kernels for 0% -> 0%
where the time goes in v10:
time: 187 us; the launch traced here: 186 us
  waiting for transfers between devices  99.5 us (53%)
  matrix products  36.8 us (20%)
  local copies, waits for them, and re-layouts  24.2 us (13%)
  between operations  14.2 us (8%)
  other arithmetic  6.29 us (3%)
  starting transfers between devices  4.98 us (3%)
    all_to_all x1, waiting for transfers between devices, per_device(): lax.all_to_all(half, 'orb', split_axis=0, concat_axis=0, tiled=True)  49.7 us
    psum x1, waiting for transfers between devices, per_device(): lax.psum(dressing_part, 'chol') * norm_factor  31.7 us
    all_gather x1, waiting for transfers between devices, per_device(): gathered = lax.all_gather(payload, 'orb', axis=0, tiled=True)  18 us
    dot_general x1, matrix products, per_device(): jnp.einsum('fks,fsa->fka', picked, all_coef, preferred_element_type=jnp.f...  13 us
    dot_general x1, matrix products, per_device(): jnp.einsum('fjkr,fjrc->fkjc', chol_groups, group_hot, preferred_element_t...  11.1 us
    reshape x2, local copies, waits for them, and re-layouts, per_device(): chol_vec.reshape(chol_local * orb_rows, orb_size, orb_rows)  9.92 us
    gather x1, local copies, waits for them, and re-layouts, per_device(): chol_groups = jnp.take(chol_blocks, group_block, axis=0)  8.39 us
    dot_general x1, matrix products, per_device(): lax.dot_general(weighted.reshape(-1, lno_width), received.reshape(-1, lno...  7.31 us
  transfers between devices with their start and end apart: 3, of which 3 were waited for; matrix products, arithmetic and copies ran while one was open for 23% of the time, Pallas kernels for 0%

profile of v10, /device:TPU:0, one launch (start us, length us, event | category | flops | bytes accessed | tf_op | source)
XLA Modules:
  0.0 186.0 jit_solution(6924868726179283273)
XLA Ops:
  7.2 0.7 reduce-precision_convert_fusion.1
  7.9 0.1 convert_element_type.47
  8.0 2.1 %pad_maximum_fusion = bf16[1,1032,384]{2,1,0:T(8,128)(2,1)} fusion(bf16[1,8,384]{2,1,0:T(8,128)(2,1)S(1)} %reshape.189, bf16[1,1024,384]{2,1,0:T(8,128)(2,1)} %param.8), kind=kLoop, calls=%fused_computation.24 | loop fusion | flops 1585152 | bytes 1585152 | tf_op jit(solution)/shard_map/concatenate | solution.py:58
  10.2 0.8 copy.52
  10.9 0.1 copy.45
  11.1 0.1 reshape.195
  11.2 6.0 %reshape.187 = bf16[768,8,192]{2,1,0:T(8,128)(2,1)} reshape(bf16[4,192,1536]{2,1,0:T(8,128)(2,1)} %param.6) | data formatting | bytes 4718592 | tf_op jit(solution)/shard_map/pick_columns/reshape | solution.py:67
  17.1 4.0 %copy.38 = bf16[768,8,192]{0,2,1:T(8,128)(2,1)S(1)} copy(bf16[768,8,192]{2,1,0:T(8,128)(2,1)} %reshape.187) | data formatting | bytes 4718592 | tf_op jit(solution)/shard_map/pick_columns/reshape | solution.py:67
  21.2 8.4 %gather_fusion = bf16[64,768,192]{1,2,0:T(8,128)(2,1)} fusion(bf16[8,768,192]{1,2,0:T(8,128)(2,1)S(1)} %bitcast.76, s32[1024]{0:T(1024)S(1)} %pad_clamp_fusion.1), kind=kCustom, calls=%fused_computation | custom fusion | bytes 37748992 | tf_op jit(solution)/shard_map/pick_columns/jit(_take)/gather | solution.py:68
  29.6 0.1 broadcast_compare_fusion
  29.7 0.1 broadcast_subtract_fusion
  29.8 11.1 %fusion.5 = bf16[8,8,128,768]{3,2,1,0:T(8,128)(2,1)} fusion(bf16[8,8,768,192]{2,3,1,0:T(8,128)(2,1)} %bitcast.77, pred[8,8]{1,0:T(8,128)(4,1)S(1)} %get-tuple-element.18, s32[8,8,128]{2,1,0:T(8,128)S(1)} %broadcast_subtract_fusion, pred[8,8,128]{2,1,0:T(8,128)(4,1)S(1)} %broadcast_compare_fusion), kind=kOutput, calls=%fused_computation.11 | convolution fusion | flops 2434793472 | bytes 31498304 | tf_op jit(solution)/shard_map/pick_columns/fjkr,fjrc->fkjc/dot_general | solution.py:69
  40.9 18.0 %all-gather.2.cloned.1.call-done = bf16[8,1032,384]{2,1,0:T(8,128)(2,1)} async-done(((bf16[1,1032,384]{2,1,0:T(8,128)(2,1)}), bf16[8,1032,384]{2,1,0:T(8,128)(2,1)}) %all-gather.2.cloned.1.call-update) | async-done | bytes 6340624 | tf_op jit(solution)/shard_map/all_gather | solution.py:59
  58.9 13.0 %select_convert_fusion = bf16[8,768,384]{2,1,0:T(8,128)(2,1)} fusion(pred[8,384]{1,0:T(8,128)(4,1)S(1)} %iota_compare_fusion.3, bf16[8,768,1024]{1,2,0:T(8,128)(2,1)} %bitcast.87, bf16[8,1032,384]{2,1,0:T(8,128)(2,1)} %all-gather.2.cloned.1.call-done), kind=kOutput, calls=%fused_computation.8 | convolution fusion | flops 4836556800 | bytes 23596032 | tf_op jit(solution)/shard_map/half/fks,fsa->fka/dot_general | solution.py:88
  71.9 4.7 %all-to-all-start = ((bf16[8,4,192,384]{3,2,1,0:T(8,128)(2,1)}), bf16[8,4,192,384]{3,2,1,0:T(8,128)(2,1)}, u32[]{:S(2)}, u32[]{:S(2)}) async-start(bf16[8,4,192,384]{3,2,1,0:T(8,128)(2,1)} %bitcast.78), calls=%async_computation | async-start | bytes 9437184 | tf_op jit(solution)/shard_map/all_to_all | solution.py:92
  76.7 0.2 all-reduce.3.cloned.1.call-start
  76.9 0.9 iota_reduce_fusion
  77.8 0.1 reshape.209
  77.9 0.8 gather_fusion.3
  78.7 0.8 gather_fusion.2
  79.5 0.7 gather_fusion.1
  80.3 0.2 fusion.36
  80.5 0.1 fusion.37
  80.7 0.1 fusion.35
  80.8 0.8 slice_bitcast_fusion
  81.6 0.1 reshape.192
  81.7 49.7 %all-to-all-done = bf16[8,4,192,384]{3,2,1,0:T(8,128)(2,1)} async-done(((bf16[8,4,192,384]{3,2,1,0:T(8,128)(2,1)}), bf16[8,4,192,384]{3,2,1,0:T(8,128)(2,1)}, u32[]{:S(2)}, u32[]{:S(2)}) %all-to-all-start) | async-done | bytes 4718624 | tf_op jit(solution)/shard_map/all_to_all | solution.py:92
  131.4 7.3 %fusion.19 = f32[384,384]{1,0:T(8,128)} fusion(bf16[8,4,192,384]{3,2,1,0:T(8,128)(2,1)} %all-to-all-done, f32[8,192]{1,0:T(8,128)S(1)} %bitcast.86), kind=kOutput, calls=%fused_computation.23 | convolution fusion | flops 1819017216 | bytes 5314560 | tf_op jit(solution)/shard_map/dressing/dot_general | solution.py:98
  138.8 5.3 %fusion.18 = bf16[4,1,384,384]{2,3,0,1:T(8,128)(2,1)S(1)} fusion(bf16[8,4,192,384]{3,2,1,0:T(8,128)(2,1)} %all-to-all-done, pred[384]{0:T(512)(128)(4,1)S(1)} %dynamic-slice_reduce_fusion, bf16[8,128,384]{2,1,0:T(8,128)(2,1)S(1)} %gather_fusion.1, pred[8]{0:T(512)(128)(4,1)S(1)} %compare_and_fusion.1, s32[1,8,128]{2,1,0:T(8,128)S(1)} %constant_dynamic-slice_fusion, ...), kind=kOutput, calls=%fused_computation.22 | convolution fusion | flops 1965490176 | bytes 6690184 | tf_op jit(solution)/shard_map/rotated/ora,ogrb->gab/dot_general | solution.py:107
  144.1 1.5 copy.40
  145.6 31.7 %all-reduce.3.cloned.1.call-done = f32[384,384]{1,0:T(8,128)} async-done(((f32[384,384]{1,0:T(8,128)}), f32[384,384]{1,0:T(8,128)}) %all-reduce.3.cloned.1.call-update) | async-done | bytes 589840 | tf_op jit(solution)/shard_map/dressing/psum | solution.py:104
  177.3 1.8 fusion.34
  (36 shorter events, 0.4 us)
Async XLA Ops:
  7.2 51.8 %all-gather.2.cloned.1.call-start = ((), (), s32[]{:S(2)}) async-start(), calls=%async_computation.1 | async-start | bytes 7133184 | tf_op jit(solution)/shard_map/all_gather | solution.py:59
  21.1 8.4 %copy-start.3 = (s32[8]{0:T(128)S(1)}, s32[8]{0:T(128)}, u32[]{:S(2)}) copy-start(s32[8]{0:T(128)} %param.11) | copy-start | bytes 100
  21.1 8.5 %copy-start.2 = (s32[8,8]{1,0:T(8,128)S(1)}, s32[8,8]{1,0:T(8,128)}, u32[]{:S(2)}) copy-start(s32[8,8]{1,0:T(8,128)} %param.10) | copy-start | bytes 772
  21.1 8.6 %copy-start.1 = (s32[8,1024]{1,0:T(8,128)S(1)}, s32[8,1024]{1,0:T(8,128)}, u32[]{:S(2)}) copy-start(s32[8,1024]{1,0:T(8,128)} %param.9) | copy-start | bytes 98308
  71.9 7.6 %copy-start = (bf16[1,1024,384]{2,1,0:T(8,128)(2,1)S(1)}, bf16[1,1024,384]{2,1,0:T(8,128)(2,1)}, u32[]{:S(2)}) copy-start(bf16[1,1024,384]{2,1,0:T(8,128)(2,1)} %param.8) | copy-start | bytes 2359300
  71.9 59.5 %all-to-all-start = ((bf16[8,4,192,384]{3,2,1,0:T(8,128)(2,1)}), bf16[8,4,192,384]{3,2,1,0:T(8,128)(2,1)}, u32[]{:S(2)}, u32[]{:S(2)}) async-start(bf16[8,4,192,384]{3,2,1,0:T(8,128)(2,1)} %bitcast.78), calls=%async_computation | async-start | bytes 9437184 | tf_op jit(solution)/shard_map/all_to_all | solution.py:92
  76.7 100.6 %all-reduce.3.cloned.1.call-start = ((), (), s32[]{:S(2)}) async-start(), calls=%async_computation.2 | async-start | bytes 1179648 | tf_op jit(solution)/shard_map/dressing/psum | solution.py:104
Sparse Core Ops, SparseCore 0:
  10.5 48.4 all-gather.1
  138.9 38.3 all-reduce.2

commit v11 on v10

--- a/solution.py
+++ b/solution.py
@@ -85,27 +85,24 @@
     )
 
     with jax.named_scope("half"):
-        half = jnp.einsum("fks,fsa->fka", picked, all_coef, preferred_element_type=jnp.float32)
-        half = jnp.where(column_ok[:, None, :], half, 0.0).astype(jnp.bfloat16)
-        half = half.reshape(frag_total, chol_local, orb_rows, lno_width)
+        half = jnp.einsum("fsa,fks->fak", all_coef, picked, preferred_element_type=jnp.float32)
+        half = jnp.where(column_ok[:, :, None], half, 0.0).astype(jnp.bfloat16)
+        half = half.reshape(frag_total, lno_width, chol_local, orb_rows)
 
     received = lax.all_to_all(half, "orb", split_axis=0, concat_axis=0, tiled=True)
 
     with jax.named_scope("dressing"):
         weighted = (
-            received.astype(jnp.float32) * weight_all.reshape(orb_size, 1, orb_rows, 1)
+            received.astype(jnp.float32) * weight_all.reshape(orb_size, 1, 1, orb_rows)
         ).astype(jnp.bfloat16)
-        dressing_part = lax.dot_general(
-            weighted.reshape(-1, lno_width),
-            received.reshape(-1, lno_width),
-            (((0,), (0,)), ((), ())),
-            preferred_element_type=jnp.float32,
+        dressing_part = jnp.einsum(
+            "oagr,obgr->ab", weighted, received, preferred_element_type=jnp.float32
         )
         dressing = (lax.psum(dressing_part, "chol") * norm_factor).astype(jnp.bfloat16)
 
     with jax.named_scope("rotated"):
         rotated = jnp.einsum(
-            "ora,ogrb->gab", own_w, received, preferred_element_type=jnp.float32
+            "ora,obgr->gab", own_w, received, preferred_element_type=jnp.float32
         ).astype(jnp.bfloat16)[:, None]
     return (rotated, dressing[None])
 

time: 187 us -> 194 us (1.037)
  local copies, waits for them, and re-layouts: 24.2 us -> 30.8 us
    convert_element_type x0 -> x1, local copies, waits for them, and re-layouts: none -> 6.62 us  [per_device(): half = jnp.where(column_ok[:, :, None], half, 0.0).astype(jnp.bfloat16)]
  transfers between devices with their start and end apart: 3 -> 3, of which waited for: 3 -> 3; matrix products, arithmetic and copies ran while one was open for 23% -> 22% of each run, Pallas kernels for 0% -> 0%
where the time goes in v11:
time: 194 us; the launch traced here: 193 us
  waiting for transfers between devices  99.3 us (51%)
  matrix products  37.7 us (19%)
  local copies, waits for them, and re-layouts  30.8 us (16%)
  between operations  14.2 us (7%)
  other arithmetic  6.29 us (3%)
  starting transfers between devices  4.98 us (3%)
    all_to_all x1, waiting for transfers between devices, per_device(): lax.all_to_all(half, 'orb', split_axis=0, concat_axis=0, tiled=True)  49.7 us
    psum x1, waiting for transfers between devices, per_device(): lax.psum(dressing_part, 'chol') * norm_factor  31.6 us
    all_gather x1, waiting for transfers between devices, per_device(): gathered = lax.all_gather(payload, 'orb', axis=0, tiled=True)  18 us
    dot_general x1, matrix products, per_device(): jnp.einsum('fsa,fks->fak', all_coef, picked, preferred_element_type=jnp.f...  13.7 us
    dot_general x1, matrix products, per_device(): jnp.einsum('fjkr,fjrc->fkjc', chol_groups, group_hot, preferred_element_t...  11.1 us
    reshape x2, local copies, waits for them, and re-layouts, per_device(): chol_vec.reshape(chol_local * orb_rows, orb_size, orb_rows)  9.92 us
    gather x1, local copies, waits for them, and re-layouts, per_device(): chol_groups = jnp.take(chol_blocks, group_block, axis=0)  8.37 us
    dot_general x1, matrix products, per_device(): jnp.einsum('oagr,obgr->ab', weighted, received, preferred_element_type=jn...  7.56 us
  transfers between devices with their start and end apart: 3, of which 3 were waited for; matrix products, arithmetic and copies ran while one was open for 22% of the time, Pallas kernels for 0%

profile of v11, /device:TPU:0, one launch (start us, length us, event | category | flops | bytes accessed | tf_op | source)
XLA Modules:
  0.0 193.4 jit_solution(15499382055758327264)
XLA Ops:
  7.2 0.7 reduce-precision_convert_fusion.1
  7.9 0.1 convert_element_type.45
  8.0 2.1 %pad_maximum_fusion = bf16[1,1032,384]{2,1,0:T(8,128)(2,1)} fusion(bf16[1,8,384]{2,1,0:T(8,128)(2,1)S(1)} %reshape.188, bf16[1,1024,384]{2,1,0:T(8,128)(2,1)} %param.8), kind=kLoop, calls=%fused_computation.25 | loop fusion | flops 1585152 | bytes 1585152 | tf_op jit(solution)/shard_map/concatenate | solution.py:58
  10.2 0.8 copy.77
  10.9 0.1 copy.62
  11.1 0.1 reshape.197
  11.2 6.0 %reshape.190 = bf16[768,8,192]{2,1,0:T(8,128)(2,1)} reshape(bf16[4,192,1536]{2,1,0:T(8,128)(2,1)} %param.6) | data formatting | bytes 4718592 | tf_op jit(solution)/shard_map/pick_columns/reshape | solution.py:67
  17.1 4.0 %copy.51 = bf16[768,8,192]{0,2,1:T(8,128)(2,1)S(1)} copy(bf16[768,8,192]{2,1,0:T(8,128)(2,1)} %reshape.190) | data formatting | bytes 4718592 | tf_op jit(solution)/shard_map/pick_columns/reshape | solution.py:67
  21.2 8.4 %gather_fusion = bf16[64,768,192]{1,2,0:T(8,128)(2,1)} fusion(bf16[8,768,192]{1,2,0:T(8,128)(2,1)S(1)} %bitcast.75, s32[1024]{0:T(1024)S(1)} %pad_clamp_fusion.1), kind=kCustom, calls=%fused_computation | custom fusion | bytes 37748992 | tf_op jit(solution)/shard_map/pick_columns/jit(_take)/gather | solution.py:68
  29.7 0.1 broadcast_subtract_fusion
  29.8 11.1 %fusion.4 = bf16[8,8,128,768]{3,2,1,0:T(8,128)(2,1)} fusion(bf16[8,8,768,192]{2,3,1,0:T(8,128)(2,1)} %bitcast.76, pred[8,8]{1,0:T(8,128)(4,1)S(1)} %get-tuple-element.18, s32[8,8,128]{2,1,0:T(8,128)S(1)} %broadcast_subtract_fusion, pred[8,8,128]{2,1,0:T(8,128)(4,1)S(1)} %broadcast_compare_fusion), kind=kOutput, calls=%fused_computation.10 | convolution fusion | flops 2434793472 | bytes 31498304 | tf_op jit(solution)/shard_map/pick_columns/fjkr,fjrc->fkjc/dot_general | solution.py:69
  40.9 18.0 %all-gather.2.cloned.1.call-done = bf16[8,1032,384]{2,1,0:T(8,128)(2,1)} async-done(((bf16[1,1032,384]{2,1,0:T(8,128)(2,1)}), bf16[8,1032,384]{2,1,0:T(8,128)(2,1)}) %all-gather.2.cloned.1.call-update) | async-done | bytes 6340624 | tf_op jit(solution)/shard_map/all_gather | solution.py:59
  58.9 13.7 %select_convert_fusion = bf16[8,384,768]{2,1,0:T(8,128)(2,1)} fusion(pred[8,384]{1,0:T(8,128)(4,1)S(1)} %iota_compare_fusion.3, bf16[8,768,1024]{1,2,0:T(8,128)(2,1)} %bitcast.86, bf16[8,1032,384]{2,1,0:T(8,128)(2,1)} %all-gather.2.cloned.1.call-done), kind=kOutput, calls=%fused_computation.8 | convolution fusion | flops 4836556800 | bytes 23596032 | tf_op jit(solution)/shard_map/half/fsa,fks->fak/dot_general | solution.py:88
  72.7 6.6 %copy.53 = bf16[8,384,768]{1,2,0:T(8,128)(2,1)} copy(bf16[8,384,768]{2,1,0:T(8,128)(2,1)} %select_convert_fusion) | data formatting | bytes 9437184 | tf_op jit(solution)/shard_map/half/convert_element_type | solution.py:89
  79.3 4.7 %all-to-all-start = ((bf16[8,384,4,192]{1,3,2,0:T(8,128)(2,1)}), bf16[8,384,4,192]{1,3,2,0:T(8,128)(2,1)}, u32[]{:S(2)}, u32[]{:S(2)}) async-start(bf16[8,384,4,192]{1,3,2,0:T(8,128)(2,1)} %bitcast.77), calls=%async_computation | async-start | bytes 9437184 | tf_op jit(solution)/shard_map/all_to_all | solution.py:92
  84.0 0.2 all-reduce.3.cloned.1.call-start
  84.2 0.9 iota_reduce_fusion
  85.2 0.1 reshape.211
  85.3 0.8 gather_fusion.3
  86.1 0.8 gather_fusion.2
  86.9 0.7 gather_fusion.1
  87.6 0.2 fusion.41
  87.9 0.1 fusion.42
  88.0 0.1 fusion.40
  88.1 0.8 slice_bitcast_fusion
  88.9 0.1 reshape.194
  89.0 49.7 %all-to-all-done = bf16[8,384,4,192]{1,3,2,0:T(8,128)(2,1)} async-done(((bf16[8,384,4,192]{1,3,2,0:T(8,128)(2,1)}), bf16[8,384,4,192]{1,3,2,0:T(8,128)(2,1)}, u32[]{:S(2)}, u32[]{:S(2)}) %all-to-all-start) | async-done | bytes 4718624 | tf_op jit(solution)/shard_map/all_to_all | solution.py:92
  138.7 7.6 %fusion.20 = f32[384,384]{1,0:T(8,128)} fusion(bf16[8,384,4,192]{1,3,2,0:T(8,128)(2,1)} %all-to-all-done, f32[8,192]{1,0:T(8,128)S(1)} %bitcast.85), kind=kOutput, calls=%fused_computation.24 | convolution fusion | flops 1819017216 | bytes 5314560 | tf_op jit(solution)/shard_map/dressing/oagr,obgr->ab/dot_general | solution.py:98
  146.3 5.3 %fusion.19 = bf16[4,1,384,384]{2,3,0,1:T(8,128)(2,1)S(1)} fusion(bf16[8,384,4,192]{1,3,2,0:T(8,128)(2,1)} %all-to-all-done, pred[384]{0:T(512)(128)(4,1)S(1)} %dynamic-slice_reduce_fusion, bf16[8,128,384]{2,1,0:T(8,128)(2,1)S(1)} %gather_fusion.1, pred[8]{0:T(512)(128)(4,1)S(1)} %compare_and_fusion.1, s32[1,8,128]{2,1,0:T(8,128)S(1)} %constant_dynamic-slice_fusion, ...), kind=kOutput, calls=%fused_computation.23 | convolution fusion | flops 1965490176 | bytes 6690184 | tf_op jit(solution)/shard_map/rotated/ora,obgr->gab/dot_general | solution.py:104
  151.7 1.5 copy.56
  153.1 31.6 %all-reduce.3.cloned.1.call-done = f32[384,384]{1,0:T(8,128)} async-done(((f32[384,384]{1,0:T(8,128)}), f32[384,384]{1,0:T(8,128)}) %all-reduce.3.cloned.1.call-update) | async-done | bytes 589840 | tf_op jit(solution)/shard_map/dressing/psum | solution.py:101
  184.7 1.8 fusion.39
  (37 shorter events, 0.5 us)
Async XLA Ops:
  7.2 51.8 %all-gather.2.cloned.1.call-start = ((), (), s32[]{:S(2)}) async-start(), calls=%async_computation.1 | async-start | bytes 7133184 | tf_op jit(solution)/shard_map/all_gather | solution.py:59
  21.1 8.4 %copy-start.3 = (s32[8]{0:T(128)S(1)}, s32[8]{0:T(128)}, u32[]{:S(2)}) copy-start(s32[8]{0:T(128)} %param.11) | copy-start | bytes 100
  21.1 8.5 %copy-start.2 = (s32[8,8]{1,0:T(8,128)S(1)}, s32[8,8]{1,0:T(8,128)}, u32[]{:S(2)}) copy-start(s32[8,8]{1,0:T(8,128)} %param.10) | copy-start | bytes 772
  21.1 8.6 %copy-start.1 = (s32[8,1024]{1,0:T(8,128)S(1)}, s32[8,1024]{1,0:T(8,128)}, u32[]{:S(2)}) copy-start(s32[8,1024]{1,0:T(8,128)} %param.9) | copy-start | bytes 98308
  79.3 7.6 %copy-start = (bf16[1,1024,384]{2,1,0:T(8,128)(2,1)S(1)}, bf16[1,1024,384]{2,1,0:T(8,128)(2,1)}, u32[]{:S(2)}) copy-start(bf16[1,1024,384]{2,1,0:T(8,128)(2,1)} %param.8) | copy-start | bytes 2359300
  79.3 59.5 %all-to-all-start = ((bf16[8,384,4,192]{1,3,2,0:T(8,128)(2,1)}), bf16[8,384,4,192]{1,3,2,0:T(8,128)(2,1)}, u32[]{:S(2)}, u32[]{:S(2)}) async-start(bf16[8,384,4,192]{1,3,2,0:T(8,128)(2,1)} %bitcast.77), calls=%async_computation | async-start | bytes 9437184 | tf_op jit(solution)/shard_map/all_to_all | solution.py:92
  84.0 100.7 %all-reduce.3.cloned.1.call-start = ((), (), s32[]{:S(2)}) async-start(), calls=%async_computation.2 | async-start | bytes 1179648 | tf_op jit(solution)/shard_map/dressing/psum | solution.py:101
Sparse Core Ops, SparseCore 0:
  10.5 48.4 all-gather.1
  146.5 38.1 all-reduce.2

commit v12 on v10

--- a/solution.py
+++ b/solution.py
@@ -51,12 +51,7 @@
 
     own_pick = lax.dynamic_index_in_dim(group_of_block, my_index, 0, keepdims=False)
     own_perm = jnp.take(lno_coef[0].reshape(group_count, group_width, lno_width), own_pick, axis=0)
-    weight_rows = -(-3 * orb_rows // lno_width)
-    pad_rows = -(-weight_rows // 8) * 8
-    weight_parts = split_bf16(env_weight).reshape(-1)
-    weight_parts = jnp.pad(weight_parts, (0, pad_rows * lno_width - weight_parts.shape[0]))
-    payload = jnp.concatenate([lno_coef, weight_parts.reshape(1, pad_rows, lno_width)], axis=1)
-    gathered = lax.all_gather(payload, "orb", axis=0, tiled=True)
+    all_coef = lax.all_gather(lno_coef, "orb", axis=0, tiled=True)
 
     with jax.named_scope("pick_columns"):
         group_rows = groups - group_block[:, :, None] * orb_rows
@@ -76,13 +71,8 @@
         own_w = jnp.einsum("orc,oca->ora", own_hot, own_perm, preferred_element_type=jnp.float32)
         own_w = jnp.where(own_cols[None, None, :], own_w, 0.0).astype(jnp.bfloat16)
 
-    all_coef = gathered[:, :slot_total]
-    weight_all = join_bf16(
-        gathered[:, slot_total:]
-        .reshape(orb_size, -1)[:, : 3 * orb_rows]
-        .reshape(orb_size, 3, orb_rows)
-        .transpose(1, 0, 2)
-    )
+    weight_all = lax.all_gather(env_weight, "orb", axis=0, tiled=False)
+    weight_all, picked = lax.optimization_barrier((weight_all, picked))
 
     with jax.named_scope("half"):
         half = jnp.einsum("fks,fsa->fka", picked, all_coef, preferred_element_type=jnp.float32)

time: 187 us -> 186 us (level)
  blocking collectives: 0 us -> 15.8 us
  waiting for transfers between devices: 99.5 us -> 85.1 us
  other arithmetic: 6.29 us -> 3.47 us
    all_gather x1, waiting for transfers between devices: 18 us -> 2.14 us  [per_device(): all_coef = lax.all_gather(lno_coef, 'orb', axis=0, tiled=True)]
    unnamed x0 -> x1, blocking collectives: none -> 15.8 us
    concatenate x1 -> x0, other arithmetic: 2.1 us -> none  [per_device(): jnp.concatenate([lno_coef, weight_parts.reshape(1, pad_rows, lno_width)],...]
where the time goes in v12:
time: 186 us; the launch traced here: 185 us
  waiting for transfers between devices  85.1 us (46%)
  matrix products  36.9 us (20%)
  local copies, waits for them, and re-layouts  24.1 us (13%)
  blocking collectives  15.8 us (8%)
  between operations  14.9 us (8%)
  starting transfers between devices  4.98 us (3%)
  other arithmetic  3.47 us (2%)
    all_to_all x1, waiting for transfers between devices, per_device(): lax.all_to_all(half, 'orb', split_axis=0, concat_axis=0, tiled=True)  50.7 us
    psum x1, waiting for transfers between devices, per_device(): lax.psum(dressing_part, 'chol') * norm_factor  31.6 us
    unnamed x1, blocking collectives  15.8 us
    dot_general x1, matrix products, per_device(): jnp.einsum('fks,fsa->fka', picked, all_coef, preferred_element_type=jnp.f...  13.1 us
    dot_general x1, matrix products, per_device(): jnp.einsum('fjkr,fjrc->fkjc', chol_groups, group_hot, preferred_element_t...  11.2 us
    reshape x2, local copies, waits for them, and re-layouts, per_device(): chol_vec.reshape(chol_local * orb_rows, orb_size, orb_rows)  9.88 us
    gather x1, local copies, waits for them, and re-layouts, per_device(): chol_groups = jnp.take(chol_blocks, group_block, axis=0)  8.43 us
    dot_general x1, matrix products, per_device(): lax.dot_general(weighted.reshape(-1, lno_width), received.reshape(-1, lno...  7.31 us
  transfers between devices with their start and end apart: 3, of which 3 were waited for; matrix products, arithmetic and copies ran while one was open for 23% of the time, Pallas kernels for 0%

profile of v12, /device:TPU:0, one launch (start us, length us, event | category | flops | bytes accessed | tf_op | source)
XLA Modules:
  0.0 185.2 jit_solution(1169127164824110483)
XLA Ops:
  7.2 0.7 all-gather.3.cloned.1.call-update
  7.9 0.8 copy.48
  8.7 0.1 copy.43
  8.8 0.1 reshape.165
  8.9 6.0 %reshape.160 = bf16[768,8,192]{2,1,0:T(8,128)(2,1)} reshape(bf16[4,192,1536]{2,1,0:T(8,128)(2,1)} %param.6) | data formatting | bytes 4718592 | tf_op jit(solution)/shard_map/pick_columns/reshape | solution.py:62
  14.9 3.9 %copy.37 = bf16[768,8,192]{0,2,1:T(8,128)(2,1)S(1)} copy(bf16[768,8,192]{2,1,0:T(8,128)(2,1)} %reshape.160) | data formatting | bytes 4718592 | tf_op jit(solution)/shard_map/pick_columns/reshape | solution.py:62
  18.8 0.6 dynamic-slice
  20.1 0.3 dynamic-update-slice
  20.4 15.8 %all-reduce = f32[1536]{0:T(1024)S(1)} all-reduce(f32[1536]{0:T(1024)S(1)} %dynamic-update-slice), channel_id=2, replica_groups=mesh['chol'=4,'orb'=8] {'orb'}, use_global_device_ids=true, to_apply=%add | all-reduce | flops 1536 | bytes 12288
  36.2 8.4 %gather_fusion = bf16[64,768,192]{1,2,0:T(8,128)(2,1)} fusion(bf16[8,768,192]{1,2,0:T(8,128)(2,1)S(1)} %bitcast.71, s32[1024]{0:T(1024)S(1)} %pad_clamp_fusion.1), kind=kCustom, calls=%fused_computation | custom fusion | bytes 37748992 | tf_op jit(solution)/shard_map/pick_columns/jit(_take)/gather | solution.py:63
  44.7 0.1 broadcast_compare_fusion
  44.8 0.1 broadcast_subtract_fusion
  44.9 11.2 %fusion.5 = bf16[8,8,128,768]{3,2,1,0:T(8,128)(2,1)} fusion(bf16[8,8,768,192]{2,3,1,0:T(8,128)(2,1)} %bitcast.72, pred[8,8]{1,0:T(8,128)(4,1)S(1)} %get-tuple-element.22, s32[8,8,128]{2,1,0:T(8,128)S(1)} %broadcast_subtract_fusion, pred[8,8,128]{2,1,0:T(8,128)(4,1)S(1)} %broadcast_compare_fusion), kind=kOutput, calls=%fused_computation.11 | convolution fusion | flops 2434793472 | bytes 31498304 | tf_op jit(solution)/shard_map/pick_columns/fjkr,fjrc->fkjc/dot_general | solution.py:64
  56.1 0.1 iota_compare_fusion.3
  56.2 2.1 %all-gather.3.cloned.1.call-done = bf16[8,1024,384]{2,1,0:T(8,128)(2,1)} async-done(((bf16[1,1024,384]{2,1,0:T(8,128)(2,1)}), bf16[8,1024,384]{2,1,0:T(8,128)(2,1)}) %all-gather.3.cloned.1.call-update) | async-done | bytes 6291472 | tf_op jit(solution)/shard_map/all_gather | solution.py:54
  58.3 13.1 %select_convert_fusion = bf16[8,768,384]{2,1,0:T(8,128)(2,1)} fusion(pred[8,384]{1,0:T(8,128)(4,1)S(1)} %iota_compare_fusion.3, bf16[8,768,1024]{1,2,0:T(8,128)(2,1)} %bitcast.79, bf16[8,1024,384]{2,1,0:T(8,128)(2,1)} %all-gather.3.cloned.1.call-done), kind=kOutput, calls=%fused_computation.8 | convolution fusion | flops 4836556800 | bytes 23596032 | tf_op jit(solution)/shard_map/half/fks,fsa->fka/dot_general | solution.py:78
  71.4 4.7 %all-to-all-start = ((bf16[8,4,192,384]{3,2,1,0:T(8,128)(2,1)}), bf16[8,4,192,384]{3,2,1,0:T(8,128)(2,1)}, u32[]{:S(2)}, u32[]{:S(2)}) async-start(bf16[8,4,192,384]{3,2,1,0:T(8,128)(2,1)} %bitcast.73), calls=%async_computation | async-start | bytes 9437184 | tf_op jit(solution)/shard_map/all_to_all | solution.py:82
  76.1 0.2 all-reduce.3.cloned.1.call-start
  76.3 0.9 iota_reduce_fusion
  77.3 0.1 reshape.179
  77.3 0.8 gather_fusion.3
  78.2 0.8 gather_fusion.2
  79.0 0.7 gather_fusion.1
  79.7 0.2 fusion.32
  80.0 0.1 fusion.33
  80.1 0.1 fusion.31
  80.2 50.7 %all-to-all-done = bf16[8,4,192,384]{3,2,1,0:T(8,128)(2,1)} async-done(((bf16[8,4,192,384]{3,2,1,0:T(8,128)(2,1)}), bf16[8,4,192,384]{3,2,1,0:T(8,128)(2,1)}, u32[]{:S(2)}, u32[]{:S(2)}) %all-to-all-start) | async-done | bytes 4718624 | tf_op jit(solution)/shard_map/all_to_all | solution.py:82
  130.8 7.3 %fusion.15 = f32[384,384]{1,0:T(8,128)} fusion(bf16[8,4,192,384]{3,2,1,0:T(8,128)(2,1)} %all-to-all-done, f32[8,192]{1,0:T(8,128)S(1)} %reshape.191), kind=kOutput, calls=%fused_computation.21 | convolution fusion | flops 1819017216 | bytes 5314560 | tf_op jit(solution)/shard_map/dressing/dot_general | solution.py:88
  138.2 5.3 %fusion.14 = bf16[4,1,384,384]{2,3,0,1:T(8,128)(2,1)S(1)} fusion(bf16[8,4,192,384]{3,2,1,0:T(8,128)(2,1)} %all-to-all-done, pred[384]{0:T(512)(128)(4,1)S(1)} %dynamic-slice_reduce_fusion, bf16[8,128,384]{2,1,0:T(8,128)(2,1)S(1)} %gather_fusion.1, pred[8]{0:T(512)(128)(4,1)S(1)} %compare_and_fusion.1, s32[1,8,128]{2,1,0:T(8,128)S(1)} %constant_dynamic-slice_fusion, ...), kind=kOutput, calls=%fused_computation.20 | convolution fusion | flops 1965490176 | bytes 6690184 | tf_op jit(solution)/shard_map/rotated/ora,ogrb->gab/dot_general | solution.py:97
  143.5 1.5 copy.39
  145.0 31.6 %all-reduce.3.cloned.1.call-done = f32[384,384]{1,0:T(8,128)} async-done(((f32[384,384]{1,0:T(8,128)}), f32[384,384]{1,0:T(8,128)}) %all-reduce.3.cloned.1.call-update) | async-done | bytes 589840 | tf_op jit(solution)/shard_map/dressing/psum | solution.py:94
  176.5 1.8 fusion.30
  (30 shorter events, 0.3 us)
Async XLA Ops:
  7.2 51.2 %all-gather.3.cloned.1.call-start = ((), (), s32[]{:S(2)}) async-start(), calls=%async_computation.1 | async-start | bytes 7077888 | tf_op jit(solution)/shard_map/all_gather | solution.py:54
  8.9 9.9 %copy-start.5 = (u32[32]{0:T(128)S(1)}, u32[32]{0:T(128)}, u32[]{:S(2)}) copy-start(u32[32]{0:T(128)} %constant.133) | copy-start | bytes 388
  8.9 11.2 %copy-start.3 = (f32[192]{0:T(256)S(1)}, f32[192]{0:T(256)}, u32[]{:S(2)}) copy-start(f32[192]{0:T(256)} %param.7) | copy-start | bytes 2308
  36.2 8.5 %copy-start.2 = (s32[8,8]{1,0:T(8,128)S(1)}, s32[8,8]{1,0:T(8,128)}, u32[]{:S(2)}) copy-start(s32[8,8]{1,0:T(8,128)} %param.10) | copy-start | bytes 772
  36.2 8.5 %copy-start.1 = (s32[8,1024]{1,0:T(8,128)S(1)}, s32[8,1024]{1,0:T(8,128)}, u32[]{:S(2)}) copy-start(s32[8,1024]{1,0:T(8,128)} %param.9) | copy-start | bytes 98308
  44.9 11.2 %copy-start.4 = (s32[8]{0:T(128)S(1)}, s32[8]{0:T(128)}, u32[]{:S(2)}) copy-start(s32[8]{0:T(128)} %param.11) | copy-start | bytes 100
  71.4 7.6 %copy-start = (bf16[1,1024,384]{2,1,0:T(8,128)(2,1)S(1)}, bf16[1,1024,384]{2,1,0:T(8,128)(2,1)}, u32[]{:S(2)}) copy-start(bf16[1,1024,384]{2,1,0:T(8,128)(2,1)} %param.8) | copy-start | bytes 2359300
  71.4 59.5 %all-to-all-start = ((bf16[8,4,192,384]{3,2,1,0:T(8,128)(2,1)}), bf16[8,4,192,384]{3,2,1,0:T(8,128)(2,1)}, u32[]{:S(2)}, u32[]{:S(2)}) async-start(bf16[8,4,192,384]{3,2,1,0:T(8,128)(2,1)} %bitcast.73), calls=%async_computation | async-start | bytes 9437184 | tf_op jit(solution)/shard_map/all_to_all | solution.py:82
  76.1 100.4 %all-reduce.3.cloned.1.call-start = ((), (), s32[]{:S(2)}) async-start(), calls=%async_computation.2 | async-start | bytes 1179648 | tf_op jit(solution)/shard_map/dressing/psum | solution.py:94
Sparse Core Ops, SparseCore 0:
  9.9 48.3 all-gather.2
  138.3 38.2 all-reduce.2

commit v13 on v12

--- a/solution.py
+++ b/solution.py
@@ -3,7 +3,10 @@
 import jax
 import jax.numpy as jnp
 from jax import lax
-from jax.sharding import PartitionSpec as P
+from jax.sharding import Mesh, PartitionSpec as P
+import numpy as np
+
+ORB = ("orb_hi", "orb_lo")
 
 
 def split_bf16(x):
@@ -26,8 +29,12 @@
     group_width = slot_total // group_count
     lno_width = lno_coef.shape[2]
     chol_size = lax.axis_size("chol")
-    orb_size = lax.axis_size("orb")
-    my_index = lax.axis_index("orb")
+    hi_size = lax.axis_size("orb_hi")
+    lo_size = lax.axis_size("orb_lo")
+    orb_size = hi_size * lo_size
+    my_index = lax.axis_index("orb_hi") * lo_size + lax.axis_index("orb_lo")
+    positions = np.arange(orb_size)
+    frag_of_pos = (positions % hi_size) * lo_size + positions // hi_size
     norm_factor = 1.0 / math.sqrt(chol_local * chol_size * orb_total)
 
     slot_index = jnp.arange(slot_total, dtype=jnp.int32)
@@ -51,16 +58,19 @@
 
     own_pick = lax.dynamic_index_in_dim(group_of_block, my_index, 0, keepdims=False)
     own_perm = jnp.take(lno_coef[0].reshape(group_count, group_width, lno_width), own_pick, axis=0)
-    all_coef = lax.all_gather(lno_coef, "orb", axis=0, tiled=True)
+    across = lax.all_gather(lno_coef, "orb_hi", axis=0, tiled=True)
+    all_coef = lax.all_gather(across, "orb_lo", axis=0, tiled=True)
 
     with jax.named_scope("pick_columns"):
-        group_rows = groups - group_block[:, :, None] * orb_rows
+        groups_p = groups[frag_of_pos]
+        block_p = group_block[frag_of_pos]
+        group_rows = groups_p - block_p[:, :, None] * orb_rows
         group_hot = (
             (group_rows[:, :, None, :] == row_ids[None, None, :, None])
-            & slot_ok.reshape(frag_total, group_count, group_width)[:, :, None, :]
+            & slot_ok.reshape(frag_total, group_count, group_width)[frag_of_pos][:, :, None, :]
         ).astype(jnp.bfloat16)
         chol_blocks = chol_vec.reshape(chol_local * orb_rows, orb_size, orb_rows).transpose(1, 0, 2)
-        chol_groups = jnp.take(chol_blocks, group_block, axis=0)
+        chol_groups = jnp.take(chol_blocks, block_p, axis=0)
         picked = jnp.einsum(
             "fjkr,fjrc->fkjc", chol_groups, group_hot, preferred_element_type=jnp.float32
         ).astype(jnp.bfloat16).reshape(frag_total, chol_local * orb_rows, slot_total)
@@ -69,17 +79,17 @@
         own_hot = lax.dynamic_index_in_dim(onehot, my_index, 0, keepdims=False)
         own_cols = lax.dynamic_index_in_dim(column_ok, my_index, 0, keepdims=False)
         own_w = jnp.einsum("orc,oca->ora", own_hot, own_perm, preferred_element_type=jnp.float32)
-        own_w = jnp.where(own_cols[None, None, :], own_w, 0.0).astype(jnp.bfloat16)
+        own_w = jnp.where(own_cols[None, None, :], own_w, 0.0).astype(jnp.bfloat16)[frag_of_pos]
 
-    weight_all = lax.all_gather(env_weight, "orb", axis=0, tiled=False)
+    weight_all = lax.all_gather(env_weight, ("orb_lo", "orb_hi"), axis=0, tiled=False)
     weight_all, picked = lax.optimization_barrier((weight_all, picked))
 
     with jax.named_scope("half"):
         half = jnp.einsum("fks,fsa->fka", picked, all_coef, preferred_element_type=jnp.float32)
-        half = jnp.where(column_ok[:, None, :], half, 0.0).astype(jnp.bfloat16)
+        half = jnp.where(column_ok[frag_of_pos][:, None, :], half, 0.0).astype(jnp.bfloat16)
         half = half.reshape(frag_total, chol_local, orb_rows, lno_width)
 
-    received = lax.all_to_all(half, "orb", split_axis=0, concat_axis=0, tiled=True)
+    received = lax.all_to_all(half, ("orb_lo", "orb_hi"), split_axis=0, concat_axis=0, tiled=True)
 
     with jax.named_scope("dressing"):
         weighted = (
@@ -101,10 +111,13 @@
 
 
 def solution(mesh):
+    devices = mesh.devices
+    lo = 2 if devices.shape[1] % 2 == 0 else 1
+    fine = Mesh(devices.reshape(devices.shape[0], devices.shape[1] // lo, lo), ("chol",) + ORB)
     return jax.shard_map(
         per_device,
-        mesh=mesh,
-        in_specs=(P("chol", "orb", None), P("orb"), P("orb", None, None), P(), P(), P()),
-        out_specs=(P("chol", "orb", None, None), P("orb", None, None)),
+        mesh=fine,
+        in_specs=(P("chol", ORB, None), P(ORB), P(ORB, None, None), P(), P(), P()),
+        out_specs=(P("chol", ORB, None, None), P(ORB, None, None)),
         check_vma=False,
     )

time: 186 us -> 231 us (1.24)
  waiting for transfers between devices: 85.1 us -> 130 us
    all_gather x1 -> x2, waiting for transfers between devices: 2.14 us -> 48.6 us  [the longest x1 48.6 us: per_device(): across = lax.all_gather(lno_coef, 'orb_hi', axis=0, tiled=True)]
    gather x1 -> x6, local copies, waits for them, and re-layouts: 8.43 us -> 11.5 us  [the longest x1 8.43 us: per_device(): chol_groups = jnp.take(chol_blocks, block_p, axis=0)]
    reshape x2, local copies, waits for them, and re-layouts: 9.88 us -> 7.53 us  [per_device(): chol_vec.reshape(chol_local * orb_rows, orb_size, orb_rows)]
  transfers between devices with their start and end apart: 3 -> 4, of which waited for: 3 -> 3; matrix products, arithmetic and copies ran while one was open for 23% -> 19% of each run, Pallas kernels for 0% -> 0%
where the time goes in v13:
time: 231 us
  waiting for transfers between devices  130 us (56%)
  matrix products  37 us (16%)
  local copies, waits for them, and re-layouts  25.3 us (11%)
  blocking collectives  14.6 us (6%)
  between operations  14.6 us (6%)
  starting transfers between devices  5.02 us (2%)
  other arithmetic  3.46 us (1%)
    all_to_all x1, waiting for transfers between devices, per_device(): lax.all_to_all(half, ('orb_lo', 'orb_hi'), split_axis=0, concat_axis=0, t...  48.7 us
    all_gather x1, waiting for transfers between devices, per_device(): across = lax.all_gather(lno_coef, 'orb_hi', axis=0, tiled=True)  48.6 us
    psum x1, waiting for transfers between devices, per_device(): lax.psum(dressing_part, 'chol') * norm_factor  32.4 us
    unnamed x1, blocking collectives  14.6 us
    dot_general x1, matrix products, per_device(): jnp.einsum('fks,fsa->fka', picked, all_coef, preferred_element_type=jnp.f...  13.1 us
    dot_general x1, matrix products, per_device(): jnp.einsum('fjkr,fjrc->fkjc', chol_groups, group_hot, preferred_element_t...  11.1 us
    gather x1, local copies, waits for them, and re-layouts, per_device(): chol_groups = jnp.take(chol_blocks, block_p, axis=0)  8.43 us
    reshape x2, local copies, waits for them, and re-layouts, per_device(): chol_vec.reshape(chol_local * orb_rows, orb_size, orb_rows)  7.53 us
  transfers between devices with their start and end apart: 4, of which 3 were waited for; matrix products, arithmetic and copies ran while one was open for 19% of the time, Pallas kernels for 0%

profile of v13, /device:TPU:0, one launch (start us, length us, event | category | flops | bytes accessed | tf_op | source)
XLA Modules:
  0.0 230.5 jit_solution(17802922429819568055)
XLA Ops:
  7.2 0.7 all-gather.4.cloned.1.call-update
  8.0 48.6 %all-gather.4.cloned.1.call-done = bf16[4,1024,384]{2,1,0:T(8,128)(2,1)} async-done(((bf16[1,1024,384]{2,1,0:T(8,128)(2,1)}), bf16[4,1024,384]{2,1,0:T(8,128)(2,1)}) %all-gather.4.cloned.1.call-update) | async-done | bytes 3145744 | tf_op jit(solution)/shard_map/all_gather | solution.py:61
  56.6 1.2 dynamic-slice
  58.5 0.9 dynamic-update-slice
  59.4 14.6 %all-reduce = f32[1536]{0:T(1024)S(1)} all-reduce(f32[1536]{0:T(1024)S(1)} %dynamic-update-slice), channel_id=2, replica_groups=mesh['chol'=4,'orb_hi'=4,'orb_lo'=2] {'orb_lo','orb_hi'}, use_global_device_ids=true, to_apply=%add | all-reduce | flops 1536 | bytes 12288
  74.1 3.6 %reshape.152 = bf16[768,8,192]{2,1,0:T(8,128)(2,1)} reshape(bf16[4,192,1536]{2,1,0:T(8,128)(2,1)S(1)} %copy-done.1) | data formatting | bytes 4718592 | tf_op jit(solution)/shard_map/pick_columns/reshape | solution.py:72
  77.8 3.9 %copy.55 = bf16[768,8,192]{0,2,1:T(8,128)(2,1)S(1)} copy(bf16[768,8,192]{2,1,0:T(8,128)(2,1)} %reshape.152) | data formatting | bytes 4718592 | tf_op jit(solution)/shard_map/pick_columns/reshape | solution.py:72
  81.8 0.6 gather_fusion
  82.4 0.6 gather_fusion.1
  82.9 0.1 copy.61
  83.1 0.6 gather_fusion.2
  83.8 0.6 gather_fusion.3
  84.4 8.4 %gather_fusion.4 = bf16[64,768,192]{1,2,0:T(8,128)(2,1)} fusion(bf16[8,768,192]{1,2,0:T(8,128)(2,1)S(1)} %bitcast.67, s32[1024]{0:T(1024)S(1)} %pad_clamp_fusion.1), kind=kCustom, calls=%fused_computation.4 | custom fusion | bytes 37748992 | tf_op jit(solution)/shard_map/pick_columns/jit(_take)/gather | solution.py:73
  92.9 11.1 %fusion.5 = bf16[8,8,128,768]{3,2,1,0:T(8,128)(2,1)} fusion(bf16[8,8,768,192]{2,3,1,0:T(8,128)(2,1)} %bitcast.68, pred[8,8]{1,0:T(8,128)(4,1)S(1)} %compare_and_fusion.1, s32[8,8,128]{2,1,0:T(8,128)S(1)} %broadcast_subtract_fusion, pred[8,8,128]{2,1,0:T(8,128)(4,1)S(1)} %gather_fusion.3), kind=kOutput, calls=%fused_computation.16 | convolution fusion | flops 2434793472 | bytes 31498304 | tf_op jit(solution)/shard_map/pick_columns/fjkr,fjrc->fkjc/dot_general | solution.py:74
  104.0 13.1 %select_convert_fusion = bf16[8,768,384]{2,1,0:T(8,128)(2,1)} fusion(pred[8,384]{1,0:T(8,128)(4,1)S(1)} %gather_fusion, bf16[8,768,1024]{1,2,0:T(8,128)(2,1)} %bitcast.75, bf16[8,1024,384]{2,1,0:T(8,128)(2,1)} %all-gather.6.cloned.1.call-done), kind=kOutput, calls=%fused_computation.13 | convolution fusion | flops 4836556800 | bytes 23596032 | tf_op jit(solution)/shard_map/half/fks,fsa->fka/dot_general | solution.py:88
  117.1 4.7 %all-to-all-start = ((bf16[8,4,192,384]{3,2,1,0:T(8,128)(2,1)}), bf16[8,4,192,384]{3,2,1,0:T(8,128)(2,1)}, u32[]{:S(2)}, u32[]{:S(2)}) async-start(bf16[8,4,192,384]{3,2,1,0:T(8,128)(2,1)} %bitcast.69), calls=%async_computation | async-start | bytes 9437184 | tf_op jit(solution)/shard_map/all_to_all | solution.py:92
  121.8 0.2 all-reduce.3.cloned.1.call-start
  122.0 0.9 iota_reduce_fusion
  122.9 0.1 reshape.211
  123.0 0.8 gather_fusion.7
  123.8 0.8 gather_fusion.8
  124.6 0.7 gather_fusion.5
  125.4 0.2 fusion.26
  125.7 0.1 fusion.27
  125.9 0.6 select_convert_fusion.1
  126.4 0.8 gather_fusion.6
  127.3 48.7 %all-to-all-done = bf16[8,4,192,384]{3,2,1,0:T(8,128)(2,1)} async-done(((bf16[8,4,192,384]{3,2,1,0:T(8,128)(2,1)}), bf16[8,4,192,384]{3,2,1,0:T(8,128)(2,1)}, u32[]{:S(2)}, u32[]{:S(2)}) %all-to-all-start) | async-done | bytes 4718624 | tf_op jit(solution)/shard_map/all_to_all | solution.py:92
  176.0 7.3 %fusion.14 = f32[384,384]{1,0:T(8,128)} fusion(bf16[8,4,192,384]{3,2,1,0:T(8,128)(2,1)} %all-to-all-done, f32[8,192]{1,0:T(8,128)S(1)} %reshape.223), kind=kOutput, calls=%fused_computation.25 | convolution fusion | flops 1819017216 | bytes 5314560 | tf_op jit(solution)/shard_map/dressing/dot_general | solution.py:98
  183.3 5.0 %fusion.13 = bf16[4,1,384,384]{2,3,0,1:T(8,128)(2,1)S(1)} fusion(bf16[8,4,192,384]{3,2,1,0:T(8,128)(2,1)} %all-to-all-done, bf16[8,192,384]{2,1,0:T(8,128)(2,1)S(1)} %gather_fusion.6), kind=kOutput, calls=%fused_computation.24 | convolution fusion | flops 1812529152 | bytes 7077888 | tf_op jit(solution)/shard_map/rotated/ora,ogrb->gab/dot_general | solution.py:107
  188.3 1.5 copy.57
  189.8 32.4 %all-reduce.3.cloned.1.call-done = f32[384,384]{1,0:T(8,128)} async-done(((f32[384,384]{1,0:T(8,128)}), f32[384,384]{1,0:T(8,128)}) %all-reduce.3.cloned.1.call-update) | async-done | bytes 589840 | tf_op jit(solution)/shard_map/dressing/psum | solution.py:104
  222.2 1.8 fusion.24
  (41 shorter events, 0.7 us)
Async XLA Ops:
  7.2 66.9 %copy-start.1 = (bf16[4,192,1536]{2,1,0:T(8,128)(2,1)S(1)}, bf16[4,192,1536]{2,1,0:T(8,128)(2,1)}, u32[]{:S(2)}) copy-start(bf16[4,192,1536]{2,1,0:T(8,128)(2,1)} %param.12) | copy-start | bytes 7077892
  7.2 49.4 %all-gather.4.cloned.1.call-start = ((), (), s32[]{:S(2)}) async-start(), calls=%async_computation.1 | async-start | bytes 3932160 | tf_op jit(solution)/shard_map/all_gather | solution.py:61
  7.9 96.1 %all-gather.6.cloned.1.call-start = ((), (), s32[]{:S(2)}) async-start(), calls=%async_computation.2 | async-start | bytes 9437184 | tf_op jit(solution)/shard_map/all_gather | solution.py:62
  74.1 7.6 %copy-start.2 = (s32[8,1024]{1,0:T(8,128)S(1)}, s32[8,1024]{1,0:T(8,128)}, u32[]{:S(2)}) copy-start(s32[8,1024]{1,0:T(8,128)} %param.15) | copy-start | bytes 98308
  74.1 7.6 %copy-start.5 = (s32[8]{0:T(128)S(1)}, s32[8]{0:T(128)}, u32[]{:S(2)}) copy-start(s32[8]{0:T(128)} %constant.145) | copy-start | bytes 100
  74.1 7.6 %copy-start.4 = (s32[8]{0:T(128)S(1)}, s32[8]{0:T(128)}, u32[]{:S(2)}) copy-start(s32[8]{0:T(128)} %param.17) | copy-start | bytes 100
  74.1 9.6 %copy-start.3 = (s32[8,8]{1,0:T(8,128)S(1)}, s32[8,8]{1,0:T(8,128)}, u32[]{:S(2)}) copy-start(s32[8,8]{1,0:T(8,128)} %param.16) | copy-start | bytes 772
  117.1 7.6 %copy-start = (bf16[1,1024,384]{2,1,0:T(8,128)(2,1)S(1)}, bf16[1,1024,384]{2,1,0:T(8,128)(2,1)}, u32[]{:S(2)}) copy-start(bf16[1,1024,384]{2,1,0:T(8,128)(2,1)} %param.14) | copy-start | bytes 2359300
  117.1 58.9 %all-to-all-start = ((bf16[8,4,192,384]{3,2,1,0:T(8,128)(2,1)}), bf16[8,4,192,384]{3,2,1,0:T(8,128)(2,1)}, u32[]{:S(2)}, u32[]{:S(2)}) async-start(bf16[8,4,192,384]{3,2,1,0:T(8,128)(2,1)} %bitcast.69), calls=%async_computation | async-start | bytes 9437184 | tf_op jit(solution)/shard_map/all_to_all | solution.py:92
  121.8 100.4 %all-reduce.3.cloned.1.call-start = ((), (), s32[]{:S(2)}) async-start(), calls=%async_computation.3 | async-start | bytes 1179648 | tf_op jit(solution)/shard_map/dressing/psum | solution.py:104
Sparse Core Ops, SparseCore 0:
  9.8 46.6 all-gather.3
  58.1 16.7 all-gather.5
  183.5 38.6 all-reduce.2

commit v14 on v12

--- a/solution.py
+++ b/solution.py
@@ -51,7 +51,13 @@
 
     own_pick = lax.dynamic_index_in_dim(group_of_block, my_index, 0, keepdims=False)
     own_perm = jnp.take(lno_coef[0].reshape(group_count, group_width, lno_width), own_pick, axis=0)
-    all_coef = lax.all_gather(lno_coef, "orb", axis=0, tiled=True)
+    split = (lno_width * 2 // 3) // 128 * 128
+    gathered = lax.all_gather(lno_coef[:, :, :split], "orb", axis=0, tiled=True)
+    rest = lno_coef[:, :, split:]
+    spread = lax.all_to_all(
+        jnp.broadcast_to(rest, (orb_size,) + rest.shape[1:]), "orb", split_axis=0, concat_axis=0, tiled=True
+    )
+    all_coef = jnp.concatenate([gathered, spread], axis=2)
 
     with jax.named_scope("pick_columns"):
         group_rows = groups - group_block[:, :, None] * orb_rows

time: 186 us -> 206 us (1.11)
  blocking collectives: 15.8 us -> 31.2 us
  starting transfers between devices: 4.98 us -> 10.2 us
    unnamed x1, blocking collectives: 15.8 us -> 31.2 us
    all_to_all x0 -> x1, starting transfers between devices: none -> 5.17 us  [per_device(): lax.all_to_all(jnp.broadcast_to(rest, (orb_size,) + rest.shape[1:]), 'orb...]
    broadcast_in_dim x0 -> x2, local copies, waits for them, and re-layouts: none -> 2.54 us  [per_device(): jnp.broadcast_to(rest, (orb_size,) + rest.shape[1:])]
    reshape x2, local copies, waits for them, and re-layouts: 9.88 us -> 7.6 us  [per_device(): chol_vec.reshape(chol_local * orb_rows, orb_size, orb_rows)]
    all_gather x1, waiting for transfers between devices: 2.14 us -> 0.01 us  [per_device(): gathered = lax.all_gather(lno_coef[:, :, :split], 'orb', axis=0, tiled=True)]
  transfers between devices with their start and end apart: 3 -> 4, of which waited for: 3 -> 2; matrix products, arithmetic and copies ran while one was open for 23% -> 20% of each run, Pallas kernels for 0% -> 0%
where the time goes in v14:
time: 206 us
  waiting for transfers between devices  83.8 us (41%)
  matrix products  36.8 us (18%)
  blocking collectives  31.2 us (15%)
  local copies, waits for them, and re-layouts  25.6 us (12%)
  between operations  14.9 us (7%)
  starting transfers between devices  10.2 us (5%)
  other arithmetic  3.47 us (2%)
    all_to_all x1, waiting for transfers between devices, per_device(): lax.all_to_all(half, 'orb', split_axis=0, concat_axis=0, tiled=True)  50.7 us
    psum x1, waiting for transfers between devices, per_device(): lax.psum(dressing_part, 'chol') * norm_factor  33.1 us
    unnamed x1, blocking collectives  31.2 us
    dot_general x1, matrix products, per_device(): jnp.einsum('fks,fsa->fka', picked, all_coef, preferred_element_type=jnp.f...  13 us
    dot_general x1, matrix products, per_device(): jnp.einsum('fjkr,fjrc->fkjc', chol_groups, group_hot, preferred_element_t...  11.1 us
    gather x1, local copies, waits for them, and re-layouts, per_device(): chol_groups = jnp.take(chol_blocks, group_block, axis=0)  8.36 us
    reshape x2, local copies, waits for them, and re-layouts, per_device(): chol_vec.reshape(chol_local * orb_rows, orb_size, orb_rows)  7.6 us
    dot_general x1, matrix products, per_device(): lax.dot_general(weighted.reshape(-1, lno_width), received.reshape(-1, lno...  7.29 us
  transfers between devices with their start and end apart: 4, of which 2 were waited for; matrix products, arithmetic and copies ran while one was open for 20% of the time, Pallas kernels for 0%

profile of v14, /device:TPU:0, one launch (start us, length us, event | category | flops | bytes accessed | tf_op | source)
XLA Modules:
  0.0 205.9 jit_solution(5778719305290640432)
XLA Ops:
  7.2 2.0 slice.10
  9.3 1.0 slice_bitcast_fusion
  10.2 1.6 broadcast_in_dim.98
  11.8 5.2 %all-to-all-start = ((bf16[8,1024,128]{2,1,0:T(8,128)(2,1)}), bf16[8,1024,128]{2,1,0:T(8,128)(2,1)}, u32[]{:S(2)}, u32[]{:S(2)}) async-start(bf16[8,1024,128]{2,1,0:T(8,128)(2,1)} %broadcast_in_dim.98), calls=%async_computation | async-start | bytes 4194304 | tf_op jit(solution)/shard_map/all_to_all | solution.py:57
  17.0 0.1 copy.43
  17.2 0.1 reshape.165
  17.3 3.6 %reshape.160 = bf16[768,8,192]{2,1,0:T(8,128)(2,1)} reshape(bf16[4,192,1536]{2,1,0:T(8,128)(2,1)S(1)} %copy-done.1) | data formatting | bytes 4718592 | tf_op jit(solution)/shard_map/pick_columns/reshape | solution.py:68
  20.9 4.0 %copy.37 = bf16[768,8,192]{0,2,1:T(8,128)(2,1)S(1)} copy(bf16[768,8,192]{2,1,0:T(8,128)(2,1)} %reshape.160) | data formatting | bytes 4718592 | tf_op jit(solution)/shard_map/pick_columns/reshape | solution.py:68
  24.9 0.6 dynamic-slice
  26.1 0.3 dynamic-update-slice
  26.4 31.2 %all-reduce = f32[1536]{0:T(1024)S(1)} all-reduce(f32[1536]{0:T(1024)S(1)} %dynamic-update-slice), channel_id=2, replica_groups=mesh['chol'=4,'orb'=8] {'orb'}, use_global_device_ids=true, to_apply=%add | all-reduce | flops 1536 | bytes 12288
  57.7 8.4 %gather_fusion = bf16[64,768,192]{1,2,0:T(8,128)(2,1)} fusion(bf16[8,768,192]{1,2,0:T(8,128)(2,1)S(1)} %bitcast.72, s32[1024]{0:T(1024)S(1)} %pad_clamp_fusion.1), kind=kCustom, calls=%fused_computation | custom fusion | bytes 37748992 | tf_op jit(solution)/shard_map/pick_columns/jit(_take)/gather | solution.py:69
  66.1 0.1 broadcast_compare_fusion
  66.2 0.1 broadcast_subtract_fusion
  66.3 11.1 %fusion.5 = bf16[8,8,128,768]{3,2,1,0:T(8,128)(2,1)} fusion(bf16[8,8,768,192]{2,3,1,0:T(8,128)(2,1)} %bitcast.73, pred[8,8]{1,0:T(8,128)(4,1)S(1)} %get-tuple-element.22, s32[8,8,128]{2,1,0:T(8,128)S(1)} %broadcast_subtract_fusion, pred[8,8,128]{2,1,0:T(8,128)(4,1)S(1)} %broadcast_compare_fusion), kind=kOutput, calls=%fused_computation.11 | convolution fusion | flops 2434793472 | bytes 31498304 | tf_op jit(solution)/shard_map/pick_columns/fjkr,fjrc->fkjc/dot_general | solution.py:70
  77.5 13.0 %select_convert_fusion = bf16[8,768,384]{2,1,0:T(8,128)(2,1)} fusion(pred[8,384]{1,0:T(8,128)(4,1)S(1)} %iota_compare_fusion.3, bf16[8,768,1024]{1,2,0:T(8,128)(2,1)} %bitcast.80, bf16[8,1024,128]{2,1,0:T(8,128)(2,1)} %all-to-all-done, bf16[8,1024,256]{2,1,0:T(8,128)(2,1)} %all-gather.3.cloned.1.call-done), kind=kOutput, calls=%fused_computation.8 | convolution fusion | flops 4849139712 | bytes 23596032 | tf_op jit(solution)/shard_map/half/fks,fsa->fka/dot_general | solution.py:84
  90.5 4.7 %all-to-all-start.1 = ((bf16[8,4,192,384]{3,2,1,0:T(8,128)(2,1)}), bf16[8,4,192,384]{3,2,1,0:T(8,128)(2,1)}, u32[]{:S(2)}, u32[]{:S(2)}) async-start(bf16[8,4,192,384]{3,2,1,0:T(8,128)(2,1)} %bitcast.74), calls=%async_computation.1 | async-start | bytes 9437184 | tf_op jit(solution)/shard_map/all_to_all | solution.py:88
  95.2 0.2 all-reduce.3.cloned.1.call-start
  95.5 0.9 iota_reduce_fusion
  96.4 0.1 reshape.179
  96.5 0.8 gather_fusion.3
  97.3 0.8 gather_fusion.2
  98.1 0.7 gather_fusion.1
  98.9 0.2 fusion.38
  99.1 0.1 fusion.39
  99.2 0.1 fusion.37
  99.3 50.7 %all-to-all-done.1 = bf16[8,4,192,384]{3,2,1,0:T(8,128)(2,1)} async-done(((bf16[8,4,192,384]{3,2,1,0:T(8,128)(2,1)}), bf16[8,4,192,384]{3,2,1,0:T(8,128)(2,1)}, u32[]{:S(2)}, u32[]{:S(2)}) %all-to-all-start.1) | async-done | bytes 4718624 | tf_op jit(solution)/shard_map/all_to_all | solution.py:88
  150.0 7.3 %fusion.21 = f32[384,384]{1,0:T(8,128)} fusion(bf16[8,4,192,384]{3,2,1,0:T(8,128)(2,1)} %all-to-all-done.1, f32[8,192]{1,0:T(8,128)S(1)} %reshape.191), kind=kOutput, calls=%fused_computation.25 | convolution fusion | flops 1819017216 | bytes 5314560 | tf_op jit(solution)/shard_map/dressing/dot_general | solution.py:94
  157.3 5.3 %fusion.20 = bf16[4,1,384,384]{2,3,0,1:T(8,128)(2,1)S(1)} fusion(bf16[8,4,192,384]{3,2,1,0:T(8,128)(2,1)} %all-to-all-done.1, pred[384]{0:T(512)(128)(4,1)S(1)} %dynamic-slice_reduce_fusion, bf16[8,128,384]{2,1,0:T(8,128)(2,1)S(1)} %gather_fusion.1, pred[8]{0:T(512)(128)(4,1)S(1)} %compare_and_fusion.1, s32[1,8,128]{2,1,0:T(8,128)S(1)} %constant_dynamic-slice_fusion, ...), kind=kOutput, calls=%fused_computation.24 | convolution fusion | flops 1965490176 | bytes 6690184 | tf_op jit(solution)/shard_map/rotated/ora,ogrb->gab/dot_general | solution.py:103
  162.7 1.5 copy.39
  164.1 33.1 %all-reduce.3.cloned.1.call-done = f32[384,384]{1,0:T(8,128)} async-done(((f32[384,384]{1,0:T(8,128)}), f32[384,384]{1,0:T(8,128)}) %all-reduce.3.cloned.1.call-update) | async-done | bytes 589840 | tf_op jit(solution)/shard_map/dressing/psum | solution.py:100
  197.2 1.8 fusion.36
  (37 shorter events, 0.4 us)
Async XLA Ops:
  7.2 9.8 %copy-start.2 = (s32[8,1024]{1,0:T(8,128)S(1)}, s32[8,1024]{1,0:T(8,128)}, u32[]{:S(2)}) copy-start(s32[8,1024]{1,0:T(8,128)} %param.9) | copy-start | bytes 98308
  7.2 10.1 %copy-start.1 = (bf16[4,192,1536]{2,1,0:T(8,128)(2,1)S(1)}, bf16[4,192,1536]{2,1,0:T(8,128)(2,1)}, u32[]{:S(2)}) copy-start(bf16[4,192,1536]{2,1,0:T(8,128)(2,1)} %param.6) | copy-start | bytes 7077892
  7.2 70.3 %all-gather.3.cloned.1.call-start = ((), (), s32[]{:S(2)}) async-start(), calls=%async_computation.2 | async-start | bytes 4718592 | tf_op jit(solution)/shard_map/all_gather | solution.py:55
  11.8 65.6 %all-to-all-start = ((bf16[8,1024,128]{2,1,0:T(8,128)(2,1)}), bf16[8,1024,128]{2,1,0:T(8,128)(2,1)}, u32[]{:S(2)}, u32[]{:S(2)}) async-start(bf16[8,1024,128]{2,1,0:T(8,128)(2,1)} %broadcast_in_dim.98), calls=%async_computation | async-start | bytes 4194304 | tf_op jit(solution)/shard_map/all_to_all | solution.py:57
  17.2 7.6 %copy-start.6 = (u32[32]{0:T(128)S(1)}, u32[32]{0:T(128)}, u32[]{:S(2)}) copy-start(u32[32]{0:T(128)} %constant.133) | copy-start | bytes 388
  17.3 8.9 %copy-start.4 = (f32[192]{0:T(256)S(1)}, f32[192]{0:T(256)}, u32[]{:S(2)}) copy-start(f32[192]{0:T(256)} %param.7) | copy-start | bytes 2308
  57.7 8.4 %copy-start.3 = (s32[8,8]{1,0:T(8,128)S(1)}, s32[8,8]{1,0:T(8,128)}, u32[]{:S(2)}) copy-start(s32[8,8]{1,0:T(8,128)} %param.10) | copy-start | bytes 772
  66.3 11.1 %copy-start.5 = (s32[8]{0:T(128)S(1)}, s32[8]{0:T(128)}, u32[]{:S(2)}) copy-start(s32[8]{0:T(128)} %param.11) | copy-start | bytes 100
  90.5 7.6 %copy-start = (bf16[1,1024,384]{2,1,0:T(8,128)(2,1)S(1)}, bf16[1,1024,384]{2,1,0:T(8,128)(2,1)}, u32[]{:S(2)}) copy-start(bf16[1,1024,384]{2,1,0:T(8,128)(2,1)} %param.8) | copy-start | bytes 2359300
  90.5 59.5 %all-to-all-start.1 = ((bf16[8,4,192,384]{3,2,1,0:T(8,128)(2,1)}), bf16[8,4,192,384]{3,2,1,0:T(8,128)(2,1)}, u32[]{:S(2)}, u32[]{:S(2)}) async-start(bf16[8,4,192,384]{3,2,1,0:T(8,128)(2,1)} %bitcast.74), calls=%async_computation.1 | async-start | bytes 9437184 | tf_op jit(solution)/shard_map/all_to_all | solution.py:88
  95.2 102.0 %all-reduce.3.cloned.1.call-start = ((), (), s32[]{:S(2)}) async-start(), calls=%async_computation.3 | async-start | bytes 1179648 | tf_op jit(solution)/shard_map/dressing/psum | solution.py:100
Sparse Core Ops, SparseCore 0:
  10.5 52.0 all-gather.2
  157.4 39.7 all-reduce.2

commit v15 on v14

--- a/solution.py
+++ b/solution.py
@@ -53,11 +53,24 @@
     own_perm = jnp.take(lno_coef[0].reshape(group_count, group_width, lno_width), own_pick, axis=0)
     split = (lno_width * 2 // 3) // 128 * 128
     gathered = lax.all_gather(lno_coef[:, :, :split], "orb", axis=0, tiled=True)
-    rest = lno_coef[:, :, split:]
+    rest_width = lno_width - split
+    weight_rows = -(-3 * orb_rows // rest_width)
+    pad_rows = -(-weight_rows // 8) * 8
+    weight_parts = split_bf16(env_weight).reshape(-1)
+    weight_parts = jnp.pad(weight_parts, (0, pad_rows * rest_width - weight_parts.shape[0]))
+    rest = jnp.concatenate(
+        [lno_coef[:, :, split:], weight_parts.reshape(1, pad_rows, rest_width)], axis=1
+    )
     spread = lax.all_to_all(
         jnp.broadcast_to(rest, (orb_size,) + rest.shape[1:]), "orb", split_axis=0, concat_axis=0, tiled=True
     )
-    all_coef = jnp.concatenate([gathered, spread], axis=2)
+    all_coef = jnp.concatenate([gathered, spread[:, :slot_total]], axis=2)
+    weight_all = join_bf16(
+        spread[:, slot_total:]
+        .reshape(orb_size, -1)[:, : 3 * orb_rows]
+        .reshape(orb_size, 3, orb_rows)
+        .transpose(1, 0, 2)
+    )
 
     with jax.named_scope("pick_columns"):
         group_rows = groups - group_block[:, :, None] * orb_rows
@@ -77,8 +90,6 @@
         own_w = jnp.einsum("orc,oca->ora", own_hot, own_perm, preferred_element_type=jnp.float32)
         own_w = jnp.where(own_cols[None, None, :], own_w, 0.0).astype(jnp.bfloat16)
 
-    weight_all = lax.all_gather(env_weight, "orb", axis=0, tiled=False)
-    weight_all, picked = lax.optimization_barrier((weight_all, picked))
 
     with jax.named_scope("half"):
         half = jnp.einsum("fks,fsa->fka", picked, all_coef, preferred_element_type=jnp.float32)

time: 206 us -> 191 us (0.927)
  blocking collectives: 31.2 us -> 0 us
  waiting for transfers between devices: 83.8 us -> 98.4 us
    unnamed x1 -> x0, blocking collectives: 31.2 us -> none
    all_gather x1, waiting for transfers between devices: 0.01 us -> 9.87 us  [per_device(): gathered = lax.all_gather(lno_coef[:, :, :split], 'orb', axis=0, tiled=True)]
    all_to_all x1, waiting for transfers between devices: 0.01 us -> 6.21 us  [per_device(): lax.all_to_all(jnp.broadcast_to(rest, (orb_size,) + rest.shape[1:]), 'orb...]
    slice x0 -> x2, local copies, waits for them, and re-layouts: none -> 2.73 us  [the longest x1 1.76 us: per_device(): all_coef = jnp.concatenate([gathered, spread[:, :slot_total]], axis=2)]
  transfers between devices with their start and end apart: 4 -> 4, of which waited for: 2 -> 4; matrix products, arithmetic and copies ran while one was open for 20% -> 23% of each run, Pallas kernels for 0% -> 0%
where the time goes in v15:
time: 191 us; the launch traced here: 190 us
  waiting for transfers between devices  98.4 us (52%)
  matrix products  36.2 us (19%)
  local copies, waits for them, and re-layouts  27.2 us (14%)
  between operations  14.3 us (7%)
  starting transfers between devices  10.1 us (5%)
  other arithmetic  4.22 us (2%)
    all_to_all x1, waiting for transfers between devices, per_device(): lax.all_to_all(half, 'orb', split_axis=0, concat_axis=0, tiled=True)  49.8 us
    psum x1, waiting for transfers between devices, per_device(): lax.psum(dressing_part, 'chol') * norm_factor  32.5 us
    dot_general x1, matrix products, per_device(): jnp.einsum('fks,fsa->fka', picked, all_coef, preferred_element_type=jnp.f...  12.4 us
    dot_general x1, matrix products, per_device(): jnp.einsum('fjkr,fjrc->fkjc', chol_groups, group_hot, preferred_element_t...  11.1 us
    all_gather x1, waiting for transfers between devices, per_device(): gathered = lax.all_gather(lno_coef[:, :, :split], 'orb', axis=0, tiled=True)  9.87 us
    gather x1, local copies, waits for them, and re-layouts, per_device(): chol_groups = jnp.take(chol_blocks, group_block, axis=0)  8.33 us
    reshape x2, local copies, waits for them, and re-layouts, per_device(): chol_vec.reshape(chol_local * orb_rows, orb_size, orb_rows)  7.52 us
    dot_general x1, matrix products, per_device(): lax.dot_general(weighted.reshape(-1, lno_width), received.reshape(-1, lno...  7.31 us
  transfers between devices with their start and end apart: 4, of which 4 were waited for; matrix products, arithmetic and copies ran while one was open for 23% of the time, Pallas kernels for 0%

profile of v15, /device:TPU:0, one launch (start us, length us, event | category | flops | bytes accessed | tf_op | source)
XLA Modules:
  0.0 190.5 jit_solution(12280318848396134789)
XLA Ops:
  7.2 2.0 %slice.28 = bf16[1,1024,256]{2,1,0:T(8,128)(2,1)} slice(bf16[1,1024,384]{2,1,0:T(8,128)(2,1)} %param.8), slice={[0:1], [0:1024], [0:256]} | slice | bytes 1048576 | tf_op jit(solution)/shard_map/slice | solution.py:55
  9.3 1.0 slice.29
  10.2 0.7 reduce-precision_convert_fusion.1
  11.0 0.1 convert_element_type.47
  11.1 1.6 broadcast_in_dim.98
  12.7 5.2 %all-to-all-start = ((bf16[8,1032,128]{2,1,0:T(8,128)(2,1)}), bf16[8,1032,128]{2,1,0:T(8,128)(2,1)}, u32[]{:S(2)}, u32[]{:S(2)}) async-start(bf16[8,1032,128]{2,1,0:T(8,128)(2,1)} %broadcast_in_dim.98), calls=%async_computation | async-start | bytes 4227072 | tf_op jit(solution)/shard_map/all_to_all | solution.py:64
  17.9 0.1 copy.45
  18.1 3.6 %reshape.187 = bf16[768,8,192]{2,1,0:T(8,128)(2,1)} reshape(bf16[4,192,1536]{2,1,0:T(8,128)(2,1)S(1)} %copy-done.1) | data formatting | bytes 4718592 | tf_op jit(solution)/shard_map/pick_columns/reshape | solution.py:81
  21.7 3.9 %copy.38 = bf16[768,8,192]{0,2,1:T(8,128)(2,1)S(1)} copy(bf16[768,8,192]{2,1,0:T(8,128)(2,1)} %reshape.187) | data formatting | bytes 4718592 | tf_op jit(solution)/shard_map/pick_columns/reshape | solution.py:81
  25.7 8.3 %gather_fusion = bf16[64,768,192]{1,2,0:T(8,128)(2,1)} fusion(bf16[8,768,192]{1,2,0:T(8,128)(2,1)S(1)} %bitcast.82, s32[1024]{0:T(1024)S(1)} %pad_clamp_fusion.1), kind=kCustom, calls=%fused_computation | custom fusion | bytes 37748992 | tf_op jit(solution)/shard_map/pick_columns/jit(_take)/gather | solution.py:82
  34.3 11.1 %fusion.5 = bf16[8,8,128,768]{3,2,1,0:T(8,128)(2,1)} fusion(bf16[8,8,768,192]{2,3,1,0:T(8,128)(2,1)} %bitcast.83, pred[8,8]{1,0:T(8,128)(4,1)S(1)} %get-tuple-element.18, s32[8,8,128]{2,1,0:T(8,128)S(1)} %broadcast_subtract_fusion, pred[8,8,128]{2,1,0:T(8,128)(4,1)S(1)} %broadcast_compare_fusion), kind=kOutput, calls=%fused_computation.11 | convolution fusion | flops 2434793472 | bytes 31498304 | tf_op jit(solution)/shard_map/pick_columns/fjkr,fjrc->fkjc/dot_general | solution.py:83
  45.4 6.2 %all-to-all-done = bf16[8,1032,128]{2,1,0:T(8,128)(2,1)} async-done(((bf16[8,1032,128]{2,1,0:T(8,128)(2,1)}), bf16[8,1032,128]{2,1,0:T(8,128)(2,1)}, u32[]{:S(2)}, u32[]{:S(2)}) %all-to-all-start) | async-done | bytes 2113568 | tf_op jit(solution)/shard_map/all_to_all | solution.py:64
  51.6 1.8 slice.45
  53.3 9.9 %all-gather.2.cloned.1.call-done = bf16[8,1024,256]{2,1,0:T(8,128)(2,1)} async-done(((bf16[1,1024,256]{2,1,0:T(8,128)(2,1)}), bf16[8,1024,256]{2,1,0:T(8,128)(2,1)}) %all-gather.2.cloned.1.call-update) | async-done | bytes 4194320 | tf_op jit(solution)/shard_map/all_gather | solution.py:55
  63.2 12.4 %select_convert_fusion = bf16[8,768,384]{2,1,0:T(8,128)(2,1)} fusion(pred[8,384]{1,0:T(8,128)(4,1)S(1)} %iota_compare_fusion.3, bf16[8,768,1024]{1,2,0:T(8,128)(2,1)} %bitcast.93, bf16[8,1024,128]{2,1,0:T(8,128)(2,1)S(1)} %slice.45, bf16[8,1024,256]{2,1,0:T(8,128)(2,1)} %all-gather.2.cloned.1.call-done), kind=kOutput, calls=%fused_computation.8 | convolution fusion | flops 4849139712 | bytes 23596032 | tf_op jit(solution)/shard_map/half/fks,fsa->fka/dot_general | solution.py:95
  75.6 4.7 %all-to-all-start.1 = ((bf16[8,4,192,384]{3,2,1,0:T(8,128)(2,1)}), bf16[8,4,192,384]{3,2,1,0:T(8,128)(2,1)}, u32[]{:S(2)}, u32[]{:S(2)}) async-start(bf16[8,4,192,384]{3,2,1,0:T(8,128)(2,1)} %bitcast.84), calls=%async_computation.1 | async-start | bytes 9437184 | tf_op jit(solution)/shard_map/all_to_all | solution.py:99
  80.4 0.2 all-reduce.3.cloned.1.call-start
  80.6 0.9 iota_reduce_fusion
  81.5 0.1 reshape.209
  81.6 0.8 gather_fusion.3
  82.4 0.8 gather_fusion.2
  83.2 0.7 gather_fusion.1
  84.0 0.2 fusion.38
  84.3 0.1 fusion.39
  84.5 0.7 slice_bitcast_fusion
  85.2 0.1 reshape.192
  85.3 49.8 %all-to-all-done.1 = bf16[8,4,192,384]{3,2,1,0:T(8,128)(2,1)} async-done(((bf16[8,4,192,384]{3,2,1,0:T(8,128)(2,1)}), bf16[8,4,192,384]{3,2,1,0:T(8,128)(2,1)}, u32[]{:S(2)}, u32[]{:S(2)}) %all-to-all-start.1) | async-done | bytes 4718624 | tf_op jit(solution)/shard_map/all_to_all | solution.py:99
  135.1 7.3 %fusion.21 = f32[384,384]{1,0:T(8,128)} fusion(bf16[8,4,192,384]{3,2,1,0:T(8,128)(2,1)} %all-to-all-done.1, f32[8,192]{1,0:T(8,128)S(1)} %bitcast.92), kind=kOutput, calls=%fused_computation.25 | convolution fusion | flops 1819017216 | bytes 5314560 | tf_op jit(solution)/shard_map/dressing/dot_general | solution.py:105
  142.4 5.3 %fusion.20 = bf16[4,1,384,384]{2,3,0,1:T(8,128)(2,1)S(1)} fusion(bf16[8,4,192,384]{3,2,1,0:T(8,128)(2,1)} %all-to-all-done.1, pred[384]{0:T(512)(128)(4,1)S(1)} %dynamic-slice_reduce_fusion, bf16[8,128,384]{2,1,0:T(8,128)(2,1)S(1)} %gather_fusion.1, pred[8]{0:T(512)(128)(4,1)S(1)} %compare_and_fusion.1, s32[1,8,128]{2,1,0:T(8,128)S(1)} %constant_dynamic-slice_fusion, ...), kind=kOutput, calls=%fused_computation.24 | convolution fusion | flops 1965490176 | bytes 6690184 | tf_op jit(solution)/shard_map/rotated/ora,ogrb->gab/dot_general | solution.py:114
  147.8 1.5 copy.40
  149.3 32.5 %all-reduce.3.cloned.1.call-done = f32[384,384]{1,0:T(8,128)} async-done(((f32[384,384]{1,0:T(8,128)}), f32[384,384]{1,0:T(8,128)}) %all-reduce.3.cloned.1.call-update) | async-done | bytes 589840 | tf_op jit(solution)/shard_map/dressing/psum | solution.py:111
  181.8 1.8 fusion.36
  (43 shorter events, 0.7 us)
Async XLA Ops:
  7.2 10.7 %copy-start.2 = (s32[8,1024]{1,0:T(8,128)S(1)}, s32[8,1024]{1,0:T(8,128)}, u32[]{:S(2)}) copy-start(s32[8,1024]{1,0:T(8,128)} %param.9) | copy-start | bytes 98308
  7.2 10.9 %copy-start.1 = (bf16[4,192,1536]{2,1,0:T(8,128)(2,1)S(1)}, bf16[4,192,1536]{2,1,0:T(8,128)(2,1)}, u32[]{:S(2)}) copy-start(bf16[4,192,1536]{2,1,0:T(8,128)(2,1)} %param.6) | copy-start | bytes 7077892
  7.2 56.0 %all-gather.2.cloned.1.call-start = ((), (), s32[]{:S(2)}) async-start(), calls=%async_computation.2 | async-start | bytes 4718592 | tf_op jit(solution)/shard_map/all_gather | solution.py:55
  12.7 38.9 %all-to-all-start = ((bf16[8,1032,128]{2,1,0:T(8,128)(2,1)}), bf16[8,1032,128]{2,1,0:T(8,128)(2,1)}, u32[]{:S(2)}, u32[]{:S(2)}) async-start(bf16[8,1032,128]{2,1,0:T(8,128)(2,1)} %broadcast_in_dim.98), calls=%async_computation | async-start | bytes 4227072 | tf_op jit(solution)/shard_map/all_to_all | solution.py:64
  25.7 8.4 %copy-start.3 = (s32[8,8]{1,0:T(8,128)S(1)}, s32[8,8]{1,0:T(8,128)}, u32[]{:S(2)}) copy-start(s32[8,8]{1,0:T(8,128)} %param.10) | copy-start | bytes 772
  25.7 8.5 %copy-start.4 = (s32[8]{0:T(128)S(1)}, s32[8]{0:T(128)}, u32[]{:S(2)}) copy-start(s32[8]{0:T(128)} %param.11) | copy-start | bytes 100
  75.6 7.6 %copy-start = (bf16[1,1024,384]{2,1,0:T(8,128)(2,1)S(1)}, bf16[1,1024,384]{2,1,0:T(8,128)(2,1)}, u32[]{:S(2)}) copy-start(bf16[1,1024,384]{2,1,0:T(8,128)(2,1)} %param.8) | copy-start | bytes 2359300
  75.6 59.5 %all-to-all-start.1 = ((bf16[8,4,192,384]{3,2,1,0:T(8,128)(2,1)}), bf16[8,4,192,384]{3,2,1,0:T(8,128)(2,1)}, u32[]{:S(2)}, u32[]{:S(2)}) async-start(bf16[8,4,192,384]{3,2,1,0:T(8,128)(2,1)} %bitcast.84), calls=%async_computation.1 | async-start | bytes 9437184 | tf_op jit(solution)/shard_map/all_to_all | solution.py:99
  80.4 101.4 %all-reduce.3.cloned.1.call-start = ((), (), s32[]{:S(2)}) async-start(), calls=%async_computation.3 | async-start | bytes 1179648 | tf_op jit(solution)/shard_map/dressing/psum | solution.py:111
Sparse Core Ops, SparseCore 0:
  10.5 52.6 all-gather.1
  142.6 39.1 all-reduce.2

commit v16 on v12

--- a/solution.py
+++ b/solution.py
@@ -3,6 +3,7 @@
 import jax
 import jax.numpy as jnp
 from jax import lax
+from jax.experimental.layout import Layout, with_layout_constraint
 from jax.sharding import PartitionSpec as P
 
 
@@ -64,6 +65,7 @@
         picked = jnp.einsum(
             "fjkr,fjrc->fkjc", chol_groups, group_hot, preferred_element_type=jnp.float32
         ).astype(jnp.bfloat16).reshape(frag_total, chol_local * orb_rows, slot_total)
+        picked = with_layout_constraint(picked, Layout(major_to_minor=(0, 1, 2)))
 
     with jax.named_scope("own_placement"):
         own_hot = lax.dynamic_index_in_dim(onehot, my_index, 0, keepdims=False)

time: 186 us -> 202 us (1.086)
  local copies, waits for them, and re-layouts: 24.1 us -> 35.8 us
  matrix products: 36.9 us -> 42.6 us
    reshape x0 -> x1, local copies, waits for them, and re-layouts: none -> 11.8 us  [per_device(): picked = jnp.einsum('fjkr,fjrc->fkjc', chol_groups, group_hot, preferred_...]
    dot_general x1, matrix products: 11.2 us -> 17.1 us  [per_device(): jnp.einsum('fjkr,fjrc->fkjc', chol_groups, group_hot, preferred_element_t...]
    all_gather x1, waiting for transfers between devices: 2.14 us -> 0.01 us  [per_device(): all_coef = lax.all_gather(lno_coef, 'orb', axis=0, tiled=True)]
  transfers between devices with their start and end apart: 3 -> 3, of which waited for: 3 -> 2; matrix products, arithmetic and copies ran while one was open for 23% -> 30% of each run, Pallas kernels for 0% -> 0%
where the time goes in v16:
time: 202 us
  waiting for transfers between devices  83.2 us (41%)
  matrix products  42.6 us (21%)
  local copies, waits for them, and re-layouts  35.8 us (18%)
  blocking collectives  16.8 us (8%)
  between operations  14.9 us (7%)
  starting transfers between devices  4.98 us (2%)
  other arithmetic  3.47 us (2%)
    all_to_all x1, waiting for transfers between devices, per_device(): lax.all_to_all(half, 'orb', split_axis=0, concat_axis=0, tiled=True)  50.7 us
    psum x1, waiting for transfers between devices, per_device(): lax.psum(dressing_part, 'chol') * norm_factor  31.9 us
    dot_general x1, matrix products, per_device(): jnp.einsum('fjkr,fjrc->fkjc', chol_groups, group_hot, preferred_element_t...  17.1 us
    unnamed x1, blocking collectives  16.8 us
    dot_general x1, matrix products, per_device(): jnp.einsum('fks,fsa->fka', picked, all_coef, preferred_element_type=jnp.f...  12.9 us
    reshape x1, local copies, waits for them, and re-layouts, per_device(): picked = jnp.einsum('fjkr,fjrc->fkjc', chol_groups, group_hot, preferred_...  11.8 us
    reshape x2, local copies, waits for them, and re-layouts, per_device(): chol_vec.reshape(chol_local * orb_rows, orb_size, orb_rows)  9.85 us
    gather x1, local copies, waits for them, and re-layouts, per_device(): chol_groups = jnp.take(chol_blocks, group_block, axis=0)  8.35 us
  transfers between devices with their start and end apart: 3, of which 2 were waited for; matrix products, arithmetic and copies ran while one was open for 30% of the time, Pallas kernels for 0%

profile of v16, /device:TPU:0, one launch (start us, length us, event | category | flops | bytes accessed | tf_op | source)
XLA Modules:
  0.0 201.7 jit_solution(1352183551904583558)
XLA Ops:
  7.2 0.7 all-gather.3.cloned.1.call-update
  7.9 0.8 copy.50
  8.7 0.1 copy.42
  8.8 0.1 reshape.165
  8.9 6.0 %reshape.160 = bf16[768,8,192]{2,1,0:T(8,128)(2,1)} reshape(bf16[4,192,1536]{2,1,0:T(8,128)(2,1)} %param.6) | data formatting | bytes 4718592 | tf_op jit(solution)/shard_map/pick_columns/reshape | solution.py:63
  14.9 3.9 %copy.37 = bf16[768,8,192]{0,2,1:T(8,128)(2,1)S(1)} copy(bf16[768,8,192]{2,1,0:T(8,128)(2,1)} %reshape.160) | data formatting | bytes 4718592 | tf_op jit(solution)/shard_map/pick_columns/reshape | solution.py:63
  18.8 8.3 %gather_fusion = bf16[64,768,192]{1,2,0:T(8,128)(2,1)} fusion(bf16[8,768,192]{1,2,0:T(8,128)(2,1)S(1)} %bitcast.74, s32[1024]{0:T(1024)S(1)} %pad_clamp_fusion.1), kind=kCustom, calls=%fused_computation | custom fusion | bytes 37748992 | tf_op jit(solution)/shard_map/pick_columns/jit(_take)/gather | solution.py:64
  27.2 0.1 broadcast_compare_fusion
  27.3 0.1 broadcast_subtract_fusion
  27.3 17.1 %convert_bitcast_fusion = bf16[8,8,96,8,128]{4,3,2,1,0:T(8,128)(2,1)} fusion(bf16[8,8,768,192]{2,3,1,0:T(8,128)(2,1)} %bitcast.75, pred[8,8]{1,0:T(8,128)(4,1)S(1)} %get-tuple-element.22, s32[8,8,128]{2,1,0:T(8,128)S(1)} %broadcast_subtract_fusion, pred[8,8,128]{2,1,0:T(8,128)(4,1)S(1)} %broadcast_compare_fusion), kind=kOutput, calls=%fused_computation.8 | convolution fusion | flops 2434793472 | bytes 31498304 | tf_op jit(solution)/shard_map/pick_columns/fjkr,fjrc->fkjc/dot_general | solution.py:65
  44.4 11.8 %copy.49 = bf16[8,8,96,8,128]{4,3,1,2,0:T(8,128)(2,1)} copy(bf16[8,8,96,8,128]{4,3,2,1,0:T(8,128)(2,1)} %convert_bitcast_fusion) | data formatting | bytes 25165824 | tf_op jit(solution)/shard_map/pick_columns/reshape | solution.py:67
  56.2 0.6 dynamic-slice
  57.4 0.3 dynamic-update-slice
  57.7 16.8 %all-reduce = f32[1536]{0:T(1024)S(1)} all-reduce(f32[1536]{0:T(1024)S(1)} %dynamic-update-slice), channel_id=2, replica_groups=mesh['chol'=4,'orb'=8] {'orb'}, use_global_device_ids=true, to_apply=%add | all-reduce | flops 1536 | bytes 12288
  74.6 0.1 iota_compare_fusion.3
  74.7 12.9 %select_convert_fusion = bf16[8,768,384]{2,1,0:T(8,128)(2,1)} fusion(pred[8,384]{1,0:T(8,128)(4,1)S(1)} %iota_compare_fusion.3, bf16[8,768,1024]{2,1,0:T(8,128)(2,1)} %bitcast.76, bf16[8,1024,384]{2,1,0:T(8,128)(2,1)} %all-gather.3.cloned.1.call-done), kind=kOutput, calls=%fused_computation.10 | convolution fusion | flops 4836556800 | bytes 23596032 | tf_op jit(solution)/shard_map/half/fks,fsa->fka/dot_general | solution.py:80
  87.6 4.7 %all-to-all-start = ((bf16[8,4,192,384]{3,2,1,0:T(8,128)(2,1)}), bf16[8,4,192,384]{3,2,1,0:T(8,128)(2,1)}, u32[]{:S(2)}, u32[]{:S(2)}) async-start(bf16[8,4,192,384]{3,2,1,0:T(8,128)(2,1)} %bitcast.77), calls=%async_computation | async-start | bytes 9437184 | tf_op jit(solution)/shard_map/all_to_all | solution.py:84
  92.3 0.2 all-reduce.3.cloned.1.call-start
  92.5 0.9 iota_reduce_fusion
  93.5 0.1 reshape.179
  93.6 0.8 gather_fusion.3
  94.4 0.8 gather_fusion.2
  95.2 0.7 gather_fusion.1
  96.0 0.2 fusion.31
  96.2 0.1 fusion.32
  96.3 0.1 fusion.30
  96.4 50.7 %all-to-all-done = bf16[8,4,192,384]{3,2,1,0:T(8,128)(2,1)} async-done(((bf16[8,4,192,384]{3,2,1,0:T(8,128)(2,1)}), bf16[8,4,192,384]{3,2,1,0:T(8,128)(2,1)}, u32[]{:S(2)}, u32[]{:S(2)}) %all-to-all-start) | async-done | bytes 4718624 | tf_op jit(solution)/shard_map/all_to_all | solution.py:84
  147.1 7.3 %fusion.14 = f32[384,384]{1,0:T(8,128)} fusion(bf16[8,4,192,384]{3,2,1,0:T(8,128)(2,1)} %all-to-all-done, f32[8,192]{1,0:T(8,128)S(1)} %reshape.191), kind=kOutput, calls=%fused_computation.22 | convolution fusion | flops 1819017216 | bytes 5314560 | tf_op jit(solution)/shard_map/dressing/dot_general | solution.py:90
  154.4 5.3 %fusion.13 = bf16[4,1,384,384]{2,3,0,1:T(8,128)(2,1)S(1)} fusion(bf16[8,4,192,384]{3,2,1,0:T(8,128)(2,1)} %all-to-all-done, pred[384]{0:T(512)(128)(4,1)S(1)} %dynamic-slice_reduce_fusion, bf16[8,128,384]{2,1,0:T(8,128)(2,1)S(1)} %gather_fusion.1, pred[8]{0:T(512)(128)(4,1)S(1)} %compare_and_fusion.1, s32[1,8,128]{2,1,0:T(8,128)S(1)} %constant_dynamic-slice_fusion, ...), kind=kOutput, calls=%fused_computation.21 | convolution fusion | flops 1965490176 | bytes 6690184 | tf_op jit(solution)/shard_map/rotated/ora,ogrb->gab/dot_general | solution.py:99
  159.7 1.5 copy.39
  161.2 31.9 %all-reduce.3.cloned.1.call-done = f32[384,384]{1,0:T(8,128)} async-done(((f32[384,384]{1,0:T(8,128)}), f32[384,384]{1,0:T(8,128)}) %all-reduce.3.cloned.1.call-update) | async-done | bytes 589840 | tf_op jit(solution)/shard_map/dressing/psum | solution.py:96
  193.0 1.8 fusion.29
  (31 shorter events, 0.3 us)
Async XLA Ops:
  7.2 67.5 %all-gather.3.cloned.1.call-start = ((), (), s32[]{:S(2)}) async-start(), calls=%async_computation.1 | async-start | bytes 7077888 | tf_op jit(solution)/shard_map/all_gather | solution.py:55
  18.8 8.4 %copy-start.2 = (s32[8,8]{1,0:T(8,128)S(1)}, s32[8,8]{1,0:T(8,128)}, u32[]{:S(2)}) copy-start(s32[8,8]{1,0:T(8,128)} %param.10) | copy-start | bytes 772
  18.8 8.5 %copy-start.1 = (s32[8,1024]{1,0:T(8,128)S(1)}, s32[8,1024]{1,0:T(8,128)}, u32[]{:S(2)}) copy-start(s32[8,1024]{1,0:T(8,128)} %param.9) | copy-start | bytes 98308
  44.4 11.8 %copy-start.5 = (u32[32]{0:T(128)S(1)}, u32[32]{0:T(128)}, u32[]{:S(2)}) copy-start(u32[32]{0:T(128)} %constant.133) | copy-start | bytes 388
  44.4 13.0 %copy-start.3 = (f32[192]{0:T(256)S(1)}, f32[192]{0:T(256)}, u32[]{:S(2)}) copy-start(f32[192]{0:T(256)} %param.7) | copy-start | bytes 2308
  44.4 30.2 %copy-start.4 = (s32[8]{0:T(128)S(1)}, s32[8]{0:T(128)}, u32[]{:S(2)}) copy-start(s32[8]{0:T(128)} %param.11) | copy-start | bytes 100
  87.6 7.6 %copy-start = (bf16[1,1024,384]{2,1,0:T(8,128)(2,1)S(1)}, bf16[1,1024,384]{2,1,0:T(8,128)(2,1)}, u32[]{:S(2)}) copy-start(bf16[1,1024,384]{2,1,0:T(8,128)(2,1)} %param.8) | copy-start | bytes 2359300
  87.6 59.5 %all-to-all-start = ((bf16[8,4,192,384]{3,2,1,0:T(8,128)(2,1)}), bf16[8,4,192,384]{3,2,1,0:T(8,128)(2,1)}, u32[]{:S(2)}, u32[]{:S(2)}) async-start(bf16[8,4,192,384]{3,2,1,0:T(8,128)(2,1)} %bitcast.77), calls=%async_computation | async-start | bytes 9437184 | tf_op jit(solution)/shard_map/all_to_all | solution.py:84
  92.3 100.7 %all-reduce.3.cloned.1.call-start = ((), (), s32[]{:S(2)}) async-start(), calls=%async_computation.2 | async-start | bytes 1179648 | tf_op jit(solution)/shard_map/dressing/psum | solution.py:96
Sparse Core Ops, SparseCore 0:
  9.9 48.2 all-gather.2
  154.5 38.4 all-reduce.2

commit v17 on v12

--- a/solution.py
+++ b/solution.py
@@ -74,29 +74,38 @@
     weight_all = lax.all_gather(env_weight, "orb", axis=0, tiled=False)
     weight_all, picked = lax.optimization_barrier((weight_all, picked))
 
-    with jax.named_scope("half"):
-        half = jnp.einsum("fks,fsa->fka", picked, all_coef, preferred_element_type=jnp.float32)
-        half = jnp.where(column_ok[:, None, :], half, 0.0).astype(jnp.bfloat16)
-        half = half.reshape(frag_total, chol_local, orb_rows, lno_width)
-
-    received = lax.all_to_all(half, "orb", split_axis=0, concat_axis=0, tiled=True)
-
+    split = chol_local // 2 if chol_local % 2 == 0 else chol_local
+    parts = [(0, split), (split, chol_local)] if split < chol_local else [(0, chol_local)]
+    dressing_part = None
+    rot_parts = []
+    for lo, hi in parts:
+        width = hi - lo
+        with jax.named_scope("half"):
+            rows = picked[:, lo * orb_rows : hi * orb_rows]
+            half = jnp.einsum("fks,fsa->fka", rows, all_coef, preferred_element_type=jnp.float32)
+            half = jnp.where(column_ok[:, None, :], half, 0.0).astype(jnp.bfloat16)
+            half = half.reshape(frag_total, width, orb_rows, lno_width)
+        received = lax.all_to_all(half, "orb", split_axis=0, concat_axis=0, tiled=True)
+        with jax.named_scope("dressing"):
+            weighted = (
+                received.astype(jnp.float32) * weight_all.reshape(orb_size, 1, orb_rows, 1)
+            ).astype(jnp.bfloat16)
+            term = lax.dot_general(
+                weighted.reshape(-1, lno_width),
+                received.reshape(-1, lno_width),
+                (((0,), (0,)), ((), ())),
+                preferred_element_type=jnp.float32,
+            )
+            dressing_part = term if dressing_part is None else dressing_part + term
+        with jax.named_scope("rotated"):
+            rot_parts.append(
+                jnp.einsum("ora,ogrb->gab", own_w, received, preferred_element_type=jnp.float32).astype(
+                    jnp.bfloat16
+                )
+            )
     with jax.named_scope("dressing"):
-        weighted = (
-            received.astype(jnp.float32) * weight_all.reshape(orb_size, 1, orb_rows, 1)
-        ).astype(jnp.bfloat16)
-        dressing_part = lax.dot_general(
-            weighted.reshape(-1, lno_width),
-            received.reshape(-1, lno_width),
-            (((0,), (0,)), ((), ())),
-            preferred_element_type=jnp.float32,
-        )
         dressing = (lax.psum(dressing_part, "chol") * norm_factor).astype(jnp.bfloat16)
-
-    with jax.named_scope("rotated"):
-        rotated = jnp.einsum(
-            "ora,ogrb->gab", own_w, received, preferred_element_type=jnp.float32
-        ).astype(jnp.bfloat16)[:, None]
+    rotated = jnp.concatenate(rot_parts, axis=0)[:, None]
     return (rotated, dressing[None])
 
 

time: 186 us -> 201 us (1.081)
  local copies, waits for them, and re-layouts: 24.1 us -> 42.9 us
  waiting for transfers between devices: 85.1 us -> 73.4 us
  matrix products: 36.9 us -> 41.4 us
  starting transfers between devices: 4.98 us -> 7.49 us
    optimization_barrier x0 -> x1, local copies, waits for them, and re-layouts: none -> 16.6 us  [per_device(): weight_all, picked = lax.optimization_barrier((weight_all, picked))]
    all_to_all x1 -> x2, waiting for transfers between devices: 50.7 us -> 39.8 us  [per_device(): lax.all_to_all(half, 'orb', split_axis=0, concat_axis=0, tiled=True)]
    dot_general x1 -> x3, matrix products: 13.1 us -> 21.9 us  [the longest x2 18.9 us: per_device(): jnp.einsum('fks,fsa->fka', rows, all_coef, preferred_element_type=jnp.flo...]
    dot_general x1 -> x2, matrix products: 7.31 us -> 4.12 us  [per_device(): lax.dot_general(weighted.reshape(-1, lno_width), received.reshape(-1, lno...]
    all_to_all x1 -> x2, starting transfers between devices: 4.72 us -> 7.23 us  [per_device(): lax.all_to_all(half, 'orb', split_axis=0, concat_axis=0, tiled=True)]
    all_gather x1, waiting for transfers between devices: 2.14 us -> 0.01 us  [per_device(): all_coef = lax.all_gather(lno_coef, 'orb', axis=0, tiled=True)]
    unnamed x18 -> x26, local copies, waits for them, and re-layouts: 3.23 us -> 4.65 us
    dot_general x1 -> x2, matrix products: 5.34 us -> 4.24 us  [per_device(): jnp.einsum('ora,ogrb->gab', own_w, received, preferred_element_type=jnp.f...]
  transfers between devices with their start and end apart: 3 -> 4, of which waited for: 3 -> 3; matrix products, arithmetic and copies ran while one was open for 23% -> 36% of each run, Pallas kernels for 0% -> 0%
where the time goes in v17:
time: 201 us; the launch traced here: 200 us
  waiting for transfers between devices  73.4 us (37%)
  local copies, waits for them, and re-layouts  42.9 us (21%)
  matrix products  41.4 us (21%)
  blocking collectives  15.8 us (8%)
  between operations  14.9 us (7%)
  starting transfers between devices  7.49 us (4%)
  other arithmetic  3.61 us (2%)
    all_to_all x2, waiting for transfers between devices, per_device(): lax.all_to_all(half, 'orb', split_axis=0, concat_axis=0, tiled=True)  39.8 us
    psum x1, waiting for transfers between devices, per_device(): lax.psum(dressing_part, 'chol') * norm_factor  32.9 us
    dot_general x2, matrix products, per_device(): jnp.einsum('fks,fsa->fka', rows, all_coef, preferred_element_type=jnp.flo...  18.9 us
    optimization_barrier x1, local copies, waits for them, and re-layouts, per_device(): weight_all, picked = lax.optimization_barrier((weight_all, picked))  16.6 us
    unnamed x1, blocking collectives  15.8 us
    dot_general x1, matrix products, per_device(): jnp.einsum('fjkr,fjrc->fkjc', chol_groups, group_hot, preferred_element_t...  11.2 us
    reshape x2, local copies, waits for them, and re-layouts, per_device(): chol_vec.reshape(chol_local * orb_rows, orb_size, orb_rows)  9.88 us
    gather x1, local copies, waits for them, and re-layouts, per_device(): chol_groups = jnp.take(chol_blocks, group_block, axis=0)  8.36 us
  transfers between devices with their start and end apart: 4, of which 3 were waited for; matrix products, arithmetic and copies ran while one was open for 36% of the time, Pallas kernels for 0%

profile of v17, /device:TPU:0, one launch (start us, length us, event | category | flops | bytes accessed | tf_op | source)
XLA Modules:
  0.0 199.6 jit_solution(12073078636331379252)
XLA Ops:
  7.2 0.7 all-gather.3.cloned.1.call-update
  7.9 0.8 copy.61
  8.9 6.0 %reshape.166 = bf16[768,8,192]{2,1,0:T(8,128)(2,1)} reshape(bf16[4,192,1536]{2,1,0:T(8,128)(2,1)} %param.6) | data formatting | bytes 4718592 | tf_op jit(solution)/shard_map/pick_columns/reshape | solution.py:62
  14.9 3.9 %copy.49 = bf16[768,8,192]{0,2,1:T(8,128)(2,1)S(1)} copy(bf16[768,8,192]{2,1,0:T(8,128)(2,1)} %reshape.166) | data formatting | bytes 4718592 | tf_op jit(solution)/shard_map/pick_columns/reshape | solution.py:62
  18.8 0.6 dynamic-slice
  20.1 0.3 dynamic-update-slice
  20.4 15.8 %all-reduce = f32[1536]{0:T(1024)S(1)} all-reduce(f32[1536]{0:T(1024)S(1)} %dynamic-update-slice), channel_id=2, replica_groups=mesh['chol'=4,'orb'=8] {'orb'}, use_global_device_ids=true, to_apply=%add | all-reduce | flops 1536 | bytes 12288
  36.2 8.4 %gather_fusion = bf16[64,768,192]{1,2,0:T(8,128)(2,1)} fusion(bf16[8,768,192]{1,2,0:T(8,128)(2,1)S(1)} %bitcast.89, s32[1024]{0:T(1024)S(1)} %pad_clamp_fusion.1), kind=kCustom, calls=%fused_computation | custom fusion | bytes 37748992 | tf_op jit(solution)/shard_map/pick_columns/jit(_take)/gather | solution.py:63
  44.8 11.2 %fusion.4 = bf16[8,8,128,768]{3,2,1,0:T(8,128)(2,1)} fusion(bf16[8,8,768,192]{2,3,1,0:T(8,128)(2,1)} %bitcast.90, pred[8,8]{1,0:T(8,128)(4,1)S(1)} %get-tuple-element.22, s32[8,8,128]{2,1,0:T(8,128)S(1)} %broadcast_subtract_fusion, pred[8,8,128]{2,1,0:T(8,128)(4,1)S(1)} %broadcast_compare_fusion), kind=kOutput, calls=%fused_computation.8 | convolution fusion | flops 2434793472 | bytes 31498304 | tf_op jit(solution)/shard_map/pick_columns/fjkr,fjrc->fkjc/dot_general | solution.py:64
  56.0 16.6 %copy.50 = bf16[8,768,1024]{2,1,0:T(8,128)(2,1)} copy(bf16[8,768,1024]{1,2,0:T(8,128)(2,1)} %bitcast.91) | data formatting | bytes 25165824 | tf_op jit(solution)/shard_map/optimization_barrier | solution.py:75
  72.7 9.4 %select_convert_fusion = bf16[8,384,384]{2,1,0:T(8,128)(2,1)} fusion(pred[8,384]{1,0:T(8,128)(4,1)S(1)} %iota_compare_fusion.3, bf16[8,1024,384]{2,1,0:T(8,128)(2,1)} %all-gather.3.cloned.1.call-done, bf16[8,768,1024]{2,1,0:T(8,128)(2,1)} %copy.50), kind=kOutput, calls=%fused_computation.17 | convolution fusion | flops 2418278400 | bytes 14945280 | tf_op jit(solution)/shard_map/half/fks,fsa->fka/dot_general | solution.py:85
  82.1 3.6 %all-to-all-start.1 = ((bf16[8,2,192,384]{3,2,1,0:T(8,128)(2,1)}), bf16[8,2,192,384]{3,2,1,0:T(8,128)(2,1)S(1)}, u32[]{:S(2)}, u32[]{:S(2)}) async-start(bf16[8,2,192,384]{3,2,1,0:T(8,128)(2,1)} %bitcast.96), calls=%async_computation.1 | async-start | bytes 4718592 | tf_op jit(solution)/shard_map/all_to_all | solution.py:88
  85.8 0.9 iota_reduce_fusion
  86.7 9.5 %select_convert_fusion.1 = bf16[8,384,384]{2,1,0:T(8,128)(2,1)} fusion(pred[8,384]{1,0:T(8,128)(4,1)S(1)} %iota_compare_fusion.3, bf16[8,1024,384]{2,1,0:T(8,128)(2,1)} %all-gather.3.cloned.1.call-done, bf16[8,768,1024]{2,1,0:T(8,128)(2,1)} %copy.50), kind=kOutput, calls=%fused_computation.18 | convolution fusion | flops 2418278400 | bytes 14945280 | tf_op jit(solution)/shard_map/half/fks,fsa->fka/dot_general | solution.py:85
  96.2 18.9 %all-to-all-done.1 = bf16[8,2,192,384]{3,2,1,0:T(8,128)(2,1)S(1)} async-done(((bf16[8,2,192,384]{3,2,1,0:T(8,128)(2,1)}), bf16[8,2,192,384]{3,2,1,0:T(8,128)(2,1)S(1)}, u32[]{:S(2)}, u32[]{:S(2)}) %all-to-all-start.1) | async-done | bytes 2359328 | tf_op jit(solution)/shard_map/all_to_all | solution.py:88
  115.2 1.4 copy-done.1
  116.6 3.6 %all-to-all-start = ((bf16[8,2,192,384]{3,2,1,0:T(8,128)(2,1)}), bf16[8,2,192,384]{3,2,1,0:T(8,128)(2,1)S(1)}, u32[]{:S(2)}, u32[]{:S(2)}) async-start(bf16[8,2,192,384]{3,2,1,0:T(8,128)(2,1)} %bitcast.95), calls=%async_computation | async-start | bytes 4718592 | tf_op jit(solution)/shard_map/all_to_all | solution.py:88
  120.2 0.2 all-reduce.3.cloned.1.call-start
  120.5 0.8 gather_fusion.3
  121.3 0.8 gather_fusion.2
  122.1 1.6 gather_fusion.1
  123.7 0.2 fusion.41
  124.2 2.9 %fusion.23 = bf16[8,192,384,1]{2,1,3,0:T(8,128)(2,1)} fusion(pred[384]{0:T(512)(128)(4,1)S(1)} %dynamic-slice_reduce_fusion, bf16[8,128,384]{2,1,0:T(8,128)(2,1)} %gather_fusion.1, pred[8]{0:T(512)(128)(4,1)S(1)} %compare_and_fusion.1, s32[1,8,128]{2,1,0:T(8,128)S(1)} %constant_dynamic-slice_fusion, pred[1,8,128]{2,1,0:T(8,128)(4,1)S(1)} %constant_dynamic-slice_fusion.2), kind=kOutput, calls=%fused_computation.26 | convolution fusion | flops 152961024 | bytes 1971592 | tf_op jit(solution)/shard_map/own_placement/orc,oca->ora/dot_general | solution.py:71
  127.1 1.6 fusion.28
  128.7 20.8 %all-to-all-done = bf16[8,2,192,384]{3,2,1,0:T(8,128)(2,1)S(1)} async-done(((bf16[8,2,192,384]{3,2,1,0:T(8,128)(2,1)}), bf16[8,2,192,384]{3,2,1,0:T(8,128)(2,1)S(1)}, u32[]{:S(2)}, u32[]{:S(2)}) %all-to-all-start) | async-done | bytes 2359328 | tf_op jit(solution)/shard_map/all_to_all | solution.py:88
  149.6 2.5 %fusion.30 = f32[384,384]{1,0:T(8,128)} fusion(f32[384,384]{1,0:T(8,128)S(1)} %fusion.28, bf16[8,2,192,384]{3,2,1,0:T(8,128)(2,1)S(1)} %all-to-all-done, f32[8,192]{1,0:T(8,128)S(1)} %reshape.198), kind=kOutput, calls=%fused_computation.35 | convolution fusion | flops 909656064 | bytes 3545088 | tf_op jit(solution)/shard_map/dressing/dot_general | solution.py:93
  152.1 2.8 %fusion.27 = bf16[2,384,384]{1,2,0:T(8,128)(2,1)S(1)} fusion(bf16[8,2,192,384]{3,2,1,0:T(8,128)(2,1)S(1)} %all-to-all-done, bf16[8,192,384,1]{2,1,3,0:T(8,128)(2,1)} %fusion.23), kind=kOutput, calls=%fused_computation.32 | convolution fusion | flops 906264576 | bytes 4128768 | tf_op jit(solution)/shard_map/rotated/ora,ogrb->gab/dot_general | solution.py:102
  154.9 1.4 fusion.26
  156.4 0.1 maximum_bitcast_fusion
  156.5 1.5 copy.52
  158.0 32.9 %all-reduce.3.cloned.1.call-done = f32[384,384]{1,0:T(8,128)} async-done(((f32[384,384]{1,0:T(8,128)}), f32[384,384]{1,0:T(8,128)}) %all-reduce.3.cloned.1.call-update) | async-done | bytes 589840 | tf_op jit(solution)/shard_map/dressing/psum | solution.py:107
  190.9 1.8 fusion.39
  (46 shorter events, 1.0 us)
Async XLA Ops:
  7.2 65.6 %all-gather.3.cloned.1.call-start = ((), (), s32[]{:S(2)}) async-start(), calls=%async_computation.2 | async-start | bytes 7077888 | tf_op jit(solution)/shard_map/all_gather | solution.py:54
  14.9 3.9 %copy-start.8 = (u32[32]{0:T(128)S(1)}, u32[32]{0:T(128)}, u32[]{:S(2)}) copy-start(u32[32]{0:T(128)} %constant.133) | copy-start | bytes 388
  14.9 5.2 %copy-start.6 = (f32[192]{0:T(256)S(1)}, f32[192]{0:T(256)}, u32[]{:S(2)}) copy-start(f32[192]{0:T(256)} %param.7) | copy-start | bytes 2308
  36.2 8.4 %copy-start.5 = (s32[8,8]{1,0:T(8,128)S(1)}, s32[8,8]{1,0:T(8,128)}, u32[]{:S(2)}) copy-start(s32[8,8]{1,0:T(8,128)} %param.10) | copy-start | bytes 772
  36.2 8.5 %copy-start.4 = (s32[8,1024]{1,0:T(8,128)S(1)}, s32[8,1024]{1,0:T(8,128)}, u32[]{:S(2)}) copy-start(s32[8,1024]{1,0:T(8,128)} %param.9) | copy-start | bytes 98308
  56.0 16.6 %copy-start.7 = (s32[8]{0:T(128)S(1)}, s32[8]{0:T(128)}, u32[]{:S(2)}) copy-start(s32[8]{0:T(128)} %param.11) | copy-start | bytes 100
  82.1 33.0 %all-to-all-start.1 = ((bf16[8,2,192,384]{3,2,1,0:T(8,128)(2,1)}), bf16[8,2,192,384]{3,2,1,0:T(8,128)(2,1)S(1)}, u32[]{:S(2)}, u32[]{:S(2)}) async-start(bf16[8,2,192,384]{3,2,1,0:T(8,128)(2,1)} %bitcast.96), calls=%async_computation.1 | async-start | bytes 4718592 | tf_op jit(solution)/shard_map/all_to_all | solution.py:88
  115.1 1.4 copy-start.1
  115.1 6.9 %copy-start = (bf16[1,1024,384]{2,1,0:T(8,128)(2,1)S(1)}, bf16[1,1024,384]{2,1,0:T(8,128)(2,1)}, u32[]{:S(2)}) copy-start(bf16[1,1024,384]{2,1,0:T(8,128)(2,1)} %param.8) | copy-start | bytes 2359300
  116.6 33.0 %all-to-all-start = ((bf16[8,2,192,384]{3,2,1,0:T(8,128)(2,1)}), bf16[8,2,192,384]{3,2,1,0:T(8,128)(2,1)S(1)}, u32[]{:S(2)}, u32[]{:S(2)}) async-start(bf16[8,2,192,384]{3,2,1,0:T(8,128)(2,1)} %bitcast.95), calls=%async_computation | async-start | bytes 4718592 | tf_op jit(solution)/shard_map/all_to_all | solution.py:88
  120.2 70.7 %all-reduce.3.cloned.1.call-start = ((), (), s32[]{:S(2)}) async-start(), calls=%async_computation.3 | async-start | bytes 1179648 | tf_op jit(solution)/shard_map/dressing/psum | solution.py:107
  123.7 3.4 %copy-start.2 = (bf16[8,2,192,384]{3,2,1,0:T(8,128)(2,1)S(1)}, bf16[8,2,192,384]{3,2,1,0:T(8,128)(2,1)}, u32[]{:S(2)}) copy-start(bf16[8,2,192,384]{3,2,1,0:T(8,128)(2,1)} %copy-done.1) | copy-start | bytes 7077892
  152.1 2.9 %copy-start.3 = (bf16[8,2,192,384]{3,2,1,0:T(8,128)(2,1)S(1)}, bf16[8,2,192,384]{3,2,1,0:T(8,128)(2,1)}, u32[]{:S(2)}) copy-start(bf16[8,2,192,384]{3,2,1,0:T(8,128)(2,1)} %copy-done.1) | copy-start | bytes 7077892
  152.1 2.9 %copy-start.9 = (bf16[8,192,384,1]{2,1,3,0:T(8,128)(2,1)S(1)}, bf16[8,192,384,1]{2,1,3,0:T(8,128)(2,1)}, u32[]{:S(2)}) copy-start(bf16[8,192,384,1]{2,1,3,0:T(8,128)(2,1)} %fusion.23) | copy-start | bytes 3538948
Sparse Core Ops, SparseCore 0:
  9.9 48.3 all-gather.2
  152.2 38.6 all-reduce.2

commit v18 on v12

--- a/solution.py
+++ b/solution.py
@@ -90,8 +90,8 @@
             received.reshape(-1, lno_width),
             (((0,), (0,)), ((), ())),
             preferred_element_type=jnp.float32,
-        )
-        dressing = (lax.psum(dressing_part, "chol") * norm_factor).astype(jnp.bfloat16)
+        ) * norm_factor
+        dressing = lax.psum(dressing_part, "chol").astype(jnp.bfloat16)
 
     with jax.named_scope("rotated"):
         rotated = jnp.einsum(

time: 186 us -> 181 us (0.973)
  waiting for transfers between devices: 85.1 us -> 53.5 us
  blocking collectives: 15.8 us -> 44.1 us
    psum x1 -> x0, waiting for transfers between devices: 31.6 us -> none  [per_device(): lax.psum(dressing_part, 'chol') * norm_factor]
    psum x0 -> x1, blocking collectives: none -> 28.4 us  [per_device(): dressing = lax.psum(dressing_part, 'chol').astype(jnp.bfloat16)]
  transfers between devices with their start and end apart: 3 -> 2, of which waited for: 3 -> 2; matrix products, arithmetic and copies ran while one was open for 23% -> 20% of each run, Pallas kernels for 0% -> 0%
where the time goes in v18:
time: 181 us; the launch traced here: 179 us
  waiting for transfers between devices  53.5 us (30%)
  blocking collectives  44.1 us (24%)
  matrix products  36.1 us (20%)
  local copies, waits for them, and re-layouts  24.1 us (13%)
  between operations  14.9 us (8%)
  starting transfers between devices  4.97 us (3%)
    all_to_all x1, waiting for transfers between devices, per_device(): lax.all_to_all(half, 'orb', split_axis=0, concat_axis=0, tiled=True)  50.7 us
    psum x1, blocking collectives, per_device(): dressing = lax.psum(dressing_part, 'chol').astype(jnp.bfloat16)  28.4 us
    unnamed x1, blocking collectives  15.8 us
    dot_general x1, matrix products, per_device(): jnp.einsum('fks,fsa->fka', picked, all_coef, preferred_element_type=jnp.f...  13 us
    dot_general x1, matrix products, per_device(): jnp.einsum('fjkr,fjrc->fkjc', chol_groups, group_hot, preferred_element_t...  11.2 us
    reshape x2, local copies, waits for them, and re-layouts, per_device(): chol_vec.reshape(chol_local * orb_rows, orb_size, orb_rows)  9.88 us
    gather x1, local copies, waits for them, and re-layouts, per_device(): chol_groups = jnp.take(chol_blocks, group_block, axis=0)  8.43 us
    dot_general x1, matrix products, per_device(): lax.dot_general(weighted.reshape(-1, lno_width), received.reshape(-1, lno...  6.47 us
  transfers between devices with their start and end apart: 2, of which 2 were waited for; matrix products, arithmetic and copies ran while one was open for 20% of the time, Pallas kernels for 0%

profile of v18, /device:TPU:0, one launch (start us, length us, event | category | flops | bytes accessed | tf_op | source)
XLA Modules:
  0.0 179.3 jit_solution(16500178387567469073)
XLA Ops:
  7.2 0.0 all-gather.3.cloned.1.call-start
  7.2 0.7 all-gather.3.cloned.1.call-update
  7.9 0.8 copy.48
  8.7 0.1 copy.43
  8.8 0.1 reshape.165
  8.9 6.0 %reshape.160 = bf16[768,8,192]{2,1,0:T(8,128)(2,1)} reshape(bf16[4,192,1536]{2,1,0:T(8,128)(2,1)} %param.6) | data formatting | bytes 4718592 | tf_op jit(solution)/shard_map/pick_columns/reshape | solution.py:62
  14.9 3.9 %copy.37 = bf16[768,8,192]{0,2,1:T(8,128)(2,1)S(1)} copy(bf16[768,8,192]{2,1,0:T(8,128)(2,1)} %reshape.160) | data formatting | bytes 4718592 | tf_op jit(solution)/shard_map/pick_columns/reshape | solution.py:62
  18.8 0.6 dynamic-slice
  20.1 0.3 dynamic-update-slice
  20.4 15.8 %all-reduce = f32[1536]{0:T(1024)S(1)} all-reduce(f32[1536]{0:T(1024)S(1)} %dynamic-update-slice), channel_id=2, replica_groups=mesh['chol'=4,'orb'=8] {'orb'}, use_global_device_ids=true, to_apply=%add | all-reduce | flops 1536 | bytes 12288
  36.1 0.1 reshape.191
  36.2 8.4 %gather_fusion = bf16[64,768,192]{1,2,0:T(8,128)(2,1)} fusion(bf16[8,768,192]{1,2,0:T(8,128)(2,1)S(1)} %bitcast.74, s32[1024]{0:T(1024)S(1)} %pad_clamp_fusion.1), kind=kCustom, calls=%fused_computation | custom fusion | bytes 37748992 | tf_op jit(solution)/shard_map/pick_columns/jit(_take)/gather | solution.py:63
  44.7 0.1 broadcast_compare_fusion
  44.8 0.1 broadcast_subtract_fusion
  44.9 11.2 %fusion.5 = bf16[8,8,128,768]{3,2,1,0:T(8,128)(2,1)} fusion(bf16[8,8,768,192]{2,3,1,0:T(8,128)(2,1)} %bitcast.75, pred[8,8]{1,0:T(8,128)(4,1)S(1)} %get-tuple-element.22, s32[8,8,128]{2,1,0:T(8,128)S(1)} %broadcast_subtract_fusion, pred[8,8,128]{2,1,0:T(8,128)(4,1)S(1)} %broadcast_compare_fusion), kind=kOutput, calls=%fused_computation.11 | convolution fusion | flops 2434793472 | bytes 31498304 | tf_op jit(solution)/shard_map/pick_columns/fjkr,fjrc->fkjc/dot_general | solution.py:64
  56.1 0.1 iota_compare_fusion.3
  56.2 2.1 %all-gather.3.cloned.1.call-done = bf16[8,1024,384]{2,1,0:T(8,128)(2,1)} async-done(((bf16[1,1024,384]{2,1,0:T(8,128)(2,1)}), bf16[8,1024,384]{2,1,0:T(8,128)(2,1)}) %all-gather.3.cloned.1.call-update) | async-done | bytes 6291472 | tf_op jit(solution)/shard_map/all_gather | solution.py:54
  58.3 13.0 %select_convert_fusion = bf16[8,768,384]{2,1,0:T(8,128)(2,1)} fusion(pred[8,384]{1,0:T(8,128)(4,1)S(1)} %iota_compare_fusion.3, bf16[8,768,1024]{1,2,0:T(8,128)(2,1)} %bitcast.83, bf16[8,1024,384]{2,1,0:T(8,128)(2,1)} %all-gather.3.cloned.1.call-done), kind=kOutput, calls=%fused_computation.8 | convolution fusion | flops 4836556800 | bytes 23596032 | tf_op jit(solution)/shard_map/half/fks,fsa->fka/dot_general | solution.py:78
  71.3 4.9 %all-to-all-start = ((bf16[8,4,192,384]{3,2,1,0:T(8,128)(2,1)}), bf16[8,4,192,384]{3,2,1,0:T(8,128)(2,1)}, u32[]{:S(2)}, u32[]{:S(2)}) async-start(bf16[8,4,192,384]{3,2,1,0:T(8,128)(2,1)} %bitcast.76), calls=%async_computation | async-start | bytes 9437184 | tf_op jit(solution)/shard_map/all_to_all | solution.py:82
  76.3 0.9 iota_reduce_fusion
  77.2 0.1 reshape.179
  77.3 0.8 gather_fusion.3
  78.1 0.8 gather_fusion.2
  78.9 0.7 gather_fusion.1
  79.7 0.2 fusion.32
  79.9 0.1 fusion.33
  80.0 0.1 fusion.31
  80.1 50.7 %all-to-all-done = bf16[8,4,192,384]{3,2,1,0:T(8,128)(2,1)} async-done(((bf16[8,4,192,384]{3,2,1,0:T(8,128)(2,1)}), bf16[8,4,192,384]{3,2,1,0:T(8,128)(2,1)}, u32[]{:S(2)}, u32[]{:S(2)}) %all-to-all-start) | async-done | bytes 4718624 | tf_op jit(solution)/shard_map/all_to_all | solution.py:82
  130.8 5.4 %fusion.14 = bf16[4,1,384,384]{2,3,0,1:T(8,128)(2,1)S(1)} fusion(bf16[8,4,192,384]{3,2,1,0:T(8,128)(2,1)} %all-to-all-done, pred[384]{0:T(512)(128)(4,1)S(1)} %dynamic-slice_reduce_fusion, bf16[8,128,384]{2,1,0:T(8,128)(2,1)S(1)} %gather_fusion.1, pred[8]{0:T(512)(128)(4,1)S(1)} %compare_and_fusion.1, s32[1,8,128]{2,1,0:T(8,128)S(1)} %constant_dynamic-slice_fusion, ...), kind=kOutput, calls=%fused_computation.20 | convolution fusion | flops 1965490176 | bytes 6690184 | tf_op jit(solution)/shard_map/rotated/ora,ogrb->gab/dot_general | solution.py:97
  136.2 1.5 copy.39
  137.6 6.5 %fusion.16 = f32[384,384]{1,0:T(8,128)S(1)} fusion(bf16[8,4,192,384]{3,2,1,0:T(8,128)(2,1)} %all-to-all-done, f32[8,192]{1,0:T(8,128)S(1)} %reshape.191), kind=kOutput, calls=%fused_computation.22 | convolution fusion | flops 1819164672 | bytes 5314560 | tf_op jit(solution)/shard_map/dressing/dot_general | solution.py:88
  144.1 28.4 %all-reduce.2 = bf16[384,384]{1,0:T(8,128)(2,1)} all-reduce(f32[384,384]{1,0:T(8,128)S(1)} %fusion.16), channel_id=1, replica_groups=mesh['chol'=4,'orb'=8] {'chol'}, use_global_device_ids=true, to_apply=%region_2.3 | all-reduce | flops 147456 | bytes 884736 | tf_op jit(solution)/shard_map/dressing/psum | solution.py:94
  (27 shorter events, 0.2 us)
Async XLA Ops:
  7.2 51.2 %all-gather.3.cloned.1.call-start = ((), (), s32[]{:S(2)}) async-start(), calls=%async_computation.1 | async-start | bytes 7077888 | tf_op jit(solution)/shard_map/all_gather | solution.py:54
  8.9 9.9 %copy-start.5 = (u32[32]{0:T(128)S(1)}, u32[32]{0:T(128)}, u32[]{:S(2)}) copy-start(u32[32]{0:T(128)} %constant.133) | copy-start | bytes 388
  8.9 11.2 %copy-start.3 = (f32[192]{0:T(256)S(1)}, f32[192]{0:T(256)}, u32[]{:S(2)}) copy-start(f32[192]{0:T(256)} %param.7) | copy-start | bytes 2308
  36.2 8.5 %copy-start.2 = (s32[8,8]{1,0:T(8,128)S(1)}, s32[8,8]{1,0:T(8,128)}, u32[]{:S(2)}) copy-start(s32[8,8]{1,0:T(8,128)} %param.10) | copy-start | bytes 772
  36.2 8.5 %copy-start.1 = (s32[8,1024]{1,0:T(8,128)S(1)}, s32[8,1024]{1,0:T(8,128)}, u32[]{:S(2)}) copy-start(s32[8,1024]{1,0:T(8,128)} %param.9) | copy-start | bytes 98308
  44.9 11.2 %copy-start.4 = (s32[8]{0:T(128)S(1)}, s32[8]{0:T(128)}, u32[]{:S(2)}) copy-start(s32[8]{0:T(128)} %param.11) | copy-start | bytes 100
  71.3 7.6 %copy-start = (bf16[1,1024,384]{2,1,0:T(8,128)(2,1)S(1)}, bf16[1,1024,384]{2,1,0:T(8,128)(2,1)}, u32[]{:S(2)}) copy-start(bf16[1,1024,384]{2,1,0:T(8,128)(2,1)} %param.8) | copy-start | bytes 2359300
  71.3 59.5 %all-to-all-start = ((bf16[8,4,192,384]{3,2,1,0:T(8,128)(2,1)}), bf16[8,4,192,384]{3,2,1,0:T(8,128)(2,1)}, u32[]{:S(2)}, u32[]{:S(2)}) async-start(bf16[8,4,192,384]{3,2,1,0:T(8,128)(2,1)} %bitcast.76), calls=%async_computation | async-start | bytes 9437184 | tf_op jit(solution)/shard_map/all_to_all | solution.py:82
Sparse Core Ops, SparseCore 0:
  9.9 48.3 all-gather.2

commit v19 on v18

--- a/solution.py
+++ b/solution.py
@@ -95,7 +95,7 @@
 
     with jax.named_scope("rotated"):
         rotated = jnp.einsum(
-            "ora,ogrb->gab", own_w, received, preferred_element_type=jnp.float32
+            "ogrb,ora->gab", received, own_w, preferred_element_type=jnp.float32
         ).astype(jnp.bfloat16)[:, None]
     return (rotated, dressing[None])
 

time: 181 us -> 180 us (level)
  transfers between devices with their start and end apart: 2 -> 2, of which waited for: 2 -> 2; matrix products, arithmetic and copies ran while one was open for 20% -> 21% of each run, Pallas kernels for 0% -> 0%
where the time goes in v19:
time: 180 us; the launch traced here: 178 us
  waiting for transfers between devices  52 us (29%)
  blocking collectives  44.1 us (24%)
  matrix products  36.5 us (20%)
  local copies, waits for them, and re-layouts  23.1 us (13%)
  between operations  14.9 us (8%)
  starting transfers between devices  4.97 us (3%)
  other arithmetic  2.66 us (1%)
    all_to_all x1, waiting for transfers between devices, per_device(): lax.all_to_all(half, 'orb', split_axis=0, concat_axis=0, tiled=True)  50.4 us
    psum x1, blocking collectives, per_device(): dressing = lax.psum(dressing_part, 'chol').astype(jnp.bfloat16)  28.4 us
    unnamed x1, blocking collectives  15.7 us
    dot_general x1, matrix products, per_device(): jnp.einsum('fks,fsa->fka', picked, all_coef, preferred_element_type=jnp.f...  13 us
    dot_general x1, matrix products, per_device(): jnp.einsum('fjkr,fjrc->fkjc', chol_groups, group_hot, preferred_element_t...  11.3 us
    reshape x2, local copies, waits for them, and re-layouts, per_device(): chol_vec.reshape(chol_local * orb_rows, orb_size, orb_rows)  9.86 us
    gather x1, local copies, waits for them, and re-layouts, per_device(): chol_groups = jnp.take(chol_blocks, group_block, axis=0)  8.36 us
    dot_general x1, matrix products, per_device(): lax.dot_general(weighted.reshape(-1, lno_width), received.reshape(-1, lno...  6.47 us
  transfers between devices with their start and end apart: 2, of which 2 were waited for; matrix products, arithmetic and copies ran while one was open for 21% of the time, Pallas kernels for 0%

profile of v19, /device:TPU:0, one launch (start us, length us, event | category | flops | bytes accessed | tf_op | source)
XLA Modules:
  0.0 178.2 jit_solution(12885288086002832834)
XLA Ops:
  7.2 0.7 all-gather.3.cloned.1.call-update
  7.9 1.2 dynamic-slice
  9.8 0.9 dynamic-update-slice
  10.7 15.7 %all-reduce = f32[1536]{0:T(1024)S(1)} all-reduce(f32[1536]{0:T(1024)S(1)} %dynamic-update-slice), channel_id=2, replica_groups=mesh['chol'=4,'orb'=8] {'orb'}, use_global_device_ids=true, to_apply=%add | all-reduce | flops 1536 | bytes 12288
  26.4 0.1 reshape.190
  26.5 6.0 %reshape.159 = bf16[768,8,192]{2,1,0:T(8,128)(2,1)} reshape(bf16[4,192,1536]{2,1,0:T(8,128)(2,1)} %param.6) | data formatting | bytes 4718592 | tf_op jit(solution)/shard_map/pick_columns/reshape | solution.py:62
  32.4 3.9 %copy.28 = bf16[768,8,192]{0,2,1:T(8,128)(2,1)S(1)} copy(bf16[768,8,192]{2,1,0:T(8,128)(2,1)} %reshape.159) | data formatting | bytes 4718592 | tf_op jit(solution)/shard_map/pick_columns/reshape | solution.py:62
  36.4 0.4 fusion.45
  36.7 0.5 multiply_reduce_fusion
  37.2 0.1 reshape.172
  37.3 8.4 %gather_fusion.1 = bf16[64,768,192]{1,2,0:T(8,128)(2,1)} fusion(bf16[8,768,192]{1,2,0:T(8,128)(2,1)S(1)} %bitcast.66, s32[1024]{0:T(1024)S(1)} %pad_clamp_fusion), kind=kCustom, calls=%fused_computation.1 | custom fusion | bytes 37748992 | tf_op jit(solution)/shard_map/pick_columns/jit(_take)/gather | solution.py:63
  45.7 0.1 broadcast_compare_fusion
  45.8 0.1 broadcast_subtract_fusion
  45.9 11.3 %fusion.5 = bf16[8,8,128,768]{3,2,1,0:T(8,128)(2,1)} fusion(bf16[8,8,768,192]{2,3,1,0:T(8,128)(2,1)} %bitcast.67, pred[8,8]{1,0:T(8,128)(4,1)S(1)} %get-tuple-element.20, s32[8,8,128]{2,1,0:T(8,128)S(1)} %broadcast_subtract_fusion, pred[8,8,128]{2,1,0:T(8,128)(4,1)S(1)} %broadcast_compare_fusion), kind=kOutput, calls=%fused_computation.11 | convolution fusion | flops 2434793472 | bytes 31498304 | tf_op jit(solution)/shard_map/pick_columns/fjkr,fjrc->fkjc/dot_general | solution.py:64
  57.1 0.1 iota_compare_fusion.3
  57.2 1.0 all-gather.3.cloned.1.call-done
  58.2 13.0 %select_convert_fusion = bf16[8,768,384]{2,1,0:T(8,128)(2,1)} fusion(pred[8,384]{1,0:T(8,128)(4,1)S(1)} %iota_compare_fusion.3, bf16[8,768,1024]{1,2,0:T(8,128)(2,1)} %bitcast.76, bf16[8,1024,384]{2,1,0:T(8,128)(2,1)} %all-gather.3.cloned.1.call-done), kind=kOutput, calls=%fused_computation.8 | convolution fusion | flops 4836556800 | bytes 23596032 | tf_op jit(solution)/shard_map/half/fks,fsa->fka/dot_general | solution.py:78
  71.2 4.9 %all-to-all-start = ((bf16[8,4,192,384]{3,2,1,0:T(8,128)(2,1)}), bf16[8,4,192,384]{3,2,1,0:T(8,128)(2,1)}, u32[]{:S(2)}, u32[]{:S(2)}) async-start(bf16[8,4,192,384]{3,2,1,0:T(8,128)(2,1)} %bitcast.68), calls=%async_computation | async-start | bytes 9437184 | tf_op jit(solution)/shard_map/all_to_all | solution.py:82
  76.2 0.9 iota_reduce_fusion
  77.1 0.1 copy.27
  77.2 0.2 or_reduce_fusion
  77.5 0.1 reshape.178
  77.5 0.8 gather_fusion.2
  78.3 0.8 gather_fusion.3
  79.2 0.7 gather_fusion
  79.9 0.2 fusion.32
  80.2 0.1 fusion.34
  80.3 0.1 fusion.31
  80.4 50.4 %all-to-all-done = bf16[8,4,192,384]{3,2,1,0:T(8,128)(2,1)} async-done(((bf16[8,4,192,384]{3,2,1,0:T(8,128)(2,1)}), bf16[8,4,192,384]{3,2,1,0:T(8,128)(2,1)}, u32[]{:S(2)}, u32[]{:S(2)}) %all-to-all-start) | async-done | bytes 4718624 | tf_op jit(solution)/shard_map/all_to_all | solution.py:82
  130.7 6.5 %fusion.16 = f32[384,384]{1,0:T(8,128)S(1)} fusion(bf16[8,4,192,384]{3,2,1,0:T(8,128)(2,1)} %all-to-all-done, f32[8,192]{1,0:T(8,128)S(1)} %reshape.190), kind=kOutput, calls=%fused_computation.22 | convolution fusion | flops 1819164672 | bytes 5314560 | tf_op jit(solution)/shard_map/dressing/dot_general | solution.py:88
  137.2 28.4 %all-reduce.2 = bf16[384,384]{1,0:T(8,128)(2,1)} all-reduce(f32[384,384]{1,0:T(8,128)S(1)} %fusion.16), channel_id=1, replica_groups=mesh['chol'=4,'orb'=8] {'chol'}, use_global_device_ids=true, to_apply=%region_2.3 | all-reduce | flops 147456 | bytes 884736 | tf_op jit(solution)/shard_map/dressing/psum | solution.py:94
  165.6 5.8 %fusion.14 = bf16[4,1,384,384]{3,2,1,0:T(8,128)(2,1)} fusion(bf16[8,4,192,384]{3,2,1,0:T(8,128)(2,1)} %all-to-all-done, pred[384]{0:T(512)(128)(4,1)S(1)} %dynamic-slice_reduce_fusion, bf16[8,128,384]{2,1,0:T(8,128)(2,1)S(1)} %gather_fusion, pred[8]{0:T(512)(128)(4,1)S(1)} %compare_and_fusion.1, s32[1,8,128]{2,1,0:T(8,128)S(1)} %constant_dynamic-slice_fusion, ...), kind=kOutput, calls=%fused_computation.20 | convolution fusion | flops 1965490176 | bytes 6690184 | tf_op jit(solution)/shard_map/rotated/ogrb,ora->gab/dot_general | solution.py:97
  (23 shorter events, 0.2 us)
Async XLA Ops:
  7.2 51.1 %all-gather.3.cloned.1.call-start = ((), (), s32[]{:S(2)}) async-start(), calls=%async_computation.1 | async-start | bytes 7077888 | tf_op jit(solution)/shard_map/all_gather | solution.py:54
  26.5 9.9 %copy-start.1 = (s32[8,1024]{1,0:T(8,128)S(1)}, s32[8,1024]{1,0:T(8,128)}, u32[]{:S(2)}) copy-start(s32[8,1024]{1,0:T(8,128)} %param.9) | copy-start | bytes 98308
  37.3 8.4 %copy-start.2 = (s32[8,8]{1,0:T(8,128)S(1)}, s32[8,8]{1,0:T(8,128)}, u32[]{:S(2)}) copy-start(s32[8,8]{1,0:T(8,128)} %param.10) | copy-start | bytes 772
  45.9 11.3 %copy-start.3 = (s32[8]{0:T(128)S(1)}, s32[8]{0:T(128)}, u32[]{:S(2)}) copy-start(s32[8]{0:T(128)} %param.11) | copy-start | bytes 100
  71.2 7.9 %copy-start = (bf16[1,1024,384]{2,1,0:T(8,128)(2,1)S(1)}, bf16[1,1024,384]{2,1,0:T(8,128)(2,1)}, u32[]{:S(2)}) copy-start(bf16[1,1024,384]{2,1,0:T(8,128)(2,1)} %param.8) | copy-start | bytes 2359300
  71.2 59.5 %all-to-all-start = ((bf16[8,4,192,384]{3,2,1,0:T(8,128)(2,1)}), bf16[8,4,192,384]{3,2,1,0:T(8,128)(2,1)}, u32[]{:S(2)}, u32[]{:S(2)}) async-start(bf16[8,4,192,384]{3,2,1,0:T(8,128)(2,1)} %bitcast.68), calls=%async_computation | async-start | bytes 9437184 | tf_op jit(solution)/shard_map/all_to_all | solution.py:82
Sparse Core Ops, SparseCore 0:
  9.9 48.2 all-gather.2
